TPU v7x, 512 devices: a whole 4x4x16 slice. The times are simulated.
512 devices in a mesh: gx: 64 (over z, y), gy: 8 (over x, core).
Axes of the slice: x: 4, y: 4, z: 16, core: 2. Of those that a mesh axis runs over, the one named last changes fastest.
Arguments:
- rhs: float32 [64, 8, 128, 128], P('gx', 'gy'), may hold values from -57 to 57
- face_rows: int32 [64, 8, 4, 128], P('gx', 'gy'), may hold values from 0 to 127
- margin_weight: float32 [64, 8, 4, 128], P('gx', 'gy'), may hold values from 0.2 to 1
- local_blocks: bfloat16 [64, 8, 1, 128, 128], P('gx', 'gy'), may hold values from -0.4 to 4.4
- subdomain_inverse: bfloat16 [64, 8, 128, 640], P('gx', 'gy'), may hold values from -0.4 to 1.8
- coarse_basis: bfloat16 [64, 8, 128, 32], P('gx', 'gy'), may hold values from -0.5 to 0.5
- coarse_inverse: bfloat16 [64, 8, 32, 16384], P('gx', 'gy'), may hold values from -0.09765625 to 0.09765625
- coarse_map: int32 [512], replicated, may hold values from 0 to 511, each once
Outputs:
- solution: float32 [64, 8, 128, 128], P('gx', 'gy')
- relative_residual: float32 [128], replicated
Inputs may be any that keep to these rules, and one draw needn't show every extreme that they name: `face_rows`: rows of the subdomain, repeats possible. `coarse_map`: every position once.
All inputs are finite; a program needn't handle non-finite values.
Results may differ from a plain program's by a relative error of at most 0.004.
Values may be sent and summed in bfloat16 or wider, within the bound.
No kernel may reach another device: no remote copies, remote signals or barrier semaphores. Data moves between devices by JAX's collectives and lax.ppermute only.
A program may use at most 64 MiB of HBM per device.

v0:
```python
import jax
import jax.numpy as jnp
from jax import lax
from jax.sharding import PartitionSpec as P

EPSILON = 1e-06


def padded(shard, sides, width):
    for axis, dim in sides:
        count, length = (lax.axis_size(axis), shard.shape[dim])
        up = [(i, (i + 1) % count) for i in range(count - 1)]
        down = [(j, i) for i, j in up]
        last = lax.slice_in_dim(shard, length - width, length, axis=dim)
        initial = lax.slice_in_dim(shard, 0, width, axis=dim)
        before = lax.ppermute(last, axis, up)
        after = lax.ppermute(initial, axis, down)
        shard = jnp.concatenate([before, shard, after], axis=dim)
    return shard


def least_squares(scale_norm, first_dot, first_norm, cross_dot, second_dot, second_norm):
    radius_one = jnp.sqrt(first_dot * first_dot + first_norm * first_norm)
    cosine_one = first_dot / radius_one
    sine_one = first_norm / radius_one
    upper_entry = cosine_one * cross_dot + sine_one * second_dot
    lower_entry = cosine_one * second_dot - sine_one * cross_dot
    radius_two = jnp.sqrt(lower_entry * lower_entry + second_norm * second_norm)
    cosine_two = lower_entry / radius_two
    sine_two = second_norm / radius_two
    weight_two = -cosine_two * sine_one * scale_norm / radius_two
    weight_one = (cosine_one * scale_norm - upper_entry * weight_two) / radius_one
    return (weight_one, weight_two, sine_one * sine_two)


def on_device(
    rhs,
    face_rows,
    margin_weight,
    local_blocks,
    subdomain_inverse,
    coarse_basis,
    coarse_inverse,
    coarse_map,
):
    right_side = rhs[0, 0]
    margin_rows = face_rows[0, 0]
    margin_weights = margin_weight[0, 0]
    local_block = local_blocks[0, 0]
    inverse_rows = subdomain_inverse[0, 0]
    basis = coarse_basis[0, 0]
    coarse_rows = coarse_inverse[0, 0]
    owned_rows = right_side.shape[0]
    system_count = right_side.shape[1]
    basis_count = basis.shape[1]
    block_rows = local_block.shape[1]
    positions = (
        coarse_map[:, None] * basis_count + jnp.arange(basis_count, dtype=jnp.int32)[None, :]
    ).reshape(-1)
    permuted = jnp.take(coarse_rows, positions, axis=1)

    def neighbour_margin(rounded):
        face_packs = rounded[margin_rows]
        along_first = padded(face_packs[0:2], (("gx", 0),), 1)
        along_second = padded(face_packs[2:4], (("gy", 0),), 1)
        return jnp.stack([along_first[0], along_first[3], along_second[0], along_second[3]], axis=0)

    def add_piece(shard_rows):
        return jnp.dot(permuted, shard_rows, preferred_element_type=jnp.float32)

    def precondition(vector):
        rounded = vector.astype(jnp.bfloat16)
        extended = jnp.concatenate(
            [rounded, neighbour_margin(rounded).reshape(-1, system_count)], axis=0
        )
        local_part = jnp.dot(inverse_rows, extended, preferred_element_type=jnp.float32)
        residual = lax.dot_general(
            basis, rounded, (((0,), (0,)), ((), ())), preferred_element_type=jnp.float32
        ).astype(jnp.bfloat16)
        solved = add_piece(lax.all_gather(residual, ("gx", "gy"), axis=0, tiled=True))
        return local_part + jnp.dot(
            basis, solved.astype(jnp.bfloat16), preferred_element_type=jnp.float32
        )

    def apply_operator(vector):
        rounded = vector.astype(jnp.bfloat16)
        own_part = jnp.einsum(
            "brc,bcn->brn",
            local_block,
            rounded.reshape(-1, block_rows, system_count),
            preferred_element_type=jnp.float32,
        ).reshape(owned_rows, system_count)
        weighted = margin_weights[:, :, None] * neighbour_margin(rounded).astype(jnp.float32)
        coupling = (
            jnp.zeros((owned_rows, system_count), jnp.float32)
            .at[margin_rows.reshape(-1)]
            .add(weighted.reshape(-1, system_count))
        )
        return own_part - coupling

    def column_norm(vector):
        squares = lax.psum(jnp.sum(vector * vector, axis=0), ("gx", "gy"))
        return jnp.sqrt(squares + EPSILON)

    def project_single(vector, direction):
        return lax.psum(jnp.sum(vector * direction, axis=0), ("gx", "gy"))

    scale_norm = column_norm(right_side)
    krylov_one = right_side / scale_norm
    precond_one = precondition(krylov_one)
    applied = apply_operator(precond_one)
    first_dot = project_single(applied, krylov_one)
    remainder = applied - first_dot * krylov_one
    first_norm = column_norm(remainder)
    krylov_two = remainder / first_norm
    precond_two = precondition(krylov_two)
    applied = apply_operator(precond_two)
    cross_dot = project_single(applied, krylov_one)
    remainder = applied - cross_dot * krylov_one
    second_dot = project_single(remainder, krylov_two)
    remainder = remainder - second_dot * krylov_two
    second_norm = column_norm(remainder)
    weight_one, weight_two, relative = least_squares(
        scale_norm, first_dot, first_norm, cross_dot, second_dot, second_norm
    )
    solution = weight_one * precond_one + weight_two * precond_two
    return (solution[None, None], relative)


def solution(mesh):
    return jax.shard_map(
        on_device,
        mesh=mesh,
        in_specs=(
            P("gx", "gy", None, None),
            P("gx", "gy", None, None),
            P("gx", "gy", None, None),
            P("gx", "gy", None, None, None),
            P("gx", "gy", None, None),
            P("gx", "gy", None, None),
            P("gx", "gy", None, None),
            P(),
        ),
        out_specs=(P("gx", "gy", None, None), P()),
        check_vma=False,
    )
```

profile of v0, /device:TPU:6, one launch (start us, length us, event | category | flops | bytes accessed | tf_op | source)
XLA Modules:
  0.0 1065.0 jit_solution(7111828778543676201)
XLA Ops:
  7.2 0.9 fusion.22
  8.1 108.3 %psum.42 = f32[128]{0:T(128)S(1)} all-reduce(f32[128]{0:T(128)S(1)} %fusion.22), channel_id=1, replica_groups=mesh['gx'=64,'gy'=8] {'gx','gy'}, use_global_device_ids=true, to_apply=%region_1.2 | all-reduce | flops 128 | bytes 1024 | tf_op jit(solution)/shard_map/psum | solution.py:102
  116.4 1.6 fusion.6
  118.1 0.7 fusion.34
  118.8 0.8 fusion.42
  119.7 1.3 gather_fusion
  121.0 3.2 collective-permute-start
  124.2 1.9 collective-permute-start.2
  126.2 1.3 collective-permute-start.1
  127.5 3.6 collective-permute-start.3
  131.1 0.7 broadcast_multiply_fusion
  132.4 4.6 copy.18
  137.0 57.6 %gather_fusion.1 = bf16[16384,32]{1,0:T(8,128)(2,1)} fusion(bf16[32,16384]{0,1:T(8,128)(2,1)} %bitcast.121, s32[16384]{0:T(1024)S(1)} %broadcast_clamp_fusion), kind=kCustom, calls=%fused_computation.1 | custom fusion | bytes 2162688 | tf_op jit(solution)/shard_map/jit(_take)/gather | solution.py:60
  195.0 116.6 %all-gather.3.cloned.1.call-done = bf16[16384,128]{1,0:T(8,128)(2,1)} async-done(((bf16[32,128]{1,0:T(8,128)(2,1)}), bf16[16384,128]{1,0:T(8,128)(2,1)}) %all-gather.3.cloned.1.call-update) | async-done | bytes 4194320 | tf_op jit(solution)/shard_map/all_gather | solution.py:80
  311.6 7.1 convolution_add_fusion.1
  318.8 1.3 gather_fusion.2
  320.2 3.3 collective-permute-start.4
  323.5 1.9 collective-permute-start.6
  325.4 1.3 collective-permute-start.5
  326.7 3.6 collective-permute-start.7
  330.4 0.8 collective-permute-done.5
  331.2 0.7 collective-permute-done.7
  332.0 2.4 scatter_custom_fusion
  334.6 102.9 %psum.43 = f32[128]{0:T(128)S(1)} all-reduce(f32[128]{0:T(128)S(1)} %get-tuple-element.29), channel_id=1, replica_groups=mesh['gx'=64,'gy'=8] {'gx','gy'}, use_global_device_ids=true, to_apply=%region_4.5 | all-reduce | flops 128 | bytes 1024 | tf_op jit(solution)/shard_map/psum | solution.py:106
  437.5 99.8 %psum.44 = f32[128]{0:T(128)S(1)} all-reduce(f32[128]{0:T(128)S(1)} %multiply_reduce_fusion.3), channel_id=1, replica_groups=mesh['gx'=64,'gy'=8] {'gx','gy'}, use_global_device_ids=true, to_apply=%region_6.7 | all-reduce | flops 128 | bytes 1024 | tf_op jit(solution)/shard_map/psum | solution.py:102
  537.4 0.7 fusion.7
  538.1 1.3 gather_fusion.3
  539.5 1.9 collective-permute-start.8
  541.4 1.9 collective-permute-start.10
  543.3 1.3 collective-permute-start.9
  544.6 3.8 collective-permute-start.11
  548.5 0.7 collective-permute-done.9
  549.1 0.7 collective-permute-done.11
  550.1 181.0 %all-gather.5.cloned.1.call-done = bf16[16384,128]{1,0:T(8,128)(2,1)} async-done(((bf16[32,128]{1,0:T(8,128)(2,1)}), bf16[16384,128]{1,0:T(8,128)(2,1)}) %all-gather.5.cloned.1.call-update) | async-done | bytes 4194320 | tf_op jit(solution)/shard_map/all_gather | solution.py:80
  731.2 7.1 convolution_add_fusion
  738.4 1.3 gather_fusion.4
  739.7 3.3 collective-permute-start.12
  743.1 1.9 collective-permute-start.14
  745.0 1.3 collective-permute-start.13
  746.3 3.6 collective-permute-start.15
  750.0 0.8 collective-permute-done.13
  750.8 0.7 collective-permute-done.15
  751.6 2.4 scatter_custom_fusion.1
  754.2 102.9 %psum.45 = f32[128]{0:T(128)S(1)} all-reduce(f32[128]{0:T(128)S(1)} %get-tuple-element.31), channel_id=1, replica_groups=mesh['gx'=64,'gy'=8] {'gx','gy'}, use_global_device_ids=true, to_apply=%region_9.10 | all-reduce | flops 128 | bytes 1024 | tf_op jit(solution)/shard_map/psum | solution.py:106
  857.1 99.8 %psum.46 = f32[128]{0:T(128)S(1)} all-reduce(f32[128]{0:T(128)S(1)} %multiply_reduce_fusion.1), channel_id=1, replica_groups=mesh['gx'=64,'gy'=8] {'gx','gy'}, use_global_device_ids=true, to_apply=%region_11.12 | all-reduce | flops 128 | bytes 1024 | tf_op jit(solution)/shard_map/psum | solution.py:106
  957.0 99.8 %psum.47 = f32[128]{0:T(128)S(1)} all-reduce(f32[128]{0:T(128)S(1)} %multiply_reduce_fusion), channel_id=1, replica_groups=mesh['gx'=64,'gy'=8] {'gx','gy'}, use_global_device_ids=true, to_apply=%region_13.14 | all-reduce | flops 128 | bytes 1024 | tf_op jit(solution)/shard_map/psum | solution.py:102
  1056.7 0.6 divide_multiply_fusion
  1057.4 0.7 copy.21
  (58 shorter events, 2.2 us)
Async XLA Ops:
  7.2 187.5 %copy-start = (bf16[1,1,128,640]{3,2,1,0:T(8,128)(2,1)S(1)}, bf16[1,1,128,640]{3,2,1,0:T(8,128)(2,1)}, u32[]{:S(2)}) copy-start(bf16[1,1,128,640]{3,2,1,0:T(8,128)(2,1)} %param.12) | copy-start | bytes 491524
  7.2 304.4 %all-gather.3.cloned.1.call-start = ((), (), s32[]{:S(2)}) async-start(), calls=%async_computation | async-start | bytes 4202496 | tf_op jit(solution)/shard_map/all_gather | solution.py:80
  118.1 613.1 %all-gather.5.cloned.1.call-start = ((), (), s32[]{:S(2)}) async-start(), calls=%async_computation.1 | async-start | bytes 4202496 | tf_op jit(solution)/shard_map/all_gather | solution.py:80
  121.0 73.6 %collective-permute-start = (bf16[1,128,128]{2,1,0:T(8,128)(2,1)S(1)}, bf16[1,128,128]{2,1,0:T(8,128)(2,1)S(1)}, u32[]{:S(2)}, u32[]{:S(2)}) collective-permute-start(bf16[1,128,128]{2,1,0:T(8,128)(2,1)S(1)} %get-tuple-element.25), channel_id=1, source_target_pairs={{0,8},{8,16},{16,24},{24,32},{32,40},{40,48},{48,56},{56,64},{64,7... | collective-permute-start | bytes 98312 | tf_op jit(solution)/shard_map/ppermute | solution.py:16
  124.2 70.4 %collective-permute-start.2 = (bf16[1,128,128]{2,1,0:T(8,128)(2,1)S(1)}, bf16[1,128,128]{2,1,0:T(8,128)(2,1)S(1)}, u32[]{:S(2)}, u32[]{:S(2)}) collective-permute-start(bf16[1,128,128]{2,1,0:T(8,128)(2,1)S(1)} %get-tuple-element.26), channel_id=1, source_target_pairs={{0,1},{1,2},{2,3},{3,4},{4,5},{5,6},{6,7},{8,9},{9,10},{10,11},{11... | collective-permute-start | bytes 98312 | tf_op jit(solution)/shard_map/ppermute | solution.py:16
  126.2 68.4 %collective-permute-start.1 = (bf16[1,128,128]{2,1,0:T(8,128)(2,1)S(1)}, bf16[1,128,128]{2,1,0:T(8,128)(2,1)S(1)}, u32[]{:S(2)}, u32[]{:S(2)}) collective-permute-start(bf16[1,128,128]{2,1,0:T(8,128)(2,1)S(1)} %get-tuple-element.27), channel_id=1, source_target_pairs={{8,0},{16,8},{24,16},{32,24},{40,32},{48,40},{56,48},{64,56},{72,6... | collective-permute-start | bytes 98312 | tf_op jit(solution)/shard_map/ppermute | solution.py:17
  127.5 67.2 %collective-permute-start.3 = (bf16[1,128,128]{2,1,0:T(8,128)(2,1)S(1)}, bf16[1,128,128]{2,1,0:T(8,128)(2,1)S(1)}, u32[]{:S(2)}, u32[]{:S(2)}) collective-permute-start(bf16[1,128,128]{2,1,0:T(8,128)(2,1)S(1)} %get-tuple-element.28), channel_id=1, source_target_pairs={{1,0},{2,1},{3,2},{4,3},{5,4},{6,5},{7,6},{9,8},{10,9},{11,10},{12... | collective-permute-start | bytes 98312 | tf_op jit(solution)/shard_map/ppermute | solution.py:17
  137.0 174.6 %copy-start.5 = (bf16[1,1,128,32]{2,3,1,0:T(8,128)(2,1)S(1)}, bf16[1,1,128,32]{2,3,1,0:T(8,128)(2,1)}, u32[]{:S(2)}) copy-start(bf16[1,1,128,32]{2,3,1,0:T(8,128)(2,1)} %param.13) | copy-start | bytes 24580
  194.9 135.5 %copy-start.4 = (s32[1,1,4,128]{3,2,1,0:T(4,128)S(1)}, s32[1,1,4,128]{3,2,1,0:T(4,128)}, u32[]{:S(2)}) copy-start(s32[1,1,4,128]{3,2,1,0:T(4,128)} %param.9) | copy-start | bytes 6148
  194.9 137.0 %copy-start.3 = (f32[1,1,4,128]{3,2,1,0:T(4,128)S(1)}, f32[1,1,4,128]{3,2,1,0:T(4,128)}, u32[]{:S(2)}) copy-start(f32[1,1,4,128]{3,2,1,0:T(4,128)} %param.10) | copy-start | bytes 6148
  194.9 139.4 %copy-start.1 = (f32[1,1,128,128]{3,2,1,0:T(8,128)S(1)}, f32[1,1,128,128]{3,2,1,0:T(8,128)}, u32[]{:S(2)}) copy-start(f32[1,1,128,128]{3,2,1,0:T(8,128)} %param.8) | copy-start | bytes 196612
  195.0 139.4 %copy-start.2 = (bf16[1,1,1,128,128]{4,3,2,1,0:T(8,128)(2,1)S(1)}, bf16[1,1,1,128,128]{4,3,2,1,0:T(8,128)(2,1)}, u32[]{:S(2)}) copy-start(bf16[1,1,1,128,128]{4,3,2,1,0:T(8,128)(2,1)} %param.11) | copy-start | bytes 98308
  320.2 10.2 collective-permute-start.4
  323.5 6.9 collective-permute-start.6
  325.4 5.8 collective-permute-start.5
  326.7 5.2 collective-permute-start.7
  539.5 9.0 collective-permute-start.8
  541.4 7.1 collective-permute-start.10
  543.3 5.8 collective-permute-start.9
  544.6 5.2 collective-permute-start.11
  739.7 10.2 collective-permute-start.12
  743.1 6.9 collective-permute-start.14
  745.0 5.8 collective-permute-start.13
  746.3 5.2 collective-permute-start.15
Sparse Core Ops, SparseCore 0:
  118.2 193.3 all-gather.2
  538.3 192.8 all-gather.4
where the time goes:
time: 1070 us
  blocking collectives  613 us (57%)
  waiting for transfers between devices  302 us (28%)
  local copies, waits for them, and re-layouts  68.9 us (6%)
  starting transfers between devices  39.4 us (4%)
  matrix products  17.3 us (2%)
  between operations  14.5 us (1%)
    psum x3, blocking collectives, column_norm(): squares = lax.psum(jnp.sum(vector * vector, axis=0), ('gx', 'gy'))  308 us
    psum x3, blocking collectives, project_single(): return lax.psum(jnp.sum(vector * direction, axis=0), ('gx', 'gy'))  306 us
    all_gather x2, waiting for transfers between devices, precondition(): lax.all_gather(residual, ('gx', 'gy'), axis=0, tiled=True)  298 us
    gather x1, local copies, waits for them, and re-layouts, on_device(): permuted = jnp.take(coarse_rows, positions, axis=1)  57.6 us
  transfers between devices with their start and end apart: 18, of which 8 were waited for; matrix products, arithmetic and copies ran while one was open for 6% of the time, Pallas kernels for 0%

commit v1 on v0

v1 whole, which is shorter than its diff:
```python
import jax
import jax.numpy as jnp
from jax import lax
from jax.sharding import PartitionSpec as P

EPSILON = 1e-06


def neighbours(rows, axis):
    count = lax.axis_size(axis)
    up = [(i, i + 1) for i in range(count - 1)]
    down = [(i + 1, i) for i in range(count - 1)]
    return lax.ppermute(rows[1], axis, up), lax.ppermute(rows[0], axis, down)


def exchange(packs):
    below_first, above_first = neighbours(packs[0:2], "gx")
    below_second, above_second = neighbours(packs[2:4], "gy")
    return jnp.stack([below_first, above_first, below_second, above_second], axis=0)


def allsum(value):
    for axis in ("gy", "gx"):
        count = lax.axis_size(axis)
        if count & (count - 1):
            value = lax.psum(value, axis)
            continue
        step = 1
        while step < count:
            value = value + lax.ppermute(value, axis, [(i, i ^ step) for i in range(count)])
            step *= 2
    return value


def least_squares(scale_norm, first_dot, first_norm, cross_dot, second_dot, second_norm):
    radius_one = jnp.sqrt(first_dot * first_dot + first_norm * first_norm)
    cosine_one = first_dot / radius_one
    sine_one = first_norm / radius_one
    upper_entry = cosine_one * cross_dot + sine_one * second_dot
    lower_entry = cosine_one * second_dot - sine_one * cross_dot
    radius_two = jnp.sqrt(lower_entry * lower_entry + second_norm * second_norm)
    cosine_two = lower_entry / radius_two
    sine_two = second_norm / radius_two
    weight_two = -cosine_two * sine_one * scale_norm / radius_two
    weight_one = (cosine_one * scale_norm - upper_entry * weight_two) / radius_one
    return (weight_one, weight_two, sine_one * sine_two)


def on_device(
    rhs,
    face_rows,
    margin_weight,
    local_blocks,
    subdomain_inverse,
    coarse_basis,
    coarse_inverse,
    coarse_map,
):
    right_side = rhs[0, 0]
    margin_rows = face_rows[0, 0]
    margin_weights = margin_weight[0, 0]
    local_block = local_blocks[0, 0]
    inverse_rows = subdomain_inverse[0, 0]
    basis = coarse_basis[0, 0]
    coarse_rows = coarse_inverse[0, 0]
    owned_rows = right_side.shape[0]
    system_count = right_side.shape[1]
    basis_count = basis.shape[1]
    block_rows = local_block.shape[1]
    count_x = lax.axis_size("gx")
    count_y = lax.axis_size("gy")
    gathered_map = coarse_map.reshape(count_x, count_y).T.reshape(-1)
    positions = (
        gathered_map[:, None] * basis_count + jnp.arange(basis_count, dtype=jnp.int32)[None, :]
    ).reshape(-1)
    permuted = jnp.take(coarse_rows, positions, axis=1)

    def margin_of(field):
        return exchange(field[margin_rows])

    def coarse_gather(residual):
        return lax.all_gather(
            lax.all_gather(residual, "gx", axis=0, tiled=True), "gy", axis=0, tiled=True
        )

    def precondition(rounded, margin):
        extended = jnp.concatenate([rounded, margin.reshape(-1, system_count)], axis=0)
        local_part = jnp.dot(inverse_rows, extended, preferred_element_type=jnp.float32)
        residual = lax.dot_general(
            basis, rounded, (((0,), (0,)), ((), ())), preferred_element_type=jnp.float32
        ).astype(jnp.bfloat16)
        solved = jnp.dot(permuted, coarse_gather(residual), preferred_element_type=jnp.float32)
        return local_part + jnp.dot(
            basis, solved.astype(jnp.bfloat16), preferred_element_type=jnp.float32
        )

    def apply_operator(vector):
        rounded = vector.astype(jnp.bfloat16)
        own_part = jnp.einsum(
            "brc,bcn->brn",
            local_block,
            rounded.reshape(-1, block_rows, system_count),
            preferred_element_type=jnp.float32,
        ).reshape(owned_rows, system_count)
        weighted = margin_weights[:, :, None] * margin_of(rounded).astype(jnp.float32)
        coupling = (
            jnp.zeros((owned_rows, system_count), jnp.float32)
            .at[margin_rows.reshape(-1)]
            .add(weighted.reshape(-1, system_count))
        )
        return own_part - coupling

    def column_norm(vector):
        return jnp.sqrt(allsum(jnp.sum(vector * vector, axis=0)) + EPSILON)

    rhs_margin = margin_of(right_side)
    scale_norm = column_norm(right_side)
    krylov_one = right_side / scale_norm
    margin_one = rhs_margin / scale_norm
    precond_one = precondition(krylov_one.astype(jnp.bfloat16), margin_one.astype(jnp.bfloat16))
    applied = apply_operator(precond_one)
    applied_margin = margin_of(applied)
    first_dot = allsum(jnp.sum(applied * krylov_one, axis=0))
    remainder = applied - first_dot * krylov_one
    first_norm = column_norm(remainder)
    krylov_two = remainder / first_norm
    margin_two = (applied_margin - first_dot * margin_one) / first_norm
    precond_two = precondition(krylov_two.astype(jnp.bfloat16), margin_two.astype(jnp.bfloat16))
    applied = apply_operator(precond_two)
    dots = allsum(
        jnp.stack([jnp.sum(applied * krylov_one, axis=0), jnp.sum(applied * krylov_two, axis=0)])
    )
    cross_dot = dots[0]
    second_dot = dots[1]
    remainder = applied - cross_dot * krylov_one - second_dot * krylov_two
    second_norm = column_norm(remainder)
    weight_one, weight_two, relative = least_squares(
        scale_norm, first_dot, first_norm, cross_dot, second_dot, second_norm
    )
    solution = weight_one * precond_one + weight_two * precond_two
    return (solution[None, None], relative)


def solution(mesh):
    return jax.shard_map(
        on_device,
        mesh=mesh,
        in_specs=(
            P("gx", "gy", None, None),
            P("gx", "gy", None, None),
            P("gx", "gy", None, None),
            P("gx", "gy", None, None, None),
            P("gx", "gy", None, None),
            P("gx", "gy", None, None),
            P("gx", "gy", None, None),
            P(),
        ),
        out_specs=(P("gx", "gy", None, None), P()),
        check_vma=False,
    )
```

time: 1070 us -> 730 us (0.68)
  blocking collectives: 613 us -> 221 us
  starting transfers between devices: 39.4 us -> 272 us
  waiting for transfers between devices: 302 us -> 126 us
    psum x6 -> x0, blocking collectives: 613 us -> none  [the longest x3 308 us: column_norm(): squares = lax.psum(jnp.sum(vector * vector, axis=0), ('gx', 'gy'))]
    all_gather x2, waiting for transfers between devices: 298 us -> 23.1 us  [coarse_gather(): lax.all_gather(lax.all_gather(residual, 'gx', axis=0, tiled=True), 'gy',...]
    ppermute x16 -> x61, starting transfers between devices: 39.4 us -> 272 us  [the longest x45 231 us: allsum(): lax.ppermute(value, axis, [(i, i ^ step) for i in range(count)])]
    all_gather x0 -> x2, blocking collectives: none -> 221 us  [coarse_gather(): lax.all_gather(residual, 'gx', axis=0, tiled=True)]
    ppermute x16 -> x61, waiting for transfers between devices: 4.49 us -> 102 us  [the longest x45 97.4 us: allsum(): lax.ppermute(value, axis, [(i, i ^ step) for i in range(count)])]
  transfers between devices with their start and end apart: 18 -> 63, of which waited for: 8 -> 52; matrix products, arithmetic and copies ran while one was open for 6% -> 9% of each run, Pallas kernels for 0% -> 0%
where the time goes in v1:
time: 730 us; the launch traced here: 726 us
  starting transfers between devices  272 us (37%)
  blocking collectives  221 us (30%)
  waiting for transfers between devices  126 us (17%)
  local copies, waits for them, and re-layouts  68.6 us (9%)
  matrix products  16.1 us (2%)
  between operations  15 us (2%)
  other arithmetic  7.87 us (1%)
    ppermute x45, starting transfers between devices, allsum(): lax.ppermute(value, axis, [(i, i ^ step) for i in range(count)])  231 us
    all_gather x2, blocking collectives, coarse_gather(): lax.all_gather(residual, 'gx', axis=0, tiled=True)  221 us
    ppermute x45, waiting for transfers between devices, allsum(): lax.ppermute(value, axis, [(i, i ^ step) for i in range(count)])  97.4 us
    gather x1, local copies, waits for them, and re-layouts, on_device(): permuted = jnp.take(coarse_rows, positions, axis=1)  58.3 us
    ppermute x16, starting transfers between devices, neighbours(): return (lax.ppermute(rows[1], axis, up), lax.ppermute(rows[0], axis, down))  41.4 us
    all_gather x2, waiting for transfers between devices, coarse_gather(): lax.all_gather(lax.all_gather(residual, 'gx', axis=0, tiled=True), 'gy',...  23.1 us
  transfers between devices with their start and end apart: 63, of which 52 were waited for; matrix products, arithmetic and copies ran while one was open for 9% of the time, Pallas kernels for 0%

profile of v1, /device:TPU:6, one launch (start us, length us, event | category | flops | bytes accessed | tf_op | source)
XLA Modules:
  0.0 726.2 jit_solution(14645991461228601917)
XLA Ops:
  16.7 7.2 collective-permute-start.2
  27.3 3.5 collective-permute-done.3
  34.2 3.6 collective-permute-done.4
  43.3 3.4 collective-permute-start.6
  49.7 7.7 %collective-permute-start.7 = (f32[128]{0:T(128)S(1)}, f32[128]{0:T(128)S(1)}, u32[]{:S(2)}, u32[]{:S(2)}) collective-permute-start(f32[128]{0:T(128)S(1)} %add.251), channel_id=1, source_target_pairs={{0,128},{8,136},{16,144},{24,152},{32,160},{40,168},{48,176},{56,1... | collective-permute-start | bytes 1544 | tf_op jit(solution)/shard_map/ppermute | solution.py:30
  59.0 14.0 %collective-permute-start.8 = (f32[128]{0:T(128)S(1)}, f32[128]{0:T(128)S(1)}, u32[]{:S(2)}, u32[]{:S(2)}) collective-permute-start(f32[128]{0:T(128)S(1)} %add.252), channel_id=1, source_target_pairs={{0,256},{8,264},{16,272},{24,280},{32,288},{40,296},{48,304},{56,3... | collective-permute-start | bytes 1544 | tf_op jit(solution)/shard_map/ppermute | solution.py:30
  75.5 112.7 %all_gather.12 = bf16[2048,128]{1,0:T(8,128)(2,1)} all-gather(bf16[32,128]{1,0:T(8,128)(2,1)S(1)} %fusion.6), channel_id=1, replica_groups=mesh['gx'=64,'gy'=8] {'gx'}, dimensions={0}, use_global_device_ids=true | all-gather | bytes 532480 | tf_op jit(solution)/shard_map/all_gather | solution.py:83
  196.7 3.6 collective-permute-start.12
  204.3 58.3 %gather_fusion.1 = bf16[16384,32]{1,0:T(8,128)(2,1)} fusion(bf16[32,16384]{0,1:T(8,128)(2,1)} %bitcast.133, s32[16384]{0:T(1024)S(1)} %broadcast_clamp_fusion), kind=kCustom, calls=%fused_computation.1 | custom fusion | bytes 2162688 | tf_op jit(solution)/shard_map/jit(_take)/gather | solution.py:76
  263.1 7.1 convolution_add_fusion.1
  271.7 4.3 collective-permute-start.13
  279.2 3.6 collective-permute-start.16
  290.1 3.7 collective-permute-start.18
  295.6 4.6 collective-permute-start.19
  302.5 4.3 collective-permute-start.20
  308.3 7.2 collective-permute-start.21
  317.0 6.4 collective-permute-start.22
  324.9 3.8 collective-permute-start.23
  331.3 8.3 %collective-permute-start.24 = (f32[128]{0:T(128)S(1)}, f32[128]{0:T(128)S(1)}, u32[]{:S(2)}, u32[]{:S(2)}) collective-permute-start(f32[128]{0:T(128)S(1)} %add.273), channel_id=1, source_target_pairs={{0,128},{8,136},{16,144},{24,152},{32,160},{40,168},{48,176},{56,1... | collective-permute-start | bytes 1544 | tf_op jit(solution)/shard_map/ppermute | solution.py:30
  341.2 11.4 %collective-permute-start.25 = (f32[128]{0:T(128)S(1)}, f32[128]{0:T(128)S(1)}, u32[]{:S(2)}, u32[]{:S(2)}) collective-permute-start(f32[128]{0:T(128)S(1)} %add.274), channel_id=1, source_target_pairs={{0,256},{8,264},{16,272},{24,280},{32,288},{40,296},{48,304},{56,3... | collective-permute-start | bytes 1544 | tf_op jit(solution)/shard_map/ppermute | solution.py:30
  358.4 3.7 collective-permute-start.27
  363.9 4.6 collective-permute-start.28
  372.8 3.5 collective-permute-done.29
  379.4 3.9 collective-permute-done.30
  383.3 3.4 collective-permute-start.31
  395.1 7.8 %collective-permute-start.33 = (f32[128]{0:T(128)S(1)}, f32[128]{0:T(128)S(1)}, u32[]{:S(2)}, u32[]{:S(2)}) collective-permute-start(f32[128]{0:T(128)S(1)} %add.282), channel_id=1, source_target_pairs={{0,128},{8,136},{16,144},{24,152},{32,160},{40,168},{48,176},{56,1... | collective-permute-start | bytes 1544 | tf_op jit(solution)/shard_map/ppermute | solution.py:30
  404.4 11.4 %collective-permute-start.34 = (f32[128]{0:T(128)S(1)}, f32[128]{0:T(128)S(1)}, u32[]{:S(2)}, u32[]{:S(2)}) collective-permute-start(f32[128]{0:T(128)S(1)} %add.283), channel_id=1, source_target_pairs={{0,256},{8,264},{16,272},{24,280},{32,288},{40,296},{48,304},{56,3... | collective-permute-start | bytes 1544 | tf_op jit(solution)/shard_map/ppermute | solution.py:30
  418.8 108.2 %all_gather.14 = bf16[2048,128]{1,0:T(8,128)(2,1)} all-gather(bf16[32,128]{1,0:T(8,128)(2,1)S(1)} %fusion.7), channel_id=1, replica_groups=mesh['gx'=64,'gy'=8] {'gx'}, dimensions={0}, use_global_device_ids=true | all-gather | bytes 532480 | tf_op jit(solution)/shard_map/all_gather | solution.py:83
  528.1 3.5 collective-permute-start.35
  534.9 3.6 collective-permute-start.38
  540.8 23.1 %all-gather.5.cloned.1.call-done = bf16[16384,128]{1,0:T(8,128)(2,1)} async-done(((bf16[2048,128]{1,0:T(8,128)(2,1)}), bf16[16384,128]{1,0:T(8,128)(2,1)}) %all-gather.5.cloned.1.call-update) | async-done | bytes 4194320 | tf_op jit(solution)/shard_map/all_gather | solution.py:82
  563.9 7.1 convolution_add_fusion
  572.5 3.4 collective-permute-start.39
  579.1 3.6 collective-permute-start.42
  590.0 3.7 collective-permute-start.44
  595.5 5.1 collective-permute-start.45
  602.5 4.3 collective-permute-start.46
  608.3 5.4 collective-permute-start.47
  615.3 6.1 collective-permute-start.48
  622.9 4.9 collective-permute-start.49
  629.4 9.2 %collective-permute-start.50 = (f32[2,128]{1,0:T(2,128)S(1)}, f32[2,128]{1,0:T(2,128)S(1)}, u32[]{:S(2)}, u32[]{:S(2)}) collective-permute-start(f32[2,128]{1,0:T(2,128)S(1)} %add.294), channel_id=1, source_target_pairs={{0,128},{8,136},{16,144},{24,152},{32,160},{40,168},{48,176},{56,1... | collective-permute-start | bytes 3080 | tf_op jit(solution)/shard_map/ppermute | solution.py:30
  640.1 13.0 %collective-permute-start.51 = (f32[2,128]{1,0:T(2,128)S(1)}, f32[2,128]{1,0:T(2,128)S(1)}, u32[]{:S(2)}, u32[]{:S(2)}) collective-permute-start(f32[2,128]{1,0:T(2,128)S(1)} %add.295), channel_id=1, source_target_pairs={{0,256},{8,264},{16,272},{24,280},{32,288},{40,296},{48,304},{56,3... | collective-permute-start | bytes 3080 | tf_op jit(solution)/shard_map/ppermute | solution.py:30
  657.8 3.7 collective-permute-start.53
  663.2 5.1 collective-permute-start.54
  672.1 3.5 collective-permute-done.55
  678.3 4.3 collective-permute-done.56
  694.4 7.5 %collective-permute-start.59 = (f32[128]{0:T(128)S(1)}, f32[128]{0:T(128)S(1)}, u32[]{:S(2)}, u32[]{:S(2)}) collective-permute-start(f32[128]{0:T(128)S(1)} %add.304), channel_id=1, source_target_pairs={{0,128},{8,136},{16,144},{24,152},{32,160},{40,168},{48,176},{56,1... | collective-permute-start | bytes 1544 | tf_op jit(solution)/shard_map/ppermute | solution.py:30
  703.8 12.6 %collective-permute-start.60 = (f32[128]{0:T(128)S(1)}, f32[128]{0:T(128)S(1)}, u32[]{:S(2)}, u32[]{:S(2)}) collective-permute-start(f32[128]{0:T(128)S(1)} %add.305), channel_id=1, source_target_pairs={{0,256},{8,264},{16,272},{24,280},{32,288},{40,296},{48,304},{56,3... | collective-permute-start | bytes 1544 | tf_op jit(solution)/shard_map/ppermute | solution.py:30
  (196 shorter events, 153.5 us)
Async XLA Ops:
  7.2 255.9 %all-gather.3.cloned.1.call-start = ((), (), s32[]{:S(2)}) async-start(), calls=%async_computation | async-start | bytes 4718592 | tf_op jit(solution)/shard_map/all_gather | solution.py:82
  16.7 8.7 %collective-permute-start.2 = (f32[128]{0:T(128)S(1)}, f32[128]{0:T(128)S(1)}, u32[]{:S(2)}, u32[]{:S(2)}) collective-permute-start(f32[128]{0:T(128)S(1)} %add.246), channel_id=1, source_target_pairs={{0,4},{1,5},{2,6},{3,7},{4,0},{5,1},{6,2},{7,3},{8,12},{9,13},{10,... | collective-permute-start | bytes 1544 | tf_op jit(solution)/shard_map/ppermute | solution.py:30
  30.9 7.0 collective-permute-start.4
  43.3 6.3 collective-permute-start.6
  49.7 9.4 %collective-permute-start.7 = (f32[128]{0:T(128)S(1)}, f32[128]{0:T(128)S(1)}, u32[]{:S(2)}, u32[]{:S(2)}) collective-permute-start(f32[128]{0:T(128)S(1)} %add.251), channel_id=1, source_target_pairs={{0,128},{8,136},{16,144},{24,152},{32,160},{40,168},{48,176},{56,1... | collective-permute-start | bytes 1544 | tf_op jit(solution)/shard_map/ppermute | solution.py:30
  59.0 15.5 %collective-permute-start.8 = (f32[128]{0:T(128)S(1)}, f32[128]{0:T(128)S(1)}, u32[]{:S(2)}, u32[]{:S(2)}) collective-permute-start(f32[128]{0:T(128)S(1)} %add.252), channel_id=1, source_target_pairs={{0,256},{8,264},{16,272},{24,280},{32,288},{40,296},{48,304},{56,3... | collective-permute-start | bytes 1544 | tf_op jit(solution)/shard_map/ppermute | solution.py:30
  188.2 375.7 %all-gather.5.cloned.1.call-start = ((), (), s32[]{:S(2)}) async-start(), calls=%async_computation.1 | async-start | bytes 4718592 | tf_op jit(solution)/shard_map/all_gather | solution.py:82
  190.9 71.8 %collective-permute-start.9 = (f32[128,128]{1,0:T(8,128)S(1)}, f32[128,128]{1,0:T(8,128)S(1)}, u32[]{:S(2)}, u32[]{:S(2)}) collective-permute-start(f32[128,128]{1,0:T(8,128)S(1)} %get-tuple-element.19), channel_id=1, source_target_pairs={{0,8},{8,16},{16,24},{24,32},{32,40},{40,48},{48,56},{56,64},{64,7... | collective-permute-start | bytes 196616 | tf_op jit(solution)/shard_map/ppermute | solution.py:13
  193.5 69.2 %collective-permute-start.11 = (f32[128,128]{1,0:T(8,128)S(1)}, f32[128,128]{1,0:T(8,128)S(1)}, u32[]{:S(2)}, u32[]{:S(2)}) collective-permute-start(f32[128,128]{1,0:T(8,128)S(1)} %get-tuple-element.20), channel_id=1, source_target_pairs={{0,1},{1,2},{2,3},{3,4},{4,5},{5,6},{6,7},{8,9},{9,10},{10,11},{11... | collective-permute-start | bytes 196616 | tf_op jit(solution)/shard_map/ppermute | solution.py:13
  195.4 67.3 %collective-permute-start.10 = (f32[128,128]{1,0:T(8,128)S(1)}, f32[128,128]{1,0:T(8,128)S(1)}, u32[]{:S(2)}, u32[]{:S(2)}) collective-permute-start(f32[128,128]{1,0:T(8,128)S(1)} %get-tuple-element.21), channel_id=1, source_target_pairs={{8,0},{16,8},{24,16},{32,24},{40,32},{48,40},{56,48},{64,56},{72,6... | collective-permute-start | bytes 196616 | tf_op jit(solution)/shard_map/ppermute | solution.py:13
  196.7 66.0 %collective-permute-start.12 = (f32[128,128]{1,0:T(8,128)S(1)}, f32[128,128]{1,0:T(8,128)S(1)}, u32[]{:S(2)}, u32[]{:S(2)}) collective-permute-start(f32[128,128]{1,0:T(8,128)S(1)} %get-tuple-element.22), channel_id=1, source_target_pairs={{1,0},{2,1},{3,2},{4,3},{5,4},{6,5},{7,6},{9,8},{10,9},{11,10},{12... | collective-permute-start | bytes 196616 | tf_op jit(solution)/shard_map/ppermute | solution.py:13
  271.7 11.2 %collective-permute-start.13 = (bf16[128,128]{1,0:T(8,128)(2,1)S(1)}, bf16[128,128]{1,0:T(8,128)(2,1)S(1)}, u32[]{:S(2)}, u32[]{:S(2)}) collective-permute-start(bf16[128,128]{1,0:T(8,128)(2,1)S(1)} %get-tuple-element.27), channel_id=1, source_target_pairs={{0,8},{8,16},{16,24},{24,32},{32,40},{40,48},{48,56},{56,64},{64,7... | collective-permute-start | bytes 98312 | tf_op jit(solution)/shard_map/ppermute | solution.py:13
  276.0 6.9 collective-permute-start.15
  277.9 5.8 collective-permute-start.14
  295.6 7.0 collective-permute-start.19
  302.5 5.8 collective-permute-start.20
  308.3 8.7 %collective-permute-start.21 = (f32[128]{0:T(128)S(1)}, f32[128]{0:T(128)S(1)}, u32[]{:S(2)}, u32[]{:S(2)}) collective-permute-start(f32[128]{0:T(128)S(1)} %add.270), channel_id=1, source_target_pairs={{0,16},{8,24},{16,0},{24,8},{32,48},{40,56},{48,32},{56,40},{64,80... | collective-permute-start | bytes 1544 | tf_op jit(solution)/shard_map/ppermute | solution.py:30
  317.0 7.9 %collective-permute-start.22 = (f32[128]{0:T(128)S(1)}, f32[128]{0:T(128)S(1)}, u32[]{:S(2)}, u32[]{:S(2)}) collective-permute-start(f32[128]{0:T(128)S(1)} %add.271), channel_id=1, source_target_pairs={{0,32},{8,40},{16,48},{24,56},{32,0},{40,8},{48,16},{56,24},{64,96... | collective-permute-start | bytes 1544 | tf_op jit(solution)/shard_map/ppermute | solution.py:30
  324.9 6.3 collective-permute-start.23
  331.3 9.9 %collective-permute-start.24 = (f32[128]{0:T(128)S(1)}, f32[128]{0:T(128)S(1)}, u32[]{:S(2)}, u32[]{:S(2)}) collective-permute-start(f32[128]{0:T(128)S(1)} %add.273), channel_id=1, source_target_pairs={{0,128},{8,136},{16,144},{24,152},{32,160},{40,168},{48,176},{56,1... | collective-permute-start | bytes 1544 | tf_op jit(solution)/shard_map/ppermute | solution.py:30
  341.2 14.2 %collective-permute-start.25 = (f32[128]{0:T(128)S(1)}, f32[128]{0:T(128)S(1)}, u32[]{:S(2)}, u32[]{:S(2)}) collective-permute-start(f32[128]{0:T(128)S(1)} %add.274), channel_id=1, source_target_pairs={{0,256},{8,264},{16,272},{24,280},{32,288},{40,296},{48,304},{56,3... | collective-permute-start | bytes 1544 | tf_op jit(solution)/shard_map/ppermute | solution.py:30
  363.9 7.0 collective-permute-start.28
  370.8 5.5 collective-permute-start.29
  376.3 7.0 collective-permute-start.30
  383.3 5.5 collective-permute-start.31
  388.7 6.3 collective-permute-start.32
  395.1 9.4 %collective-permute-start.33 = (f32[128]{0:T(128)S(1)}, f32[128]{0:T(128)S(1)}, u32[]{:S(2)}, u32[]{:S(2)}) collective-permute-start(f32[128]{0:T(128)S(1)} %add.282), channel_id=1, source_target_pairs={{0,128},{8,136},{16,144},{24,152},{32,160},{40,168},{48,176},{56,1... | collective-permute-start | bytes 1544 | tf_op jit(solution)/shard_map/ppermute | solution.py:30
  404.4 14.2 %collective-permute-start.34 = (f32[128]{0:T(128)S(1)}, f32[128]{0:T(128)S(1)}, u32[]{:S(2)}, u32[]{:S(2)}) collective-permute-start(f32[128]{0:T(128)S(1)} %add.283), channel_id=1, source_target_pairs={{0,256},{8,264},{16,272},{24,280},{32,288},{40,296},{48,304},{56,3... | collective-permute-start | bytes 1544 | tf_op jit(solution)/shard_map/ppermute | solution.py:30
  528.1 10.5 %collective-permute-start.35 = (f32[128,128]{1,0:T(8,128)S(1)}, f32[128,128]{1,0:T(8,128)S(1)}, u32[]{:S(2)}, u32[]{:S(2)}) collective-permute-start(f32[128,128]{1,0:T(8,128)S(1)} %get-tuple-element.15), channel_id=1, source_target_pairs={{0,8},{8,16},{16,24},{24,32},{32,40},{40,48},{48,56},{56,64},{64,7... | collective-permute-start | bytes 196616 | tf_op jit(solution)/shard_map/ppermute | solution.py:13
  531.5 7.1 collective-permute-start.37
  533.5 6.2 collective-permute-start.36
  534.9 5.5 collective-permute-start.38
  572.5 10.3 %collective-permute-start.39 = (bf16[128,128]{1,0:T(8,128)(2,1)S(1)}, bf16[128,128]{1,0:T(8,128)(2,1)S(1)}, u32[]{:S(2)}, u32[]{:S(2)}) collective-permute-start(bf16[128,128]{1,0:T(8,128)(2,1)S(1)} %get-tuple-element.23), channel_id=1, source_target_pairs={{0,8},{8,16},{16,24},{24,32},{32,40},{40,48},{48,56},{56,64},{64,7... | collective-permute-start | bytes 98312 | tf_op jit(solution)/shard_map/ppermute | solution.py:13
  575.9 6.9 collective-permute-start.41
  577.8 5.8 collective-permute-start.40
  590.0 5.5 collective-permute-start.44
  595.5 7.0 collective-permute-start.45
  602.5 5.8 collective-permute-start.46
  608.3 7.0 collective-permute-start.47
  615.3 7.6 %collective-permute-start.48 = (f32[2,128]{1,0:T(2,128)S(1)}, f32[2,128]{1,0:T(2,128)S(1)}, u32[]{:S(2)}, u32[]{:S(2)}) collective-permute-start(f32[2,128]{1,0:T(2,128)S(1)} %add.292), channel_id=1, source_target_pairs={{0,32},{8,40},{16,48},{24,56},{32,0},{40,8},{48,16},{56,24},{64,96... | collective-permute-start | bytes 3080 | tf_op jit(solution)/shard_map/ppermute | solution.py:30
  622.9 6.4 collective-permute-start.49
  629.4 10.8 %collective-permute-start.50 = (f32[2,128]{1,0:T(2,128)S(1)}, f32[2,128]{1,0:T(2,128)S(1)}, u32[]{:S(2)}, u32[]{:S(2)}) collective-permute-start(f32[2,128]{1,0:T(2,128)S(1)} %add.294), channel_id=1, source_target_pairs={{0,128},{8,136},{16,144},{24,152},{32,160},{40,168},{48,176},{56,1... | collective-permute-start | bytes 3080 | tf_op jit(solution)/shard_map/ppermute | solution.py:30
  640.1 14.5 %collective-permute-start.51 = (f32[2,128]{1,0:T(2,128)S(1)}, f32[2,128]{1,0:T(2,128)S(1)}, u32[]{:S(2)}, u32[]{:S(2)}) collective-permute-start(f32[2,128]{1,0:T(2,128)S(1)} %add.295), channel_id=1, source_target_pairs={{0,256},{8,264},{16,272},{24,280},{32,288},{40,296},{48,304},{56,3... | collective-permute-start | bytes 3080 | tf_op jit(solution)/shard_map/ppermute | solution.py:30
  663.2 7.0 collective-permute-start.54
  675.6 7.0 collective-permute-start.56
  688.1 6.3 collective-permute-start.58
  694.4 9.4 %collective-permute-start.59 = (f32[128]{0:T(128)S(1)}, f32[128]{0:T(128)S(1)}, u32[]{:S(2)}, u32[]{:S(2)}) collective-permute-start(f32[128]{0:T(128)S(1)} %add.304), channel_id=1, source_target_pairs={{0,128},{8,136},{16,144},{24,152},{32,160},{40,168},{48,176},{56,1... | collective-permute-start | bytes 1544 | tf_op jit(solution)/shard_map/ppermute | solution.py:30
  703.8 14.2 %collective-permute-start.60 = (f32[128]{0:T(128)S(1)}, f32[128]{0:T(128)S(1)}, u32[]{:S(2)}, u32[]{:S(2)}) collective-permute-start(f32[128]{0:T(128)S(1)} %add.305), channel_id=1, source_target_pairs={{0,256},{8,264},{16,272},{24,280},{32,288},{40,296},{48,304},{56,3... | collective-permute-start | bytes 1544 | tf_op jit(solution)/shard_map/ppermute | solution.py:30
  (23 other events, 894.1 us)
Sparse Core Ops, SparseCore 0:
  188.4 32.3 all-gather.2
  527.1 36.7 all-gather.4

commit v2 on v1

--- a/solution.py
+++ b/solution.py
@@ -1,4 +1,5 @@
 import jax
+import numpy as np
 import jax.numpy as jnp
 from jax import lax
 from jax.sharding import PartitionSpec as P
@@ -30,6 +31,38 @@
             value = value + lax.ppermute(value, axis, [(i, i ^ step) for i in range(count)])
             step *= 2
     return value
+
+
+GATHER_ROUNDS = (
+    ("gx", 32), ("gx", 16), ("gx", 8), ("gx", 4), ("gx", 2), ("gx", 1), ("gy", 4), ("gy", 2), ("gy", 1),
+)
+
+
+def gather_rounds(count_x, count_y):
+    sizes = {"gx": count_x, "gy": count_y}
+    return tuple((axis, step) for axis, step in GATHER_ROUNDS if step < sizes[axis])
+
+
+def doubling_gather(block, rounds):
+    held = block[None]
+    for axis, step in rounds:
+        count = lax.axis_size(axis)
+        got = lax.ppermute(held, axis, [(i, i ^ step) for i in range(count)])
+        upper = (lax.axis_index(axis) // step) % 2 == 1
+        held = jnp.where(
+            upper, jnp.concatenate([got, held], axis=0), jnp.concatenate([held, got], axis=0)
+        )
+    return held.reshape(-1, block.shape[-1])
+
+
+def gathered_order(rounds, count_y):
+    order = []
+    for position in range(2 ** len(rounds)):
+        index = {"gx": 0, "gy": 0}
+        for bit, (axis, step) in enumerate(rounds):
+            index[axis] += ((position >> bit) & 1) * step
+        order.append(index["gx"] * count_y + index["gy"])
+    return np.asarray(order, np.int32)
 
 
 def least_squares(scale_norm, first_dot, first_norm, cross_dot, second_dot, second_norm):
@@ -69,19 +102,23 @@
     block_rows = local_block.shape[1]
     count_x = lax.axis_size("gx")
     count_y = lax.axis_size("gy")
-    gathered_map = coarse_map.reshape(count_x, count_y).T.reshape(-1)
-    positions = (
-        gathered_map[:, None] * basis_count + jnp.arange(basis_count, dtype=jnp.int32)[None, :]
-    ).reshape(-1)
-    permuted = jnp.take(coarse_rows, positions, axis=1)
+    rounds = gather_rounds(count_x, count_y)
+    gathered_map = coarse_map[gathered_order(rounds, count_y)]
+    selection = (
+        gathered_map[:, None] == jnp.arange(gathered_map.shape[0], dtype=jnp.int32)[None, :]
+    ).astype(coarse_rows.dtype)
+    permuted = jnp.einsum(
+        "bq,rqc->rbc",
+        selection,
+        coarse_rows.reshape(basis_count, -1, basis_count),
+        preferred_element_type=jnp.float32,
+    ).astype(coarse_rows.dtype).reshape(basis_count, -1)
 
     def margin_of(field):
         return exchange(field[margin_rows])
 
     def coarse_gather(residual):
-        return lax.all_gather(
-            lax.all_gather(residual, "gx", axis=0, tiled=True), "gy", axis=0, tiled=True
-        )
+        return doubling_gather(residual, rounds)
 
     def precondition(rounded, margin):
         extended = jnp.concatenate([rounded, margin.reshape(-1, system_count)], axis=0)

time: 730 us -> 618 us (0.85)
  blocking collectives: 221 us -> 0 us
  waiting for transfers between devices: 126 us -> 215 us
  starting transfers between devices: 272 us -> 348 us
  local copies, waits for them, and re-layouts: 68.6 us -> 25.9 us
  between operations: 15 us -> 2.04 us
    all_gather x2 -> x0, blocking collectives: 221 us -> none  [coarse_gather(): lax.all_gather(residual, 'gx', axis=0, tiled=True)]
    ppermute x0 -> x18, waiting for transfers between devices: none -> 101 us  [doubling_gather(): got = lax.ppermute(held, axis, [(i, i ^ step) for i in range(count)])]
    ppermute x0 -> x18, starting transfers between devices: none -> 79.4 us  [doubling_gather(): got = lax.ppermute(held, axis, [(i, i ^ step) for i in range(count)])]
    gather x1, local copies, waits for them, and re-layouts: 58.3 us -> 3.49 us  [on_device(): gathered_map = coarse_map[gathered_order(rounds, count_y)]]
    all_gather x2 -> x0, waiting for transfers between devices: 23.1 us -> none  [coarse_gather(): lax.all_gather(lax.all_gather(residual, 'gx', axis=0, tiled=True), 'gy',...]
    ppermute x45, waiting for transfers between devices: 97.4 us -> 109 us  [allsum(): lax.ppermute(value, axis, [(i, i ^ step) for i in range(count)])]
    another operation x0 -> x2, local copies, waits for them, and re-layouts: none -> 7.91 us  [on_device(): coarse_rows.reshape(basis_count, -1, basis_count)]
  transfers between devices with their start and end apart: 63 -> 79, of which waited for: 52 -> 65; matrix products, arithmetic and copies ran while one was open for 9% -> 4% of each run, Pallas kernels for 0% -> 0%
where the time goes in v2:
time: 618 us; the launch traced here: 615 us
  starting transfers between devices  348 us (56%)
  waiting for transfers between devices  215 us (35%)
  local copies, waits for them, and re-layouts  25.9 us (4%)
  matrix products  13.2 us (2%)
  other arithmetic  10.8 us (2%)
    ppermute x45, starting transfers between devices, allsum(): lax.ppermute(value, axis, [(i, i ^ step) for i in range(count)])  225 us
    ppermute x45, waiting for transfers between devices, allsum(): lax.ppermute(value, axis, [(i, i ^ step) for i in range(count)])  109 us
    ppermute x18, waiting for transfers between devices, doubling_gather(): got = lax.ppermute(held, axis, [(i, i ^ step) for i in range(count)])  101 us
    ppermute x18, starting transfers between devices, doubling_gather(): got = lax.ppermute(held, axis, [(i, i ^ step) for i in range(count)])  79.4 us
    ppermute x16, starting transfers between devices, neighbours(): return (lax.ppermute(rows[1], axis, up), lax.ppermute(rows[0], axis, down))  44.1 us
  transfers between devices with their start and end apart: 79, of which 65 were waited for; matrix products, arithmetic and copies ran while one was open for 4% of the time, Pallas kernels for 0%

profile of v2, /device:TPU:6, one launch (start us, length us, event | category | flops | bytes accessed | tf_op | source)
XLA Modules:
  0.0 615.1 jit_solution(9220306237715375837)
XLA Ops:
  10.1 7.2 %collective-permute-start.2 = (f32[128]{0:T(128)S(1)}, f32[128]{0:T(128)S(1)}, u32[]{:S(2)}, u32[]{:S(2)}) collective-permute-start(f32[128]{0:T(128)S(1)} %add.248), channel_id=1, source_target_pairs={{0,4},{1,5},{2,6},{3,7},{4,0},{5,1},{6,2},{7,3},{8,12},{9,13},{10,... | collective-permute-start | bytes 1544 | tf_op jit(solution)/shard_map/ppermute | solution.py:31
  43.0 7.7 %collective-permute-start.7 = (f32[128]{0:T(128)S(1)}, f32[128]{0:T(128)S(1)}, u32[]{:S(2)}, u32[]{:S(2)}) collective-permute-start(f32[128]{0:T(128)S(1)} %add.253), channel_id=1, source_target_pairs={{0,128},{8,136},{16,144},{24,152},{32,160},{40,168},{48,176},{56,1... | collective-permute-start | bytes 1544 | tf_op jit(solution)/shard_map/ppermute | solution.py:31
  52.4 14.0 %collective-permute-start.8 = (f32[128]{0:T(128)S(1)}, f32[128]{0:T(128)S(1)}, u32[]{:S(2)}, u32[]{:S(2)}) collective-permute-start(f32[128]{0:T(128)S(1)} %add.254), channel_id=1, source_target_pairs={{0,256},{8,264},{16,272},{24,280},{32,288},{40,296},{48,304},{56,3... | collective-permute-start | bytes 1544 | tf_op jit(solution)/shard_map/ppermute | solution.py:31
  68.9 12.6 %collective-permute-start.13 = (bf16[1,32,128]{2,1,0:T(8,128)(2,1)S(1)}, bf16[1,32,128]{2,1,0:T(8,128)(2,1)S(1)}, u32[]{:S(2)}, u32[]{:S(2)}) collective-permute-start(bf16[1,32,128]{2,1,0:T(8,128)(2,1)S(1)} %fusion.20), channel_id=1, source_target_pairs={{0,256},{8,264},{16,272},{24,280},{32,288},{40,296},{48,304},{56,3... | collective-permute-start | bytes 24584 | tf_op jit(solution)/shard_map/ppermute | solution.py:50
  83.1 6.4 %collective-permute-start.14 = (bf16[2,32,128]{2,1,0:T(8,128)(2,1)S(1)}, bf16[2,32,128]{2,1,0:T(8,128)(2,1)S(1)}, u32[]{:S(2)}, u32[]{:S(2)}) collective-permute-start(bf16[2,32,128]{2,1,0:T(8,128)(2,1)S(1)} %maximum_select_fusion.30), channel_id=1, source_target_pairs={{0,128},{8,136},{16,144},{24,152},{32,160},{40,168},{48,176},{56,1... | collective-permute-start | bytes 49160 | tf_op jit(solution)/shard_map/ppermute | solution.py:50
  105.7 5.1 collective-permute-start.17
  117.6 4.8 collective-permute-done.18
  122.4 4.1 collective-permute-start.19
  126.5 14.1 %collective-permute-done.19 = bf16[64,32,128]{2,1,0:T(8,128)(2,1)S(1)} collective-permute-done((bf16[64,32,128]{2,1,0:T(8,128)(2,1)S(1)}, bf16[64,32,128]{2,1,0:T(8,128)(2,1)S(1)}, u32[]{:S(2)}, u32[]{:S(2)}) %collective-permute-start.19) | collective-permute-done | bytes 524320 | tf_op jit(solution)/shard_map/ppermute | solution.py:50
  143.6 14.0 %collective-permute-done.20 = bf16[128,32,128]{2,1,0:T(8,128)(2,1)} collective-permute-done((bf16[128,32,128]{2,1,0:T(8,128)(2,1)S(1)}, bf16[128,32,128]{2,1,0:T(8,128)(2,1)}, u32[]{:S(2)}, u32[]{:S(2)}) %collective-permute-start.20) | collective-permute-done | bytes 1048608 | tf_op jit(solution)/shard_map/ppermute | solution.py:50
  170.9 5.2 collective-permute-start.9
  176.1 4.4 reshape_squeeze.7
  188.6 6.4 %copy.20 = bf16[32,512,32]{2,0,1:T(8,128)(2,1)} copy(bf16[32,512,32]{1,2,0:T(8,128)(2,1)S(1)} %convert_bitcast_fusion) | data formatting | bytes 2097152 | tf_op jit(solution)/shard_map/convert_element_type | solution.py:115
  196.4 5.2 convolution_add_fusion.1
  209.4 4.5 collective-permute-start.22
  226.7 4.8 collective-permute-start.28
  233.7 4.2 collective-permute-start.29
  239.4 7.2 %collective-permute-start.30 = (f32[128]{0:T(128)S(1)}, f32[128]{0:T(128)S(1)}, u32[]{:S(2)}, u32[]{:S(2)}) collective-permute-start(f32[128]{0:T(128)S(1)} %add.274), channel_id=1, source_target_pairs={{0,16},{8,24},{16,0},{24,8},{32,48},{40,56},{48,32},{56,40},{64,80... | collective-permute-start | bytes 1544 | tf_op jit(solution)/shard_map/ppermute | solution.py:31
  248.2 7.7 %collective-permute-start.31 = (f32[128]{0:T(128)S(1)}, f32[128]{0:T(128)S(1)}, u32[]{:S(2)}, u32[]{:S(2)}) collective-permute-start(f32[128]{0:T(128)S(1)} %add.275), channel_id=1, source_target_pairs={{0,32},{8,40},{16,48},{24,56},{32,0},{40,8},{48,16},{56,24},{64,96... | collective-permute-start | bytes 1544 | tf_op jit(solution)/shard_map/ppermute | solution.py:31
  257.5 4.4 collective-permute-start.32
  263.8 10.1 %collective-permute-start.33 = (f32[128]{0:T(128)S(1)}, f32[128]{0:T(128)S(1)}, u32[]{:S(2)}, u32[]{:S(2)}) collective-permute-start(f32[128]{0:T(128)S(1)} %add.277), channel_id=1, source_target_pairs={{0,128},{8,136},{16,144},{24,152},{32,160},{40,168},{48,176},{56,1... | collective-permute-start | bytes 1544 | tf_op jit(solution)/shard_map/ppermute | solution.py:31
  275.5 12.9 %collective-permute-start.34 = (f32[128]{0:T(128)S(1)}, f32[128]{0:T(128)S(1)}, u32[]{:S(2)}, u32[]{:S(2)}) collective-permute-start(f32[128]{0:T(128)S(1)} %add.278), channel_id=1, source_target_pairs={{0,256},{8,264},{16,272},{24,280},{32,288},{40,296},{48,304},{56,3... | collective-permute-start | bytes 1544 | tf_op jit(solution)/shard_map/ppermute | solution.py:31
  312.8 5.0 collective-permute-done.39
  325.2 4.4 collective-permute-done.41
  329.6 7.6 %collective-permute-start.42 = (f32[128]{0:T(128)S(1)}, f32[128]{0:T(128)S(1)}, u32[]{:S(2)}, u32[]{:S(2)}) collective-permute-start(f32[128]{0:T(128)S(1)} %add.286), channel_id=1, source_target_pairs={{0,128},{8,136},{16,144},{24,152},{32,160},{40,168},{48,176},{56,1... | collective-permute-start | bytes 1544 | tf_op jit(solution)/shard_map/ppermute | solution.py:31
  339.0 12.6 %collective-permute-start.43 = (f32[128]{0:T(128)S(1)}, f32[128]{0:T(128)S(1)}, u32[]{:S(2)}, u32[]{:S(2)}) collective-permute-start(f32[128]{0:T(128)S(1)} %add.287), channel_id=1, source_target_pairs={{0,256},{8,264},{16,272},{24,280},{32,288},{40,296},{48,304},{56,3... | collective-permute-start | bytes 1544 | tf_op jit(solution)/shard_map/ppermute | solution.py:31
  353.3 12.6 %collective-permute-start.48 = (bf16[1,32,128]{2,1,0:T(8,128)(2,1)S(1)}, bf16[1,32,128]{2,1,0:T(8,128)(2,1)S(1)}, u32[]{:S(2)}, u32[]{:S(2)}) collective-permute-start(bf16[1,32,128]{2,1,0:T(8,128)(2,1)S(1)} %fusion.21), channel_id=1, source_target_pairs={{0,256},{8,264},{16,272},{24,280},{32,288},{40,296},{48,304},{56,3... | collective-permute-start | bytes 24584 | tf_op jit(solution)/shard_map/ppermute | solution.py:50
  367.6 7.6 %collective-permute-start.49 = (bf16[2,32,128]{2,1,0:T(8,128)(2,1)S(1)}, bf16[2,32,128]{2,1,0:T(8,128)(2,1)S(1)}, u32[]{:S(2)}, u32[]{:S(2)}) collective-permute-start(bf16[2,32,128]{2,1,0:T(8,128)(2,1)S(1)} %maximum_select_fusion.31), channel_id=1, source_target_pairs={{0,128},{8,136},{16,144},{24,152},{32,160},{40,168},{48,176},{56,1... | collective-permute-start | bytes 49160 | tf_op jit(solution)/shard_map/ppermute | solution.py:50
  379.5 4.5 collective-permute-done.50
  385.9 4.2 collective-permute-done.51
  392.2 6.3 %collective-permute-done.52 = bf16[16,32,128]{2,1,0:T(8,128)(2,1)S(1)} collective-permute-done((bf16[16,32,128]{2,1,0:T(8,128)(2,1)S(1)}, bf16[16,32,128]{2,1,0:T(8,128)(2,1)S(1)}, u32[]{:S(2)}, u32[]{:S(2)}) %collective-permute-start.52) | collective-permute-done | bytes 131104 | tf_op jit(solution)/shard_map/ppermute | solution.py:50
  400.5 6.3 %collective-permute-done.53 = bf16[32,32,128]{2,1,0:T(8,128)(2,1)S(1)} collective-permute-done((bf16[32,32,128]{2,1,0:T(8,128)(2,1)S(1)}, bf16[32,32,128]{2,1,0:T(8,128)(2,1)S(1)}, u32[]{:S(2)}, u32[]{:S(2)}) %collective-permute-start.53) | collective-permute-done | bytes 262176 | tf_op jit(solution)/shard_map/ppermute | solution.py:50
  410.5 14.4 %collective-permute-done.54 = bf16[64,32,128]{2,1,0:T(8,128)(2,1)S(1)} collective-permute-done((bf16[64,32,128]{2,1,0:T(8,128)(2,1)S(1)}, bf16[64,32,128]{2,1,0:T(8,128)(2,1)S(1)}, u32[]{:S(2)}, u32[]{:S(2)}) %collective-permute-start.54) | collective-permute-done | bytes 524320 | tf_op jit(solution)/shard_map/ppermute | solution.py:50
  427.9 13.8 %collective-permute-done.55 = bf16[128,32,128]{2,1,0:T(8,128)(2,1)S(1)} collective-permute-done((bf16[128,32,128]{2,1,0:T(8,128)(2,1)S(1)}, bf16[128,32,128]{2,1,0:T(8,128)(2,1)S(1)}, u32[]{:S(2)}, u32[]{:S(2)}) %collective-permute-start.55) | collective-permute-done | bytes 1048608 | tf_op jit(solution)/shard_map/ppermute | solution.py:50
  451.3 4.5 collective-permute-start.44
  458.1 5.2 convolution_add_fusion
  471.1 5.0 collective-permute-start.57
  495.8 4.2 collective-permute-start.64
  501.6 6.0 collective-permute-start.65
  509.1 6.0 collective-permute-start.66
  516.6 5.1 collective-permute-start.67
  523.2 10.7 %collective-permute-start.68 = (f32[2,128]{1,0:T(2,128)S(1)}, f32[2,128]{1,0:T(2,128)S(1)}, u32[]{:S(2)}, u32[]{:S(2)}) collective-permute-start(f32[2,128]{1,0:T(2,128)S(1)} %add.298), channel_id=1, source_target_pairs={{0,128},{8,136},{16,144},{24,152},{32,160},{40,168},{48,176},{56,1... | collective-permute-start | bytes 3080 | tf_op jit(solution)/shard_map/ppermute | solution.py:31
  535.5 13.3 %collective-permute-start.69 = (f32[2,128]{1,0:T(2,128)S(1)}, f32[2,128]{1,0:T(2,128)S(1)}, u32[]{:S(2)}, u32[]{:S(2)}) collective-permute-start(f32[2,128]{1,0:T(2,128)S(1)} %add.299), channel_id=1, source_target_pairs={{0,256},{8,264},{16,272},{24,280},{32,288},{40,296},{48,304},{56,3... | collective-permute-start | bytes 3080 | tf_op jit(solution)/shard_map/ppermute | solution.py:31
  561.8 4.0 collective-permute-done.72
  573.3 5.0 collective-permute-done.74
  585.7 4.4 collective-permute-done.76
  590.1 7.1 %collective-permute-start.77 = (f32[128]{0:T(128)S(1)}, f32[128]{0:T(128)S(1)}, u32[]{:S(2)}, u32[]{:S(2)}) collective-permute-start(f32[128]{0:T(128)S(1)} %add.308), channel_id=1, source_target_pairs={{0,128},{8,136},{16,144},{24,152},{32,160},{40,168},{48,176},{56,1... | collective-permute-start | bytes 1544 | tf_op jit(solution)/shard_map/ppermute | solution.py:31
  599.5 12.6 %collective-permute-start.78 = (f32[128]{0:T(128)S(1)}, f32[128]{0:T(128)S(1)}, u32[]{:S(2)}, u32[]{:S(2)}) collective-permute-start(f32[128]{0:T(128)S(1)} %add.309), channel_id=1, source_target_pairs={{0,256},{8,264},{16,272},{24,280},{32,288},{40,296},{48,304},{56,3... | collective-permute-start | bytes 1544 | tf_op jit(solution)/shard_map/ppermute | solution.py:31
  (237 shorter events, 253.5 us)
Async XLA Ops:
  10.1 8.7 %collective-permute-start.2 = (f32[128]{0:T(128)S(1)}, f32[128]{0:T(128)S(1)}, u32[]{:S(2)}, u32[]{:S(2)}) collective-permute-start(f32[128]{0:T(128)S(1)} %add.248), channel_id=1, source_target_pairs={{0,4},{1,5},{2,6},{3,7},{4,0},{5,1},{6,2},{7,3},{8,12},{9,13},{10,... | collective-permute-start | bytes 1544 | tf_op jit(solution)/shard_map/ppermute | solution.py:31
  24.2 7.0 %collective-permute-start.4 = (f32[128]{0:T(128)S(1)}, f32[128]{0:T(128)S(1)}, u32[]{:S(2)}, u32[]{:S(2)}) collective-permute-start(f32[128]{0:T(128)S(1)} %add.250), channel_id=1, source_target_pairs={{0,16},{8,24},{16,0},{24,8},{32,48},{40,56},{48,32},{56,40},{64,80... | collective-permute-start | bytes 1544 | tf_op jit(solution)/shard_map/ppermute | solution.py:31
  43.0 9.4 %collective-permute-start.7 = (f32[128]{0:T(128)S(1)}, f32[128]{0:T(128)S(1)}, u32[]{:S(2)}, u32[]{:S(2)}) collective-permute-start(f32[128]{0:T(128)S(1)} %add.253), channel_id=1, source_target_pairs={{0,128},{8,136},{16,144},{24,152},{32,160},{40,168},{48,176},{56,1... | collective-permute-start | bytes 1544 | tf_op jit(solution)/shard_map/ppermute | solution.py:31
  52.4 15.5 %collective-permute-start.8 = (f32[128]{0:T(128)S(1)}, f32[128]{0:T(128)S(1)}, u32[]{:S(2)}, u32[]{:S(2)}) collective-permute-start(f32[128]{0:T(128)S(1)} %add.254), channel_id=1, source_target_pairs={{0,256},{8,264},{16,272},{24,280},{32,288},{40,296},{48,304},{56,3... | collective-permute-start | bytes 1544 | tf_op jit(solution)/shard_map/ppermute | solution.py:31
  68.9 14.3 %collective-permute-start.13 = (bf16[1,32,128]{2,1,0:T(8,128)(2,1)S(1)}, bf16[1,32,128]{2,1,0:T(8,128)(2,1)S(1)}, u32[]{:S(2)}, u32[]{:S(2)}) collective-permute-start(bf16[1,32,128]{2,1,0:T(8,128)(2,1)S(1)} %fusion.20), channel_id=1, source_target_pairs={{0,256},{8,264},{16,272},{24,280},{32,288},{40,296},{48,304},{56,3... | collective-permute-start | bytes 24584 | tf_op jit(solution)/shard_map/ppermute | solution.py:50
  83.1 9.6 %collective-permute-start.14 = (bf16[2,32,128]{2,1,0:T(8,128)(2,1)S(1)}, bf16[2,32,128]{2,1,0:T(8,128)(2,1)S(1)}, u32[]{:S(2)}, u32[]{:S(2)}) collective-permute-start(bf16[2,32,128]{2,1,0:T(8,128)(2,1)S(1)} %maximum_select_fusion.30), channel_id=1, source_target_pairs={{0,128},{8,136},{16,144},{24,152},{32,160},{40,168},{48,176},{56,1... | collective-permute-start | bytes 49160 | tf_op jit(solution)/shard_map/ppermute | solution.py:50
  92.8 6.7 %collective-permute-start.15 = (bf16[4,32,128]{2,1,0:T(8,128)(2,1)S(1)}, bf16[4,32,128]{2,1,0:T(8,128)(2,1)S(1)}, u32[]{:S(2)}, u32[]{:S(2)}) collective-permute-start(bf16[4,32,128]{2,1,0:T(8,128)(2,1)S(1)} %maximum_select_fusion.28), channel_id=1, source_target_pairs={{0,64},{8,72},{16,80},{24,88},{32,96},{40,104},{48,112},{56,120},{... | collective-permute-start | bytes 98312 | tf_op jit(solution)/shard_map/ppermute | solution.py:50
  105.7 8.4 %collective-permute-start.17 = (bf16[16,32,128]{2,1,0:T(8,128)(2,1)S(1)}, bf16[16,32,128]{2,1,0:T(8,128)(2,1)S(1)}, u32[]{:S(2)}, u32[]{:S(2)}) collective-permute-start(bf16[16,32,128]{2,1,0:T(8,128)(2,1)S(1)} %maximum_select_fusion.24), channel_id=1, source_target_pairs={{0,16},{8,24},{16,0},{24,8},{32,48},{40,56},{48,32},{56,40},{64,80... | collective-permute-start | bytes 393224 | tf_op jit(solution)/shard_map/ppermute | solution.py:50
  114.0 8.3 %collective-permute-start.18 = (bf16[32,32,128]{2,1,0:T(8,128)(2,1)S(1)}, bf16[32,32,128]{2,1,0:T(8,128)(2,1)S(1)}, u32[]{:S(2)}, u32[]{:S(2)}) collective-permute-start(bf16[32,32,128]{2,1,0:T(8,128)(2,1)S(1)} %maximum_select_fusion.22), channel_id=1, source_target_pairs={{0,8},{8,0},{16,24},{24,16},{32,40},{40,32},{48,56},{56,48},{64,72... | collective-permute-start | bytes 786440 | tf_op jit(solution)/shard_map/ppermute | solution.py:50
  122.4 18.2 %collective-permute-start.19 = (bf16[64,32,128]{2,1,0:T(8,128)(2,1)S(1)}, bf16[64,32,128]{2,1,0:T(8,128)(2,1)S(1)}, u32[]{:S(2)}, u32[]{:S(2)}) collective-permute-start(bf16[64,32,128]{2,1,0:T(8,128)(2,1)S(1)} %maximum_select_fusion.20), channel_id=1, source_target_pairs={{0,4},{1,5},{2,6},{3,7},{4,0},{5,1},{6,2},{7,3},{8,12},{9,13},{10,... | collective-permute-start | bytes 1572872 | tf_op jit(solution)/shard_map/ppermute | solution.py:50
  140.8 16.8 %collective-permute-start.20 = (bf16[128,32,128]{2,1,0:T(8,128)(2,1)S(1)}, bf16[128,32,128]{2,1,0:T(8,128)(2,1)}, u32[]{:S(2)}, u32[]{:S(2)}) collective-permute-start(bf16[128,32,128]{2,1,0:T(8,128)(2,1)S(1)} %maximum_select_fusion.18), channel_id=1, source_target_pairs={{0,2},{1,3},{2,0},{3,1},{4,6},{5,7},{6,4},{7,5},{8,10},{9,11},{10,... | collective-permute-start | bytes 3145736 | tf_op jit(solution)/shard_map/ppermute | solution.py:50
  159.5 36.8 %collective-permute-start.21 = (bf16[256,32,128]{2,1,0:T(8,128)(2,1)S(1)}, bf16[256,32,128]{2,1,0:T(8,128)(2,1)}, u32[]{:S(2)}, u32[]{:S(2)}) collective-permute-start(bf16[256,32,128]{2,1,0:T(8,128)(2,1)S(1)} %maximum_select_fusion.4), channel_id=1, source_target_pairs={{0,1},{1,0},{2,3},{3,2},{4,5},{5,4},{6,7},{7,6},{8,9},{9,8},{10,11... | collective-permute-start | bytes 6291464 | tf_op jit(solution)/shard_map/ppermute | solution.py:50
  164.9 30.2 %collective-permute-start.12 = (f32[128,128]{1,0:T(8,128)}, f32[128,128]{1,0:T(8,128)S(1)}, u32[]{:S(2)}, u32[]{:S(2)}) collective-permute-start(f32[128,128]{1,0:T(8,128)} %get-tuple-element.20), channel_id=1, source_target_pairs={{1,0},{2,1},{3,2},{4,3},{5,4},{6,5},{7,6},{9,8},{10,9},{11,10},{12... | collective-permute-start | bytes 196616 | tf_op jit(solution)/shard_map/ppermute | solution.py:14
  167.7 27.4 %collective-permute-start.11 = (f32[128,128]{1,0:T(8,128)}, f32[128,128]{1,0:T(8,128)}, u32[]{:S(2)}, u32[]{:S(2)}) collective-permute-start(f32[128,128]{1,0:T(8,128)} %get-tuple-element.18), channel_id=1, source_target_pairs={{0,1},{1,2},{2,3},{3,4},{4,5},{5,6},{6,7},{8,9},{9,10},{10,11},{11... | collective-permute-start | bytes 196616 | tf_op jit(solution)/shard_map/ppermute | solution.py:14
  169.6 25.4 %collective-permute-start.10 = (f32[128,128]{1,0:T(8,128)}, f32[128,128]{1,0:T(8,128)}, u32[]{:S(2)}, u32[]{:S(2)}) collective-permute-start(f32[128,128]{1,0:T(8,128)} %get-tuple-element.19), channel_id=1, source_target_pairs={{8,0},{16,8},{24,16},{32,24},{40,32},{48,40},{56,48},{64,56},{72,6... | collective-permute-start | bytes 196616 | tf_op jit(solution)/shard_map/ppermute | solution.py:14
  170.9 24.2 %collective-permute-start.9 = (f32[128,128]{1,0:T(8,128)S(1)}, f32[128,128]{1,0:T(8,128)}, u32[]{:S(2)}, u32[]{:S(2)}) collective-permute-start(f32[128,128]{1,0:T(8,128)S(1)} %get-tuple-element.17), channel_id=1, source_target_pairs={{0,8},{8,16},{16,24},{24,32},{32,40},{40,48},{48,56},{56,64},{64,7... | collective-permute-start | bytes 196616 | tf_op jit(solution)/shard_map/ppermute | solution.py:14
  203.1 10.9 %collective-permute-start.25 = (bf16[128,128]{1,0:T(8,128)(2,1)S(1)}, bf16[128,128]{1,0:T(8,128)(2,1)S(1)}, u32[]{:S(2)}, u32[]{:S(2)}) collective-permute-start(bf16[128,128]{1,0:T(8,128)(2,1)S(1)} %get-tuple-element.28), channel_id=1, source_target_pairs={{1,0},{2,1},{3,2},{4,3},{5,4},{6,5},{7,6},{9,8},{10,9},{11,10},{12... | collective-permute-start | bytes 98312 | tf_op jit(solution)/shard_map/ppermute | solution.py:14
  206.2 7.8 %collective-permute-start.24 = (bf16[128,128]{1,0:T(8,128)(2,1)S(1)}, bf16[128,128]{1,0:T(8,128)(2,1)S(1)}, u32[]{:S(2)}, u32[]{:S(2)}) collective-permute-start(bf16[128,128]{1,0:T(8,128)(2,1)S(1)} %get-tuple-element.26), channel_id=1, source_target_pairs={{0,1},{1,2},{2,3},{3,4},{4,5},{5,6},{6,7},{8,9},{9,10},{10,11},{11... | collective-permute-start | bytes 98312 | tf_op jit(solution)/shard_map/ppermute | solution.py:14
  226.7 7.0 %collective-permute-start.28 = (f32[128]{0:T(128)S(1)}, f32[128]{0:T(128)S(1)}, u32[]{:S(2)}, u32[]{:S(2)}) collective-permute-start(f32[128]{0:T(128)S(1)} %add.272), channel_id=1, source_target_pairs={{0,4},{1,5},{2,6},{3,7},{4,0},{5,1},{6,2},{7,3},{8,12},{9,13},{10,... | collective-permute-start | bytes 1544 | tf_op jit(solution)/shard_map/ppermute | solution.py:31
  239.4 8.8 %collective-permute-start.30 = (f32[128]{0:T(128)S(1)}, f32[128]{0:T(128)S(1)}, u32[]{:S(2)}, u32[]{:S(2)}) collective-permute-start(f32[128]{0:T(128)S(1)} %add.274), channel_id=1, source_target_pairs={{0,16},{8,24},{16,0},{24,8},{32,48},{40,56},{48,32},{56,40},{64,80... | collective-permute-start | bytes 1544 | tf_op jit(solution)/shard_map/ppermute | solution.py:31
  248.2 9.3 %collective-permute-start.31 = (f32[128]{0:T(128)S(1)}, f32[128]{0:T(128)S(1)}, u32[]{:S(2)}, u32[]{:S(2)}) collective-permute-start(f32[128]{0:T(128)S(1)} %add.275), channel_id=1, source_target_pairs={{0,32},{8,40},{16,48},{24,56},{32,0},{40,8},{48,16},{56,24},{64,96... | collective-permute-start | bytes 1544 | tf_op jit(solution)/shard_map/ppermute | solution.py:31
  263.8 11.6 %collective-permute-start.33 = (f32[128]{0:T(128)S(1)}, f32[128]{0:T(128)S(1)}, u32[]{:S(2)}, u32[]{:S(2)}) collective-permute-start(f32[128]{0:T(128)S(1)} %add.277), channel_id=1, source_target_pairs={{0,128},{8,136},{16,144},{24,152},{32,160},{40,168},{48,176},{56,1... | collective-permute-start | bytes 1544 | tf_op jit(solution)/shard_map/ppermute | solution.py:31
  275.5 14.4 %collective-permute-start.34 = (f32[128]{0:T(128)S(1)}, f32[128]{0:T(128)S(1)}, u32[]{:S(2)}, u32[]{:S(2)}) collective-permute-start(f32[128]{0:T(128)S(1)} %add.278), channel_id=1, source_target_pairs={{0,256},{8,264},{16,272},{24,280},{32,288},{40,296},{48,304},{56,3... | collective-permute-start | bytes 1544 | tf_op jit(solution)/shard_map/ppermute | solution.py:31
  298.4 7.0 %collective-permute-start.37 = (f32[128]{0:T(128)S(1)}, f32[128]{0:T(128)S(1)}, u32[]{:S(2)}, u32[]{:S(2)}) collective-permute-start(f32[128]{0:T(128)S(1)} %add.281), channel_id=1, source_target_pairs={{0,4},{1,5},{2,6},{3,7},{4,0},{5,1},{6,2},{7,3},{8,12},{9,13},{10,... | collective-permute-start | bytes 1544 | tf_op jit(solution)/shard_map/ppermute | solution.py:31
  310.9 7.0 %collective-permute-start.39 = (f32[128]{0:T(128)S(1)}, f32[128]{0:T(128)S(1)}, u32[]{:S(2)}, u32[]{:S(2)}) collective-permute-start(f32[128]{0:T(128)S(1)} %add.283), channel_id=1, source_target_pairs={{0,16},{8,24},{16,0},{24,8},{32,48},{40,56},{48,32},{56,40},{64,80... | collective-permute-start | bytes 1544 | tf_op jit(solution)/shard_map/ppermute | solution.py:31
  329.6 9.4 %collective-permute-start.42 = (f32[128]{0:T(128)S(1)}, f32[128]{0:T(128)S(1)}, u32[]{:S(2)}, u32[]{:S(2)}) collective-permute-start(f32[128]{0:T(128)S(1)} %add.286), channel_id=1, source_target_pairs={{0,128},{8,136},{16,144},{24,152},{32,160},{40,168},{48,176},{56,1... | collective-permute-start | bytes 1544 | tf_op jit(solution)/shard_map/ppermute | solution.py:31
  339.0 14.2 %collective-permute-start.43 = (f32[128]{0:T(128)S(1)}, f32[128]{0:T(128)S(1)}, u32[]{:S(2)}, u32[]{:S(2)}) collective-permute-start(f32[128]{0:T(128)S(1)} %add.287), channel_id=1, source_target_pairs={{0,256},{8,264},{16,272},{24,280},{32,288},{40,296},{48,304},{56,3... | collective-permute-start | bytes 1544 | tf_op jit(solution)/shard_map/ppermute | solution.py:31
  353.3 14.3 %collective-permute-start.48 = (bf16[1,32,128]{2,1,0:T(8,128)(2,1)S(1)}, bf16[1,32,128]{2,1,0:T(8,128)(2,1)S(1)}, u32[]{:S(2)}, u32[]{:S(2)}) collective-permute-start(bf16[1,32,128]{2,1,0:T(8,128)(2,1)S(1)} %fusion.21), channel_id=1, source_target_pairs={{0,256},{8,264},{16,272},{24,280},{32,288},{40,296},{48,304},{56,3... | collective-permute-start | bytes 24584 | tf_op jit(solution)/shard_map/ppermute | solution.py:50
  367.6 9.7 %collective-permute-start.49 = (bf16[2,32,128]{2,1,0:T(8,128)(2,1)S(1)}, bf16[2,32,128]{2,1,0:T(8,128)(2,1)S(1)}, u32[]{:S(2)}, u32[]{:S(2)}) collective-permute-start(bf16[2,32,128]{2,1,0:T(8,128)(2,1)S(1)} %maximum_select_fusion.31), channel_id=1, source_target_pairs={{0,128},{8,136},{16,144},{24,152},{32,160},{40,168},{48,176},{56,1... | collective-permute-start | bytes 49160 | tf_op jit(solution)/shard_map/ppermute | solution.py:50
  377.2 6.7 %collective-permute-start.50 = (bf16[4,32,128]{2,1,0:T(8,128)(2,1)S(1)}, bf16[4,32,128]{2,1,0:T(8,128)(2,1)S(1)}, u32[]{:S(2)}, u32[]{:S(2)}) collective-permute-start(bf16[4,32,128]{2,1,0:T(8,128)(2,1)S(1)} %maximum_select_fusion.29), channel_id=1, source_target_pairs={{0,64},{8,72},{16,80},{24,88},{32,96},{40,104},{48,112},{56,120},{... | collective-permute-start | bytes 98312 | tf_op jit(solution)/shard_map/ppermute | solution.py:50
  390.1 8.4 %collective-permute-start.52 = (bf16[16,32,128]{2,1,0:T(8,128)(2,1)S(1)}, bf16[16,32,128]{2,1,0:T(8,128)(2,1)S(1)}, u32[]{:S(2)}, u32[]{:S(2)}) collective-permute-start(bf16[16,32,128]{2,1,0:T(8,128)(2,1)S(1)} %maximum_select_fusion.25), channel_id=1, source_target_pairs={{0,16},{8,24},{16,0},{24,8},{32,48},{40,56},{48,32},{56,40},{64,80... | collective-permute-start | bytes 393224 | tf_op jit(solution)/shard_map/ppermute | solution.py:50
  398.5 8.3 %collective-permute-start.53 = (bf16[32,32,128]{2,1,0:T(8,128)(2,1)S(1)}, bf16[32,32,128]{2,1,0:T(8,128)(2,1)S(1)}, u32[]{:S(2)}, u32[]{:S(2)}) collective-permute-start(bf16[32,32,128]{2,1,0:T(8,128)(2,1)S(1)} %maximum_select_fusion.23), channel_id=1, source_target_pairs={{0,8},{8,0},{16,24},{24,16},{32,40},{40,32},{48,56},{56,48},{64,72... | collective-permute-start | bytes 786440 | tf_op jit(solution)/shard_map/ppermute | solution.py:50
  406.9 18.0 %collective-permute-start.54 = (bf16[64,32,128]{2,1,0:T(8,128)(2,1)S(1)}, bf16[64,32,128]{2,1,0:T(8,128)(2,1)S(1)}, u32[]{:S(2)}, u32[]{:S(2)}) collective-permute-start(bf16[64,32,128]{2,1,0:T(8,128)(2,1)S(1)} %maximum_select_fusion.21), channel_id=1, source_target_pairs={{0,4},{1,5},{2,6},{3,7},{4,0},{5,1},{6,2},{7,3},{8,12},{9,13},{10,... | collective-permute-start | bytes 1572872 | tf_op jit(solution)/shard_map/ppermute | solution.py:50
  425.1 16.7 %collective-permute-start.55 = (bf16[128,32,128]{2,1,0:T(8,128)(2,1)S(1)}, bf16[128,32,128]{2,1,0:T(8,128)(2,1)S(1)}, u32[]{:S(2)}, u32[]{:S(2)}) collective-permute-start(bf16[128,32,128]{2,1,0:T(8,128)(2,1)S(1)} %maximum_select_fusion.19), channel_id=1, source_target_pairs={{0,2},{1,3},{2,0},{3,1},{4,6},{5,7},{6,4},{7,5},{8,10},{9,11},{10,... | collective-permute-start | bytes 3145736 | tf_op jit(solution)/shard_map/ppermute | solution.py:50
  442.1 16.0 %collective-permute-start.56 = (bf16[256,32,128]{2,1,0:T(8,128)(2,1)S(1)}, bf16[256,32,128]{2,1,0:T(8,128)(2,1)}, u32[]{:S(2)}, u32[]{:S(2)}) collective-permute-start(bf16[256,32,128]{2,1,0:T(8,128)(2,1)S(1)} %maximum_select_fusion.5), channel_id=1, source_target_pairs={{0,1},{1,0},{2,3},{3,2},{4,5},{5,4},{6,7},{7,6},{8,9},{9,8},{10,11... | collective-permute-start | bytes 6291464 | tf_op jit(solution)/shard_map/ppermute | solution.py:50
  445.1 10.8 %collective-permute-start.47 = (f32[128,128]{1,0:T(8,128)S(1)}, f32[128,128]{1,0:T(8,128)S(1)}, u32[]{:S(2)}, u32[]{:S(2)}) collective-permute-start(f32[128,128]{1,0:T(8,128)S(1)} %get-tuple-element.16), channel_id=1, source_target_pairs={{1,0},{2,1},{3,2},{4,3},{5,4},{6,5},{7,6},{9,8},{10,9},{11,10},{12... | collective-permute-start | bytes 196616 | tf_op jit(solution)/shard_map/ppermute | solution.py:14
  448.1 7.8 %collective-permute-start.46 = (f32[128,128]{1,0:T(8,128)S(1)}, f32[128,128]{1,0:T(8,128)S(1)}, u32[]{:S(2)}, u32[]{:S(2)}) collective-permute-start(f32[128,128]{1,0:T(8,128)S(1)} %get-tuple-element.14), channel_id=1, source_target_pairs={{0,1},{1,2},{2,3},{3,4},{4,5},{5,6},{6,7},{8,9},{9,10},{10,11},{11... | collective-permute-start | bytes 196616 | tf_op jit(solution)/shard_map/ppermute | solution.py:14
  464.8 11.3 %collective-permute-start.60 = (bf16[128,128]{1,0:T(8,128)(2,1)S(1)}, bf16[128,128]{1,0:T(8,128)(2,1)S(1)}, u32[]{:S(2)}, u32[]{:S(2)}) collective-permute-start(bf16[128,128]{1,0:T(8,128)(2,1)S(1)} %get-tuple-element.24), channel_id=1, source_target_pairs={{1,0},{2,1},{3,2},{4,3},{5,4},{6,5},{7,6},{9,8},{10,9},{11,10},{12... | collective-permute-start | bytes 98312 | tf_op jit(solution)/shard_map/ppermute | solution.py:14
  467.9 8.3 %collective-permute-start.59 = (bf16[128,128]{1,0:T(8,128)(2,1)S(1)}, bf16[128,128]{1,0:T(8,128)(2,1)S(1)}, u32[]{:S(2)}, u32[]{:S(2)}) collective-permute-start(bf16[128,128]{1,0:T(8,128)(2,1)S(1)} %get-tuple-element.22), channel_id=1, source_target_pairs={{0,1},{1,2},{2,3},{3,4},{4,5},{5,6},{6,7},{8,9},{9,10},{10,11},{11... | collective-permute-start | bytes 98312 | tf_op jit(solution)/shard_map/ppermute | solution.py:14
  488.9 7.0 %collective-permute-start.63 = (f32[2,128]{1,0:T(2,128)S(1)}, f32[2,128]{1,0:T(2,128)S(1)}, u32[]{:S(2)}, u32[]{:S(2)}) collective-permute-start(f32[2,128]{1,0:T(2,128)S(1)} %fusion.74), channel_id=1, source_target_pairs={{0,4},{1,5},{2,6},{3,7},{4,0},{5,1},{6,2},{7,3},{8,12},{9,13},{10,... | collective-permute-start | bytes 3080 | tf_op jit(solution)/shard_map/ppermute | solution.py:31
  501.6 7.5 %collective-permute-start.65 = (f32[2,128]{1,0:T(2,128)S(1)}, f32[2,128]{1,0:T(2,128)S(1)}, u32[]{:S(2)}, u32[]{:S(2)}) collective-permute-start(f32[2,128]{1,0:T(2,128)S(1)} %add.295), channel_id=1, source_target_pairs={{0,16},{8,24},{16,0},{24,8},{32,48},{40,56},{48,32},{56,40},{64,80... | collective-permute-start | bytes 3080 | tf_op jit(solution)/shard_map/ppermute | solution.py:31
  509.1 7.5 %collective-permute-start.66 = (f32[2,128]{1,0:T(2,128)S(1)}, f32[2,128]{1,0:T(2,128)S(1)}, u32[]{:S(2)}, u32[]{:S(2)}) collective-permute-start(f32[2,128]{1,0:T(2,128)S(1)} %add.296), channel_id=1, source_target_pairs={{0,32},{8,40},{16,48},{24,56},{32,0},{40,8},{48,16},{56,24},{64,96... | collective-permute-start | bytes 3080 | tf_op jit(solution)/shard_map/ppermute | solution.py:31
  523.2 12.2 %collective-permute-start.68 = (f32[2,128]{1,0:T(2,128)S(1)}, f32[2,128]{1,0:T(2,128)S(1)}, u32[]{:S(2)}, u32[]{:S(2)}) collective-permute-start(f32[2,128]{1,0:T(2,128)S(1)} %add.298), channel_id=1, source_target_pairs={{0,128},{8,136},{16,144},{24,152},{32,160},{40,168},{48,176},{56,1... | collective-permute-start | bytes 3080 | tf_op jit(solution)/shard_map/ppermute | solution.py:31
  535.5 14.9 %collective-permute-start.69 = (f32[2,128]{1,0:T(2,128)S(1)}, f32[2,128]{1,0:T(2,128)S(1)}, u32[]{:S(2)}, u32[]{:S(2)}) collective-permute-start(f32[2,128]{1,0:T(2,128)S(1)} %add.299), channel_id=1, source_target_pairs={{0,256},{8,264},{16,272},{24,280},{32,288},{40,296},{48,304},{56,3... | collective-permute-start | bytes 3080 | tf_op jit(solution)/shard_map/ppermute | solution.py:31
  558.9 7.0 %collective-permute-start.72 = (f32[128]{0:T(128)S(1)}, f32[128]{0:T(128)S(1)}, u32[]{:S(2)}, u32[]{:S(2)}) collective-permute-start(f32[128]{0:T(128)S(1)} %add.303), channel_id=1, source_target_pairs={{0,4},{1,5},{2,6},{3,7},{4,0},{5,1},{6,2},{7,3},{8,12},{9,13},{10,... | collective-permute-start | bytes 1544 | tf_op jit(solution)/shard_map/ppermute | solution.py:31
  571.3 7.0 %collective-permute-start.74 = (f32[128]{0:T(128)S(1)}, f32[128]{0:T(128)S(1)}, u32[]{:S(2)}, u32[]{:S(2)}) collective-permute-start(f32[128]{0:T(128)S(1)} %add.305), channel_id=1, source_target_pairs={{0,16},{8,24},{16,0},{24,8},{32,48},{40,56},{48,32},{56,40},{64,80... | collective-permute-start | bytes 1544 | tf_op jit(solution)/shard_map/ppermute | solution.py:31
  590.1 9.4 %collective-permute-start.77 = (f32[128]{0:T(128)S(1)}, f32[128]{0:T(128)S(1)}, u32[]{:S(2)}, u32[]{:S(2)}) collective-permute-start(f32[128]{0:T(128)S(1)} %add.308), channel_id=1, source_target_pairs={{0,128},{8,136},{16,144},{24,152},{32,160},{40,168},{48,176},{56,1... | collective-permute-start | bytes 1544 | tf_op jit(solution)/shard_map/ppermute | solution.py:31
  599.5 14.2 %collective-permute-start.78 = (f32[128]{0:T(128)S(1)}, f32[128]{0:T(128)S(1)}, u32[]{:S(2)}, u32[]{:S(2)}) collective-permute-start(f32[128]{0:T(128)S(1)} %add.309), channel_id=1, source_target_pairs={{0,256},{8,264},{16,272},{24,280},{32,288},{40,296},{48,304},{56,3... | collective-permute-start | bytes 1544 | tf_op jit(solution)/shard_map/ppermute | solution.py:31
  (40 other events, 467.3 us)

commit v3 on v2

--- a/solution.py
+++ b/solution.py
@@ -5,6 +5,7 @@
 from jax.sharding import PartitionSpec as P
 
 EPSILON = 1e-06
+KEPT_SHARE = 1.0 / 64
 
 
 def neighbours(rows, axis):
@@ -150,6 +151,15 @@
     def column_norm(vector):
         return jnp.sqrt(allsum(jnp.sum(vector * vector, axis=0)) + EPSILON)
 
+    def guarded_norm(expanded, whole, remainder):
+        kept = jnp.all(jnp.isfinite(expanded) & (expanded >= KEPT_SHARE * whole))
+        return lax.cond(
+            kept,
+            lambda vector: jnp.sqrt(expanded + EPSILON),
+            column_norm,
+            remainder,
+        )
+
     rhs_margin = margin_of(right_side)
     scale_norm = column_norm(right_side)
     krylov_one = right_side / scale_norm
@@ -157,20 +167,47 @@
     precond_one = precondition(krylov_one.astype(jnp.bfloat16), margin_one.astype(jnp.bfloat16))
     applied = apply_operator(precond_one)
     applied_margin = margin_of(applied)
-    first_dot = allsum(jnp.sum(applied * krylov_one, axis=0))
+    sums = allsum(
+        jnp.stack(
+            [
+                jnp.sum(applied * krylov_one, axis=0),
+                jnp.sum(applied * applied, axis=0),
+                jnp.sum(krylov_one * krylov_one, axis=0),
+            ]
+        )
+    )
+    first_dot = sums[0]
     remainder = applied - first_dot * krylov_one
-    first_norm = column_norm(remainder)
+    expanded = sums[1] - 2.0 * first_dot * first_dot + first_dot * first_dot * sums[2]
+    first_norm = guarded_norm(expanded, sums[1], remainder)
     krylov_two = remainder / first_norm
     margin_two = (applied_margin - first_dot * margin_one) / first_norm
     precond_two = precondition(krylov_two.astype(jnp.bfloat16), margin_two.astype(jnp.bfloat16))
     applied = apply_operator(precond_two)
     dots = allsum(
-        jnp.stack([jnp.sum(applied * krylov_one, axis=0), jnp.sum(applied * krylov_two, axis=0)])
+        jnp.stack(
+            [
+                jnp.sum(applied * krylov_one, axis=0),
+                jnp.sum(applied * krylov_two, axis=0),
+                jnp.sum(applied * applied, axis=0),
+                jnp.sum(krylov_one * krylov_one, axis=0),
+                jnp.sum(krylov_one * krylov_two, axis=0),
+                jnp.sum(krylov_two * krylov_two, axis=0),
+            ]
+        )
     )
     cross_dot = dots[0]
     second_dot = dots[1]
     remainder = applied - cross_dot * krylov_one - second_dot * krylov_two
-    second_norm = column_norm(remainder)
+    expanded = (
+        dots[2]
+        - 2.0 * cross_dot * cross_dot
+        - 2.0 * second_dot * second_dot
+        + cross_dot * cross_dot * dots[3]
+        + 2.0 * cross_dot * second_dot * dots[4]
+        + second_dot * second_dot * dots[5]
+    )
+    second_norm = guarded_norm(expanded, dots[2], remainder)
     weight_one, weight_two, relative = least_squares(
         scale_norm, first_dot, first_norm, cross_dot, second_dot, second_norm
     )

time: 618 us -> 494 us (0.80)
  starting transfers between devices: 348 us -> 277 us
  waiting for transfers between devices: 215 us -> 160 us
    ppermute x45 -> x27, starting transfers between devices: 225 us -> 154 us  [allsum(): lax.ppermute(value, axis, [(i, i ^ step) for i in range(count)])]
    ppermute x45 -> x27, waiting for transfers between devices: 109 us -> 54.5 us  [allsum(): lax.ppermute(value, axis, [(i, i ^ step) for i in range(count)])]
  transfers between devices with their start and end apart: 79 -> 61, of which waited for: 65 -> 47; matrix products, arithmetic and copies ran while one was open for 4% -> 5% of each run, Pallas kernels for 0% -> 0%
where the time goes in v3:
time: 494 us; the launch traced here: 492 us
  starting transfers between devices  277 us (56%)
  waiting for transfers between devices  160 us (32%)
  local copies, waits for them, and re-layouts  25.9 us (5%)
  matrix products  13.2 us (3%)
  other arithmetic  12 us (2%)
    ppermute x27, starting transfers between devices, allsum(): lax.ppermute(value, axis, [(i, i ^ step) for i in range(count)])  154 us
    ppermute x18, waiting for transfers between devices, doubling_gather(): got = lax.ppermute(held, axis, [(i, i ^ step) for i in range(count)])  101 us
    ppermute x18, starting transfers between devices, doubling_gather(): got = lax.ppermute(held, axis, [(i, i ^ step) for i in range(count)])  79.3 us
    ppermute x27, waiting for transfers between devices, allsum(): lax.ppermute(value, axis, [(i, i ^ step) for i in range(count)])  54.5 us
    ppermute x16, starting transfers between devices, neighbours(): return (lax.ppermute(rows[1], axis, up), lax.ppermute(rows[0], axis, down))  43.9 us
    dot_general x2, matrix products, precondition(): jnp.dot(basis, solved.astype(jnp.bfloat16), preferred_element_type=jnp.fl...  10.4 us
  transfers between devices with their start and end apart: 61, of which 47 were waited for; matrix products, arithmetic and copies ran while one was open for 5% of the time, Pallas kernels for 0%

profile of v3, /device:TPU:6, one launch (start us, length us, event | category | flops | bytes accessed | tf_op | source)
XLA Modules:
  0.0 491.9 jit_solution(4478167914631724242)
XLA Ops:
  10.1 7.2 %collective-permute-start.20 = (f32[128]{0:T(128)S(1)}, f32[128]{0:T(128)S(1)}, u32[]{:S(2)}, u32[]{:S(2)}) collective-permute-start(f32[128]{0:T(128)S(1)} %add.270), channel_id=1, source_target_pairs={{0,4},{1,5},{2,6},{3,7},{4,0},{5,1},{6,2},{7,3},{8,12},{9,13},{10,... | collective-permute-start | bytes 1544 | tf_op jit(solution)/shard_map/ppermute | solution.py:32
  20.7 3.5 collective-permute-done.21
  27.6 3.6 collective-permute-done.22
  36.6 3.4 collective-permute-start.24
  43.0 7.7 %collective-permute-start.25 = (f32[128]{0:T(128)S(1)}, f32[128]{0:T(128)S(1)}, u32[]{:S(2)}, u32[]{:S(2)}) collective-permute-start(f32[128]{0:T(128)S(1)} %add.275), channel_id=1, source_target_pairs={{0,128},{8,136},{16,144},{24,152},{32,160},{40,168},{48,176},{56,1... | collective-permute-start | bytes 1544 | tf_op jit(solution)/shard_map/ppermute | solution.py:32
  52.4 14.0 %collective-permute-start.26 = (f32[128]{0:T(128)S(1)}, f32[128]{0:T(128)S(1)}, u32[]{:S(2)}, u32[]{:S(2)}) collective-permute-start(f32[128]{0:T(128)S(1)} %add.276), channel_id=1, source_target_pairs={{0,256},{8,264},{16,272},{24,280},{32,288},{40,296},{48,304},{56,3... | collective-permute-start | bytes 1544 | tf_op jit(solution)/shard_map/ppermute | solution.py:32
  68.9 12.6 %collective-permute-start.31 = (bf16[1,32,128]{2,1,0:T(8,128)(2,1)S(1)}, bf16[1,32,128]{2,1,0:T(8,128)(2,1)S(1)}, u32[]{:S(2)}, u32[]{:S(2)}) collective-permute-start(bf16[1,32,128]{2,1,0:T(8,128)(2,1)S(1)} %fusion.20), channel_id=1, source_target_pairs={{0,256},{8,264},{16,272},{24,280},{32,288},{40,296},{48,304},{56,3... | collective-permute-start | bytes 24584 | tf_op jit(solution)/shard_map/ppermute | solution.py:51
  83.1 6.4 %collective-permute-start.32 = (bf16[2,32,128]{2,1,0:T(8,128)(2,1)S(1)}, bf16[2,32,128]{2,1,0:T(8,128)(2,1)S(1)}, u32[]{:S(2)}, u32[]{:S(2)}) collective-permute-start(bf16[2,32,128]{2,1,0:T(8,128)(2,1)S(1)} %maximum_select_fusion.30), channel_id=1, source_target_pairs={{0,128},{8,136},{16,144},{24,152},{32,160},{40,168},{48,176},{56,1... | collective-permute-start | bytes 49160 | tf_op jit(solution)/shard_map/ppermute | solution.py:51
  92.8 3.4 collective-permute-start.33
  105.7 5.1 %collective-permute-start.35 = (bf16[16,32,128]{2,1,0:T(8,128)(2,1)S(1)}, bf16[16,32,128]{2,1,0:T(8,128)(2,1)S(1)}, u32[]{:S(2)}, u32[]{:S(2)}) collective-permute-start(bf16[16,32,128]{2,1,0:T(8,128)(2,1)S(1)} %maximum_select_fusion.24), channel_id=1, source_target_pairs={{0,16},{8,24},{16,0},{24,8},{32,48},{40,56},{48,32},{56,40},{64,80... | collective-permute-start | bytes 393224 | tf_op jit(solution)/shard_map/ppermute | solution.py:51
  114.0 3.5 collective-permute-start.36
  117.6 4.8 collective-permute-done.36
  122.4 4.1 collective-permute-start.37
  126.5 14.1 %collective-permute-done.37 = bf16[64,32,128]{2,1,0:T(8,128)(2,1)S(1)} collective-permute-done((bf16[64,32,128]{2,1,0:T(8,128)(2,1)S(1)}, bf16[64,32,128]{2,1,0:T(8,128)(2,1)S(1)}, u32[]{:S(2)}, u32[]{:S(2)}) %collective-permute-start.37) | collective-permute-done | bytes 524320 | tf_op jit(solution)/shard_map/ppermute | solution.py:51
  143.6 14.0 %collective-permute-done.38 = bf16[128,32,128]{2,1,0:T(8,128)(2,1)} collective-permute-done((bf16[128,32,128]{2,1,0:T(8,128)(2,1)S(1)}, bf16[128,32,128]{2,1,0:T(8,128)(2,1)}, u32[]{:S(2)}, u32[]{:S(2)}) %collective-permute-start.38) | collective-permute-done | bytes 1048608 | tf_op jit(solution)/shard_map/ppermute | solution.py:51
  171.0 5.2 %collective-permute-start.27 = (f32[128,128]{1,0:T(8,128)S(1)}, f32[128,128]{1,0:T(8,128)}, u32[]{:S(2)}, u32[]{:S(2)}) collective-permute-start(f32[128,128]{1,0:T(8,128)S(1)} %get-tuple-element.64), channel_id=1, source_target_pairs={{0,8},{8,16},{16,24},{24,32},{32,40},{40,48},{48,56},{56,64},{64,7... | collective-permute-start | bytes 196616 | tf_op jit(solution)/shard_map/ppermute | solution.py:15
  176.2 4.4 reshape_squeeze.7
  180.6 3.5 copy.16
  184.2 3.5 gather_fusion.1
  188.7 6.4 %copy.20 = bf16[32,512,32]{2,0,1:T(8,128)(2,1)} copy(bf16[32,512,32]{1,2,0:T(8,128)(2,1)S(1)} %convert_bitcast_fusion) | data formatting | bytes 2097152 | tf_op jit(solution)/shard_map/convert_element_type | solution.py:116
  196.5 5.2 %convolution_add_fusion.1 = f32[128,128]{1,0:T(8,128)S(1)} fusion(f32[128,128]{1,0:T(8,128)S(1)} %fusion.28, bf16[32,512,32]{2,0,1:T(8,128)(2,1)} %copy.20, bf16[256,32,128]{2,1,0:T(8,128)(2,1)S(1)} %maximum_select_fusion.4, bf16[256,32,128]{2,1,0:T(8,128)(2,1)} %collective-permute-done.39, pred[]{:T(512)S(6)} %eq.71, bf16[1,1,128,32]{2,3,1,0:T(8,128)(2,1)S(1)} %copy-done.7), kind=kOutput, calls=%fused_computation.32 | convolution fusion | flops 141578240 | bytes 5382145 | tf_op jit(solution)/shard_map/dot_general | solution.py:131
  209.4 4.5 collective-permute-start.40
  226.7 4.8 collective-permute-start.46
  233.7 4.2 collective-permute-start.47
  239.5 7.3 %collective-permute-start.48 = (f32[3,128]{1,0:T(4,128)S(1)}, f32[3,128]{1,0:T(4,128)S(1)}, u32[]{:S(2)}, u32[]{:S(2)}) collective-permute-start(f32[3,128]{1,0:T(4,128)S(1)} %add.296), channel_id=1, source_target_pairs={{0,16},{8,24},{16,0},{24,8},{32,48},{40,56},{48,32},{56,40},{64,80... | collective-permute-start | bytes 4616 | tf_op jit(solution)/shard_map/ppermute | solution.py:32
  248.3 7.7 %collective-permute-start.49 = (f32[3,128]{1,0:T(4,128)S(1)}, f32[3,128]{1,0:T(4,128)S(1)}, u32[]{:S(2)}, u32[]{:S(2)}) collective-permute-start(f32[3,128]{1,0:T(4,128)S(1)} %add.297), channel_id=1, source_target_pairs={{0,32},{8,40},{16,48},{24,56},{32,0},{40,8},{48,16},{56,24},{64,96... | collective-permute-start | bytes 4616 | tf_op jit(solution)/shard_map/ppermute | solution.py:32
  257.6 4.4 collective-permute-start.50
  264.0 10.1 %collective-permute-start.51 = (f32[3,128]{1,0:T(4,128)S(1)}, f32[3,128]{1,0:T(4,128)S(1)}, u32[]{:S(2)}, u32[]{:S(2)}) collective-permute-start(f32[3,128]{1,0:T(4,128)S(1)} %add.299), channel_id=1, source_target_pairs={{0,128},{8,136},{16,144},{24,152},{32,160},{40,168},{48,176},{56,1... | collective-permute-start | bytes 4616 | tf_op jit(solution)/shard_map/ppermute | solution.py:32
  275.6 12.9 %collective-permute-start.52 = (f32[3,128]{1,0:T(4,128)S(1)}, f32[3,128]{1,0:T(4,128)S(1)}, u32[]{:S(2)}, u32[]{:S(2)}) collective-permute-start(f32[3,128]{1,0:T(4,128)S(1)} %add.300), channel_id=1, source_target_pairs={{0,256},{8,264},{16,272},{24,280},{32,288},{40,296},{48,304},{56,3... | collective-permute-start | bytes 4616 | tf_op jit(solution)/shard_map/ppermute | solution.py:32
  291.8 12.6 %collective-permute-start.57 = (bf16[1,32,128]{2,1,0:T(8,128)(2,1)S(1)}, bf16[1,32,128]{2,1,0:T(8,128)(2,1)S(1)}, u32[]{:S(2)}, u32[]{:S(2)}) collective-permute-start(bf16[1,32,128]{2,1,0:T(8,128)(2,1)S(1)} %fusion.21), channel_id=1, source_target_pairs={{0,256},{8,264},{16,272},{24,280},{32,288},{40,296},{48,304},{56,3... | collective-permute-start | bytes 24584 | tf_op jit(solution)/shard_map/ppermute | solution.py:51
  306.0 7.5 %collective-permute-start.58 = (bf16[2,32,128]{2,1,0:T(8,128)(2,1)S(1)}, bf16[2,32,128]{2,1,0:T(8,128)(2,1)S(1)}, u32[]{:S(2)}, u32[]{:S(2)}) collective-permute-start(bf16[2,32,128]{2,1,0:T(8,128)(2,1)S(1)} %maximum_select_fusion.31), channel_id=1, source_target_pairs={{0,128},{8,136},{16,144},{24,152},{32,160},{40,168},{48,176},{56,1... | collective-permute-start | bytes 49160 | tf_op jit(solution)/shard_map/ppermute | solution.py:51
  317.8 4.8 collective-permute-done.59
  324.5 4.2 collective-permute-done.60
  330.6 6.4 %collective-permute-done.61 = bf16[16,32,128]{2,1,0:T(8,128)(2,1)S(1)} collective-permute-done((bf16[16,32,128]{2,1,0:T(8,128)(2,1)S(1)}, bf16[16,32,128]{2,1,0:T(8,128)(2,1)S(1)}, u32[]{:S(2)}, u32[]{:S(2)}) %collective-permute-start.61) | collective-permute-done | bytes 131104 | tf_op jit(solution)/shard_map/ppermute | solution.py:51
  339.1 6.3 %collective-permute-done.62 = bf16[32,32,128]{2,1,0:T(8,128)(2,1)S(1)} collective-permute-done((bf16[32,32,128]{2,1,0:T(8,128)(2,1)S(1)}, bf16[32,32,128]{2,1,0:T(8,128)(2,1)S(1)}, u32[]{:S(2)}, u32[]{:S(2)}) %collective-permute-start.62) | collective-permute-done | bytes 262176 | tf_op jit(solution)/shard_map/ppermute | solution.py:51
  345.5 3.8 collective-permute-start.63
  349.3 14.1 %collective-permute-done.63 = bf16[64,32,128]{2,1,0:T(8,128)(2,1)S(1)} collective-permute-done((bf16[64,32,128]{2,1,0:T(8,128)(2,1)S(1)}, bf16[64,32,128]{2,1,0:T(8,128)(2,1)S(1)}, u32[]{:S(2)}, u32[]{:S(2)}) %collective-permute-start.63) | collective-permute-done | bytes 524320 | tf_op jit(solution)/shard_map/ppermute | solution.py:51
  366.5 13.8 %collective-permute-done.64 = bf16[128,32,128]{2,1,0:T(8,128)(2,1)S(1)} collective-permute-done((bf16[128,32,128]{2,1,0:T(8,128)(2,1)S(1)}, bf16[128,32,128]{2,1,0:T(8,128)(2,1)S(1)}, u32[]{:S(2)}, u32[]{:S(2)}) %collective-permute-start.64) | collective-permute-done | bytes 1048608 | tf_op jit(solution)/shard_map/ppermute | solution.py:51
  389.9 4.5 collective-permute-start.53
  396.6 5.2 %convolution_add_fusion = f32[128,128]{1,0:T(8,128)S(1)} fusion(f32[128,128]{1,0:T(8,128)S(1)} %fusion.32, bf16[32,512,32]{2,0,1:T(8,128)(2,1)} %copy.20, bf16[256,32,128]{2,1,0:T(8,128)(2,1)S(1)} %maximum_select_fusion.5, bf16[256,32,128]{2,1,0:T(8,128)(2,1)} %collective-permute-done.65, pred[]{:T(512)S(6)} %eq.71, bf16[1,1,128,32]{2,3,1,0:T(8,128)(2,1)S(1)} %copy-done.7), kind=kOutput, calls=%fused_computation.29 | convolution fusion | flops 141578240 | bytes 5382145 | tf_op jit(solution)/shard_map/dot_general | solution.py:131
  409.4 5.0 %collective-permute-start.66 = (bf16[128,128]{1,0:T(8,128)(2,1)S(1)}, bf16[128,128]{1,0:T(8,128)(2,1)S(1)}, u32[]{:S(2)}, u32[]{:S(2)}) collective-permute-start(bf16[128,128]{1,0:T(8,128)(2,1)S(1)} %get-tuple-element.68), channel_id=1, source_target_pairs={{0,8},{8,16},{16,24},{24,32},{32,40},{40,48},{48,56},{56,64},{64,7... | collective-permute-start | bytes 98312 | tf_op jit(solution)/shard_map/ppermute | solution.py:15
  430.6 3.6 collective-permute-done.72
  434.2 4.2 collective-permute-start.73
  440.0 6.0 %collective-permute-start.74 = (f32[6,128]{1,0:T(8,128)S(1)}, f32[6,128]{1,0:T(8,128)S(1)}, u32[]{:S(2)}, u32[]{:S(2)}) collective-permute-start(f32[6,128]{1,0:T(8,128)S(1)} %add.309), channel_id=1, source_target_pairs={{0,16},{8,24},{16,0},{24,8},{32,48},{40,56},{48,32},{56,40},{64,80... | collective-permute-start | bytes 9224 | tf_op jit(solution)/shard_map/ppermute | solution.py:32
  447.6 6.1 %collective-permute-start.75 = (f32[6,128]{1,0:T(8,128)S(1)}, f32[6,128]{1,0:T(8,128)S(1)}, u32[]{:S(2)}, u32[]{:S(2)}) collective-permute-start(f32[6,128]{1,0:T(8,128)S(1)} %add.310), channel_id=1, source_target_pairs={{0,32},{8,40},{16,48},{24,56},{32,0},{40,8},{48,16},{56,24},{64,96... | collective-permute-start | bytes 9224 | tf_op jit(solution)/shard_map/ppermute | solution.py:32
  455.3 4.6 collective-permute-start.76
  461.7 10.7 %collective-permute-start.77 = (f32[6,128]{1,0:T(8,128)S(1)}, f32[6,128]{1,0:T(8,128)S(1)}, u32[]{:S(2)}, u32[]{:S(2)}) collective-permute-start(f32[6,128]{1,0:T(8,128)S(1)} %add.312), channel_id=1, source_target_pairs={{0,128},{8,136},{16,144},{24,152},{32,160},{40,168},{48,176},{56,1... | collective-permute-start | bytes 9224 | tf_op jit(solution)/shard_map/ppermute | solution.py:32
  473.9 13.6 %collective-permute-start.78 = (f32[6,128]{1,0:T(8,128)S(1)}, f32[6,128]{1,0:T(8,128)S(1)}, u32[]{:S(2)}, u32[]{:S(2)}) collective-permute-start(f32[6,128]{1,0:T(8,128)S(1)} %add.313), channel_id=1, source_target_pairs={{0,256},{8,264},{16,272},{24,280},{32,288},{40,296},{48,304},{56,3... | collective-permute-start | bytes 9224 | tf_op jit(solution)/shard_map/ppermute | solution.py:32
  (190 shorter events, 160.0 us)
Async XLA Ops:
  10.1 8.7 %collective-permute-start.20 = (f32[128]{0:T(128)S(1)}, f32[128]{0:T(128)S(1)}, u32[]{:S(2)}, u32[]{:S(2)}) collective-permute-start(f32[128]{0:T(128)S(1)} %add.270), channel_id=1, source_target_pairs={{0,4},{1,5},{2,6},{3,7},{4,0},{5,1},{6,2},{7,3},{8,12},{9,13},{10,... | collective-permute-start | bytes 1544 | tf_op jit(solution)/shard_map/ppermute | solution.py:32
  24.2 7.0 %collective-permute-start.22 = (f32[128]{0:T(128)S(1)}, f32[128]{0:T(128)S(1)}, u32[]{:S(2)}, u32[]{:S(2)}) collective-permute-start(f32[128]{0:T(128)S(1)} %add.272), channel_id=1, source_target_pairs={{0,16},{8,24},{16,0},{24,8},{32,48},{40,56},{48,32},{56,40},{64,80... | collective-permute-start | bytes 1544 | tf_op jit(solution)/shard_map/ppermute | solution.py:32
  36.6 6.3 %collective-permute-start.24 = (f32[128]{0:T(128)S(1)}, f32[128]{0:T(128)S(1)}, u32[]{:S(2)}, u32[]{:S(2)}) collective-permute-start(f32[128]{0:T(128)S(1)} %add.274), channel_id=1, source_target_pairs={{0,64},{8,72},{16,80},{24,88},{32,96},{40,104},{48,112},{56,120},{... | collective-permute-start | bytes 1544 | tf_op jit(solution)/shard_map/ppermute | solution.py:32
  43.0 9.4 %collective-permute-start.25 = (f32[128]{0:T(128)S(1)}, f32[128]{0:T(128)S(1)}, u32[]{:S(2)}, u32[]{:S(2)}) collective-permute-start(f32[128]{0:T(128)S(1)} %add.275), channel_id=1, source_target_pairs={{0,128},{8,136},{16,144},{24,152},{32,160},{40,168},{48,176},{56,1... | collective-permute-start | bytes 1544 | tf_op jit(solution)/shard_map/ppermute | solution.py:32
  52.4 15.5 %collective-permute-start.26 = (f32[128]{0:T(128)S(1)}, f32[128]{0:T(128)S(1)}, u32[]{:S(2)}, u32[]{:S(2)}) collective-permute-start(f32[128]{0:T(128)S(1)} %add.276), channel_id=1, source_target_pairs={{0,256},{8,264},{16,272},{24,280},{32,288},{40,296},{48,304},{56,3... | collective-permute-start | bytes 1544 | tf_op jit(solution)/shard_map/ppermute | solution.py:32
  68.9 14.3 %collective-permute-start.31 = (bf16[1,32,128]{2,1,0:T(8,128)(2,1)S(1)}, bf16[1,32,128]{2,1,0:T(8,128)(2,1)S(1)}, u32[]{:S(2)}, u32[]{:S(2)}) collective-permute-start(bf16[1,32,128]{2,1,0:T(8,128)(2,1)S(1)} %fusion.20), channel_id=1, source_target_pairs={{0,256},{8,264},{16,272},{24,280},{32,288},{40,296},{48,304},{56,3... | collective-permute-start | bytes 24584 | tf_op jit(solution)/shard_map/ppermute | solution.py:51
  83.1 9.6 %collective-permute-start.32 = (bf16[2,32,128]{2,1,0:T(8,128)(2,1)S(1)}, bf16[2,32,128]{2,1,0:T(8,128)(2,1)S(1)}, u32[]{:S(2)}, u32[]{:S(2)}) collective-permute-start(bf16[2,32,128]{2,1,0:T(8,128)(2,1)S(1)} %maximum_select_fusion.30), channel_id=1, source_target_pairs={{0,128},{8,136},{16,144},{24,152},{32,160},{40,168},{48,176},{56,1... | collective-permute-start | bytes 49160 | tf_op jit(solution)/shard_map/ppermute | solution.py:51
  92.8 6.7 %collective-permute-start.33 = (bf16[4,32,128]{2,1,0:T(8,128)(2,1)S(1)}, bf16[4,32,128]{2,1,0:T(8,128)(2,1)S(1)}, u32[]{:S(2)}, u32[]{:S(2)}) collective-permute-start(bf16[4,32,128]{2,1,0:T(8,128)(2,1)S(1)} %maximum_select_fusion.28), channel_id=1, source_target_pairs={{0,64},{8,72},{16,80},{24,88},{32,96},{40,104},{48,112},{56,120},{... | collective-permute-start | bytes 98312 | tf_op jit(solution)/shard_map/ppermute | solution.py:51
  99.5 6.2 %collective-permute-start.34 = (bf16[8,32,128]{2,1,0:T(8,128)(2,1)S(1)}, bf16[8,32,128]{2,1,0:T(8,128)(2,1)S(1)}, u32[]{:S(2)}, u32[]{:S(2)}) collective-permute-start(bf16[8,32,128]{2,1,0:T(8,128)(2,1)S(1)} %maximum_select_fusion.26), channel_id=1, source_target_pairs={{0,32},{8,40},{16,48},{24,56},{32,0},{40,8},{48,16},{56,24},{64,96... | collective-permute-start | bytes 196616 | tf_op jit(solution)/shard_map/ppermute | solution.py:51
  105.7 8.4 %collective-permute-start.35 = (bf16[16,32,128]{2,1,0:T(8,128)(2,1)S(1)}, bf16[16,32,128]{2,1,0:T(8,128)(2,1)S(1)}, u32[]{:S(2)}, u32[]{:S(2)}) collective-permute-start(bf16[16,32,128]{2,1,0:T(8,128)(2,1)S(1)} %maximum_select_fusion.24), channel_id=1, source_target_pairs={{0,16},{8,24},{16,0},{24,8},{32,48},{40,56},{48,32},{56,40},{64,80... | collective-permute-start | bytes 393224 | tf_op jit(solution)/shard_map/ppermute | solution.py:51
  114.0 8.3 %collective-permute-start.36 = (bf16[32,32,128]{2,1,0:T(8,128)(2,1)S(1)}, bf16[32,32,128]{2,1,0:T(8,128)(2,1)S(1)}, u32[]{:S(2)}, u32[]{:S(2)}) collective-permute-start(bf16[32,32,128]{2,1,0:T(8,128)(2,1)S(1)} %maximum_select_fusion.22), channel_id=1, source_target_pairs={{0,8},{8,0},{16,24},{24,16},{32,40},{40,32},{48,56},{56,48},{64,72... | collective-permute-start | bytes 786440 | tf_op jit(solution)/shard_map/ppermute | solution.py:51
  122.4 18.2 %collective-permute-start.37 = (bf16[64,32,128]{2,1,0:T(8,128)(2,1)S(1)}, bf16[64,32,128]{2,1,0:T(8,128)(2,1)S(1)}, u32[]{:S(2)}, u32[]{:S(2)}) collective-permute-start(bf16[64,32,128]{2,1,0:T(8,128)(2,1)S(1)} %maximum_select_fusion.20), channel_id=1, source_target_pairs={{0,4},{1,5},{2,6},{3,7},{4,0},{5,1},{6,2},{7,3},{8,12},{9,13},{10,... | collective-permute-start | bytes 1572872 | tf_op jit(solution)/shard_map/ppermute | solution.py:51
  140.8 16.8 %collective-permute-start.38 = (bf16[128,32,128]{2,1,0:T(8,128)(2,1)S(1)}, bf16[128,32,128]{2,1,0:T(8,128)(2,1)}, u32[]{:S(2)}, u32[]{:S(2)}) collective-permute-start(bf16[128,32,128]{2,1,0:T(8,128)(2,1)S(1)} %maximum_select_fusion.18), channel_id=1, source_target_pairs={{0,2},{1,3},{2,0},{3,1},{4,6},{5,7},{6,4},{7,5},{8,10},{9,11},{10,... | collective-permute-start | bytes 3145736 | tf_op jit(solution)/shard_map/ppermute | solution.py:51
  159.5 37.0 %collective-permute-start.39 = (bf16[256,32,128]{2,1,0:T(8,128)(2,1)S(1)}, bf16[256,32,128]{2,1,0:T(8,128)(2,1)}, u32[]{:S(2)}, u32[]{:S(2)}) collective-permute-start(bf16[256,32,128]{2,1,0:T(8,128)(2,1)S(1)} %maximum_select_fusion.4), channel_id=1, source_target_pairs={{0,1},{1,0},{2,3},{3,2},{4,5},{5,4},{6,7},{7,6},{8,9},{9,8},{10,11... | collective-permute-start | bytes 6291464 | tf_op jit(solution)/shard_map/ppermute | solution.py:51
  164.8 30.4 %collective-permute-start.30 = (f32[128,128]{1,0:T(8,128)}, f32[128,128]{1,0:T(8,128)}, u32[]{:S(2)}, u32[]{:S(2)}) collective-permute-start(f32[128,128]{1,0:T(8,128)} %get-tuple-element.67), channel_id=1, source_target_pairs={{1,0},{2,1},{3,2},{4,3},{5,4},{6,5},{7,6},{9,8},{10,9},{11,10},{12... | collective-permute-start | bytes 196616 | tf_op jit(solution)/shard_map/ppermute | solution.py:15
  167.7 27.5 %collective-permute-start.29 = (f32[128,128]{1,0:T(8,128)}, f32[128,128]{1,0:T(8,128)}, u32[]{:S(2)}, u32[]{:S(2)}) collective-permute-start(f32[128,128]{1,0:T(8,128)} %get-tuple-element.65), channel_id=1, source_target_pairs={{0,1},{1,2},{2,3},{3,4},{4,5},{5,6},{6,7},{8,9},{9,10},{10,11},{11... | collective-permute-start | bytes 196616 | tf_op jit(solution)/shard_map/ppermute | solution.py:15
  169.7 25.4 %collective-permute-start.28 = (f32[128,128]{1,0:T(8,128)}, f32[128,128]{1,0:T(8,128)}, u32[]{:S(2)}, u32[]{:S(2)}) collective-permute-start(f32[128,128]{1,0:T(8,128)} %get-tuple-element.66), channel_id=1, source_target_pairs={{8,0},{16,8},{24,16},{32,24},{40,32},{48,40},{56,48},{64,56},{72,6... | collective-permute-start | bytes 196616 | tf_op jit(solution)/shard_map/ppermute | solution.py:15
  171.0 24.2 %collective-permute-start.27 = (f32[128,128]{1,0:T(8,128)S(1)}, f32[128,128]{1,0:T(8,128)}, u32[]{:S(2)}, u32[]{:S(2)}) collective-permute-start(f32[128,128]{1,0:T(8,128)S(1)} %get-tuple-element.64), channel_id=1, source_target_pairs={{0,8},{8,16},{16,24},{24,32},{32,40},{40,48},{48,56},{56,64},{64,7... | collective-permute-start | bytes 196616 | tf_op jit(solution)/shard_map/ppermute | solution.py:15
  203.2 10.7 %collective-permute-start.43 = (bf16[128,128]{1,0:T(8,128)(2,1)S(1)}, bf16[128,128]{1,0:T(8,128)(2,1)S(1)}, u32[]{:S(2)}, u32[]{:S(2)}) collective-permute-start(bf16[128,128]{1,0:T(8,128)(2,1)S(1)} %get-tuple-element.75), channel_id=1, source_target_pairs={{1,0},{2,1},{3,2},{4,3},{5,4},{6,5},{7,6},{9,8},{10,9},{11,10},{12... | collective-permute-start | bytes 98312 | tf_op jit(solution)/shard_map/ppermute | solution.py:15
  206.2 7.8 %collective-permute-start.42 = (bf16[128,128]{1,0:T(8,128)(2,1)S(1)}, bf16[128,128]{1,0:T(8,128)(2,1)S(1)}, u32[]{:S(2)}, u32[]{:S(2)}) collective-permute-start(bf16[128,128]{1,0:T(8,128)(2,1)S(1)} %get-tuple-element.73), channel_id=1, source_target_pairs={{0,1},{1,2},{2,3},{3,4},{4,5},{5,6},{6,7},{8,9},{9,10},{10,11},{11... | collective-permute-start | bytes 98312 | tf_op jit(solution)/shard_map/ppermute | solution.py:15
  226.7 7.0 %collective-permute-start.46 = (f32[3,128]{1,0:T(4,128)S(1)}, f32[3,128]{1,0:T(4,128)S(1)}, u32[]{:S(2)}, u32[]{:S(2)}) collective-permute-start(f32[3,128]{1,0:T(4,128)S(1)} %fusion.84), channel_id=1, source_target_pairs={{0,4},{1,5},{2,6},{3,7},{4,0},{5,1},{6,2},{7,3},{8,12},{9,13},{10,... | collective-permute-start | bytes 4616 | tf_op jit(solution)/shard_map/ppermute | solution.py:32
  239.5 8.8 %collective-permute-start.48 = (f32[3,128]{1,0:T(4,128)S(1)}, f32[3,128]{1,0:T(4,128)S(1)}, u32[]{:S(2)}, u32[]{:S(2)}) collective-permute-start(f32[3,128]{1,0:T(4,128)S(1)} %add.296), channel_id=1, source_target_pairs={{0,16},{8,24},{16,0},{24,8},{32,48},{40,56},{48,32},{56,40},{64,80... | collective-permute-start | bytes 4616 | tf_op jit(solution)/shard_map/ppermute | solution.py:32
  248.3 9.3 %collective-permute-start.49 = (f32[3,128]{1,0:T(4,128)S(1)}, f32[3,128]{1,0:T(4,128)S(1)}, u32[]{:S(2)}, u32[]{:S(2)}) collective-permute-start(f32[3,128]{1,0:T(4,128)S(1)} %add.297), channel_id=1, source_target_pairs={{0,32},{8,40},{16,48},{24,56},{32,0},{40,8},{48,16},{56,24},{64,96... | collective-permute-start | bytes 4616 | tf_op jit(solution)/shard_map/ppermute | solution.py:32
  257.6 6.4 %collective-permute-start.50 = (f32[3,128]{1,0:T(4,128)S(1)}, f32[3,128]{1,0:T(4,128)S(1)}, u32[]{:S(2)}, u32[]{:S(2)}) collective-permute-start(f32[3,128]{1,0:T(4,128)S(1)} %add.298), channel_id=1, source_target_pairs={{0,64},{8,72},{16,80},{24,88},{32,96},{40,104},{48,112},{56,120},{... | collective-permute-start | bytes 4616 | tf_op jit(solution)/shard_map/ppermute | solution.py:32
  264.0 11.7 %collective-permute-start.51 = (f32[3,128]{1,0:T(4,128)S(1)}, f32[3,128]{1,0:T(4,128)S(1)}, u32[]{:S(2)}, u32[]{:S(2)}) collective-permute-start(f32[3,128]{1,0:T(4,128)S(1)} %add.299), channel_id=1, source_target_pairs={{0,128},{8,136},{16,144},{24,152},{32,160},{40,168},{48,176},{56,1... | collective-permute-start | bytes 4616 | tf_op jit(solution)/shard_map/ppermute | solution.py:32
  275.6 14.5 %collective-permute-start.52 = (f32[3,128]{1,0:T(4,128)S(1)}, f32[3,128]{1,0:T(4,128)S(1)}, u32[]{:S(2)}, u32[]{:S(2)}) collective-permute-start(f32[3,128]{1,0:T(4,128)S(1)} %add.300), channel_id=1, source_target_pairs={{0,256},{8,264},{16,272},{24,280},{32,288},{40,296},{48,304},{56,3... | collective-permute-start | bytes 4616 | tf_op jit(solution)/shard_map/ppermute | solution.py:32
  291.8 14.3 %collective-permute-start.57 = (bf16[1,32,128]{2,1,0:T(8,128)(2,1)S(1)}, bf16[1,32,128]{2,1,0:T(8,128)(2,1)S(1)}, u32[]{:S(2)}, u32[]{:S(2)}) collective-permute-start(bf16[1,32,128]{2,1,0:T(8,128)(2,1)S(1)} %fusion.21), channel_id=1, source_target_pairs={{0,256},{8,264},{16,272},{24,280},{32,288},{40,296},{48,304},{56,3... | collective-permute-start | bytes 24584 | tf_op jit(solution)/shard_map/ppermute | solution.py:51
  306.0 9.8 %collective-permute-start.58 = (bf16[2,32,128]{2,1,0:T(8,128)(2,1)S(1)}, bf16[2,32,128]{2,1,0:T(8,128)(2,1)S(1)}, u32[]{:S(2)}, u32[]{:S(2)}) collective-permute-start(bf16[2,32,128]{2,1,0:T(8,128)(2,1)S(1)} %maximum_select_fusion.31), channel_id=1, source_target_pairs={{0,128},{8,136},{16,144},{24,152},{32,160},{40,168},{48,176},{56,1... | collective-permute-start | bytes 49160 | tf_op jit(solution)/shard_map/ppermute | solution.py:51
  315.8 6.7 %collective-permute-start.59 = (bf16[4,32,128]{2,1,0:T(8,128)(2,1)S(1)}, bf16[4,32,128]{2,1,0:T(8,128)(2,1)S(1)}, u32[]{:S(2)}, u32[]{:S(2)}) collective-permute-start(bf16[4,32,128]{2,1,0:T(8,128)(2,1)S(1)} %maximum_select_fusion.29), channel_id=1, source_target_pairs={{0,64},{8,72},{16,80},{24,88},{32,96},{40,104},{48,112},{56,120},{... | collective-permute-start | bytes 98312 | tf_op jit(solution)/shard_map/ppermute | solution.py:51
  328.7 8.4 %collective-permute-start.61 = (bf16[16,32,128]{2,1,0:T(8,128)(2,1)S(1)}, bf16[16,32,128]{2,1,0:T(8,128)(2,1)S(1)}, u32[]{:S(2)}, u32[]{:S(2)}) collective-permute-start(bf16[16,32,128]{2,1,0:T(8,128)(2,1)S(1)} %maximum_select_fusion.25), channel_id=1, source_target_pairs={{0,16},{8,24},{16,0},{24,8},{32,48},{40,56},{48,32},{56,40},{64,80... | collective-permute-start | bytes 393224 | tf_op jit(solution)/shard_map/ppermute | solution.py:51
  337.1 8.3 %collective-permute-start.62 = (bf16[32,32,128]{2,1,0:T(8,128)(2,1)S(1)}, bf16[32,32,128]{2,1,0:T(8,128)(2,1)S(1)}, u32[]{:S(2)}, u32[]{:S(2)}) collective-permute-start(bf16[32,32,128]{2,1,0:T(8,128)(2,1)S(1)} %maximum_select_fusion.23), channel_id=1, source_target_pairs={{0,8},{8,0},{16,24},{24,16},{32,40},{40,32},{48,56},{56,48},{64,72... | collective-permute-start | bytes 786440 | tf_op jit(solution)/shard_map/ppermute | solution.py:51
  345.5 18.0 %collective-permute-start.63 = (bf16[64,32,128]{2,1,0:T(8,128)(2,1)S(1)}, bf16[64,32,128]{2,1,0:T(8,128)(2,1)S(1)}, u32[]{:S(2)}, u32[]{:S(2)}) collective-permute-start(bf16[64,32,128]{2,1,0:T(8,128)(2,1)S(1)} %maximum_select_fusion.21), channel_id=1, source_target_pairs={{0,4},{1,5},{2,6},{3,7},{4,0},{5,1},{6,2},{7,3},{8,12},{9,13},{10,... | collective-permute-start | bytes 1572872 | tf_op jit(solution)/shard_map/ppermute | solution.py:51
  363.6 16.7 %collective-permute-start.64 = (bf16[128,32,128]{2,1,0:T(8,128)(2,1)S(1)}, bf16[128,32,128]{2,1,0:T(8,128)(2,1)S(1)}, u32[]{:S(2)}, u32[]{:S(2)}) collective-permute-start(bf16[128,32,128]{2,1,0:T(8,128)(2,1)S(1)} %maximum_select_fusion.19), channel_id=1, source_target_pairs={{0,2},{1,3},{2,0},{3,1},{4,6},{5,7},{6,4},{7,5},{8,10},{9,11},{10,... | collective-permute-start | bytes 3145736 | tf_op jit(solution)/shard_map/ppermute | solution.py:51
  380.6 16.0 %collective-permute-start.65 = (bf16[256,32,128]{2,1,0:T(8,128)(2,1)S(1)}, bf16[256,32,128]{2,1,0:T(8,128)(2,1)}, u32[]{:S(2)}, u32[]{:S(2)}) collective-permute-start(bf16[256,32,128]{2,1,0:T(8,128)(2,1)S(1)} %maximum_select_fusion.5), channel_id=1, source_target_pairs={{0,1},{1,0},{2,3},{3,2},{4,5},{5,4},{6,7},{7,6},{8,9},{9,8},{10,11... | collective-permute-start | bytes 6291464 | tf_op jit(solution)/shard_map/ppermute | solution.py:51
  383.6 10.8 %collective-permute-start.56 = (f32[128,128]{1,0:T(8,128)S(1)}, f32[128,128]{1,0:T(8,128)S(1)}, u32[]{:S(2)}, u32[]{:S(2)}) collective-permute-start(f32[128,128]{1,0:T(8,128)S(1)} %get-tuple-element.63), channel_id=1, source_target_pairs={{1,0},{2,1},{3,2},{4,3},{5,4},{6,5},{7,6},{9,8},{10,9},{11,10},{12... | collective-permute-start | bytes 196616 | tf_op jit(solution)/shard_map/ppermute | solution.py:15
  386.6 7.8 %collective-permute-start.55 = (f32[128,128]{1,0:T(8,128)S(1)}, f32[128,128]{1,0:T(8,128)S(1)}, u32[]{:S(2)}, u32[]{:S(2)}) collective-permute-start(f32[128,128]{1,0:T(8,128)S(1)} %get-tuple-element.61), channel_id=1, source_target_pairs={{0,1},{1,2},{2,3},{3,4},{4,5},{5,6},{6,7},{8,9},{9,10},{10,11},{11... | collective-permute-start | bytes 196616 | tf_op jit(solution)/shard_map/ppermute | solution.py:15
  388.6 6.2 %collective-permute-start.54 = (f32[128,128]{1,0:T(8,128)S(1)}, f32[128,128]{1,0:T(8,128)S(1)}, u32[]{:S(2)}, u32[]{:S(2)}) collective-permute-start(f32[128,128]{1,0:T(8,128)S(1)} %get-tuple-element.62), channel_id=1, source_target_pairs={{8,0},{16,8},{24,16},{32,24},{40,32},{48,40},{56,48},{64,56},{72,6... | collective-permute-start | bytes 196616 | tf_op jit(solution)/shard_map/ppermute | solution.py:15
  389.9 6.4 %collective-permute-start.53 = (f32[128,128]{1,0:T(8,128)S(1)}, f32[128,128]{1,0:T(8,128)S(1)}, u32[]{:S(2)}, u32[]{:S(2)}) collective-permute-start(f32[128,128]{1,0:T(8,128)S(1)} %get-tuple-element.60), channel_id=1, source_target_pairs={{0,8},{8,16},{16,24},{24,32},{32,40},{40,48},{48,56},{56,64},{64,7... | collective-permute-start | bytes 196616 | tf_op jit(solution)/shard_map/ppermute | solution.py:15
  403.3 11.1 %collective-permute-start.69 = (bf16[128,128]{1,0:T(8,128)(2,1)S(1)}, bf16[128,128]{1,0:T(8,128)(2,1)S(1)}, u32[]{:S(2)}, u32[]{:S(2)}) collective-permute-start(bf16[128,128]{1,0:T(8,128)(2,1)S(1)} %get-tuple-element.71), channel_id=1, source_target_pairs={{1,0},{2,1},{3,2},{4,3},{5,4},{6,5},{7,6},{9,8},{10,9},{11,10},{12... | collective-permute-start | bytes 98312 | tf_op jit(solution)/shard_map/ppermute | solution.py:15
  406.2 8.3 %collective-permute-start.68 = (bf16[128,128]{1,0:T(8,128)(2,1)S(1)}, bf16[128,128]{1,0:T(8,128)(2,1)S(1)}, u32[]{:S(2)}, u32[]{:S(2)}) collective-permute-start(bf16[128,128]{1,0:T(8,128)(2,1)S(1)} %get-tuple-element.69), channel_id=1, source_target_pairs={{0,1},{1,2},{2,3},{3,4},{4,5},{5,6},{6,7},{8,9},{9,10},{10,11},{11... | collective-permute-start | bytes 98312 | tf_op jit(solution)/shard_map/ppermute | solution.py:15
  408.1 6.3 %collective-permute-start.67 = (bf16[128,128]{1,0:T(8,128)(2,1)S(1)}, bf16[128,128]{1,0:T(8,128)(2,1)S(1)}, u32[]{:S(2)}, u32[]{:S(2)}) collective-permute-start(bf16[128,128]{1,0:T(8,128)(2,1)S(1)} %get-tuple-element.70), channel_id=1, source_target_pairs={{8,0},{16,8},{24,16},{32,24},{40,32},{48,40},{56,48},{64,56},{72,6... | collective-permute-start | bytes 98312 | tf_op jit(solution)/shard_map/ppermute | solution.py:15
  409.4 6.6 %collective-permute-start.66 = (bf16[128,128]{1,0:T(8,128)(2,1)S(1)}, bf16[128,128]{1,0:T(8,128)(2,1)S(1)}, u32[]{:S(2)}, u32[]{:S(2)}) collective-permute-start(bf16[128,128]{1,0:T(8,128)(2,1)S(1)} %get-tuple-element.68), channel_id=1, source_target_pairs={{0,8},{8,16},{16,24},{24,32},{32,40},{40,48},{48,56},{56,64},{64,7... | collective-permute-start | bytes 98312 | tf_op jit(solution)/shard_map/ppermute | solution.py:15
  427.2 7.0 %collective-permute-start.72 = (f32[6,128]{1,0:T(8,128)S(1)}, f32[6,128]{1,0:T(8,128)S(1)}, u32[]{:S(2)}, u32[]{:S(2)}) collective-permute-start(f32[6,128]{1,0:T(8,128)S(1)} %add.307), channel_id=1, source_target_pairs={{0,4},{1,5},{2,6},{3,7},{4,0},{5,1},{6,2},{7,3},{8,12},{9,13},{10,... | collective-permute-start | bytes 9224 | tf_op jit(solution)/shard_map/ppermute | solution.py:32
  440.0 7.5 %collective-permute-start.74 = (f32[6,128]{1,0:T(8,128)S(1)}, f32[6,128]{1,0:T(8,128)S(1)}, u32[]{:S(2)}, u32[]{:S(2)}) collective-permute-start(f32[6,128]{1,0:T(8,128)S(1)} %add.309), channel_id=1, source_target_pairs={{0,16},{8,24},{16,0},{24,8},{32,48},{40,56},{48,32},{56,40},{64,80... | collective-permute-start | bytes 9224 | tf_op jit(solution)/shard_map/ppermute | solution.py:32
  447.6 7.7 %collective-permute-start.75 = (f32[6,128]{1,0:T(8,128)S(1)}, f32[6,128]{1,0:T(8,128)S(1)}, u32[]{:S(2)}, u32[]{:S(2)}) collective-permute-start(f32[6,128]{1,0:T(8,128)S(1)} %add.310), channel_id=1, source_target_pairs={{0,32},{8,40},{16,48},{24,56},{32,0},{40,8},{48,16},{56,24},{64,96... | collective-permute-start | bytes 9224 | tf_op jit(solution)/shard_map/ppermute | solution.py:32
  455.3 6.4 %collective-permute-start.76 = (f32[6,128]{1,0:T(8,128)S(1)}, f32[6,128]{1,0:T(8,128)S(1)}, u32[]{:S(2)}, u32[]{:S(2)}) collective-permute-start(f32[6,128]{1,0:T(8,128)S(1)} %add.311), channel_id=1, source_target_pairs={{0,64},{8,72},{16,80},{24,88},{32,96},{40,104},{48,112},{56,120},{... | collective-permute-start | bytes 9224 | tf_op jit(solution)/shard_map/ppermute | solution.py:32
  461.7 12.2 %collective-permute-start.77 = (f32[6,128]{1,0:T(8,128)S(1)}, f32[6,128]{1,0:T(8,128)S(1)}, u32[]{:S(2)}, u32[]{:S(2)}) collective-permute-start(f32[6,128]{1,0:T(8,128)S(1)} %add.312), channel_id=1, source_target_pairs={{0,128},{8,136},{16,144},{24,152},{32,160},{40,168},{48,176},{56,1... | collective-permute-start | bytes 9224 | tf_op jit(solution)/shard_map/ppermute | solution.py:32
  473.9 15.2 %collective-permute-start.78 = (f32[6,128]{1,0:T(8,128)S(1)}, f32[6,128]{1,0:T(8,128)S(1)}, u32[]{:S(2)}, u32[]{:S(2)}) collective-permute-start(f32[6,128]{1,0:T(8,128)S(1)} %add.313), channel_id=1, source_target_pairs={{0,256},{8,264},{16,272},{24,280},{32,288},{40,296},{48,304},{56,3... | collective-permute-start | bytes 9224 | tf_op jit(solution)/shard_map/ppermute | solution.py:32
  (22 other events, 364.8 us)

commit v4 on v3

--- a/solution.py
+++ b/solution.py
@@ -107,13 +107,7 @@
     gathered_map = coarse_map[gathered_order(rounds, count_y)]
     selection = (
         gathered_map[:, None] == jnp.arange(gathered_map.shape[0], dtype=jnp.int32)[None, :]
-    ).astype(coarse_rows.dtype)
-    permuted = jnp.einsum(
-        "bq,rqc->rbc",
-        selection,
-        coarse_rows.reshape(basis_count, -1, basis_count),
-        preferred_element_type=jnp.float32,
-    ).astype(coarse_rows.dtype).reshape(basis_count, -1)
+    ).astype(jnp.bfloat16)
 
     def margin_of(field):
         return exchange(field[margin_rows])
@@ -127,7 +121,13 @@
         residual = lax.dot_general(
             basis, rounded, (((0,), (0,)), ((), ())), preferred_element_type=jnp.float32
         ).astype(jnp.bfloat16)
-        solved = jnp.dot(permuted, coarse_gather(residual), preferred_element_type=jnp.float32)
+        gathered = coarse_gather(residual).reshape(selection.shape[0], -1)
+        placed = lax.dot_general(
+            selection, gathered, (((0,), (0,)), ((), ())), preferred_element_type=jnp.float32
+        ).astype(jnp.bfloat16)
+        solved = jnp.dot(
+            coarse_rows, placed.reshape(-1, system_count), preferred_element_type=jnp.float32
+        )
         return local_part + jnp.dot(
             basis, solved.astype(jnp.bfloat16), preferred_element_type=jnp.float32
         )

time: 494 us -> 494 us (level)
  waiting for transfers between devices: 160 us -> 138 us
  local copies, waits for them, and re-layouts: 25.9 us -> 33.5 us
  starting transfers between devices: 277 us -> 282 us
    ppermute x18, waiting for transfers between devices: 101 us -> 83.4 us  [doubling_gather(): got = lax.ppermute(held, axis, [(i, i ^ step) for i in range(count)])]
    reshape x0 -> x2, local copies, waits for them, and re-layouts: none -> 14.8 us  [precondition(): placed.reshape(-1, system_count)]
    dot_general x0 -> x2, matrix products: none -> 8.49 us  [precondition(): lax.dot_general(selection, gathered, (((0,), (0,)), ((), ())), preferred_...]
    unnamed x19 -> x103, local copies, waits for them, and re-layouts: 0.78 us -> 8.77 us
    another operation x2 -> x0, local copies, waits for them, and re-layouts: 7.9 us -> none  [on_device(): coarse_rows.reshape(basis_count, -1, basis_count)]
    convert_element_type x1 -> x0, local copies, waits for them, and re-layouts: 6.43 us -> none  [on_device(): permuted = jnp.einsum('bq,rqc->rbc', selection, coarse_rows.reshape(basis...]
    ppermute x27, starting transfers between devices: 154 us -> 159 us  [allsum(): lax.ppermute(value, axis, [(i, i ^ step) for i in range(count)])]
  transfers between devices with their start and end apart: 61 -> 61, of which waited for: 47 -> 49; matrix products, arithmetic and copies ran while one was open for 5% -> 2% of each run, Pallas kernels for 0% -> 0%
where the time goes in v4:
time: 494 us; the launch traced here: 490 us
  starting transfers between devices  282 us (57%)
  waiting for transfers between devices  138 us (28%)
  local copies, waits for them, and re-layouts  33.5 us (7%)
  matrix products  17.6 us (4%)
  other arithmetic  13.9 us (3%)
    ppermute x27, starting transfers between devices, allsum(): lax.ppermute(value, axis, [(i, i ^ step) for i in range(count)])  159 us
    ppermute x18, waiting for transfers between devices, doubling_gather(): got = lax.ppermute(held, axis, [(i, i ^ step) for i in range(count)])  83.4 us
    ppermute x18, starting transfers between devices, doubling_gather(): got = lax.ppermute(held, axis, [(i, i ^ step) for i in range(count)])  81.6 us
    ppermute x27, waiting for transfers between devices, allsum(): lax.ppermute(value, axis, [(i, i ^ step) for i in range(count)])  50.2 us
    ppermute x16, starting transfers between devices, neighbours(): return (lax.ppermute(rows[1], axis, up), lax.ppermute(rows[0], axis, down))  42 us
    reshape x2, local copies, waits for them, and re-layouts, precondition(): placed.reshape(-1, system_count)  14.8 us
  transfers between devices with their start and end apart: 61, of which 49 were waited for; matrix products, arithmetic and copies ran while one was open for 2% of the time, Pallas kernels for 0%

profile of v4, /device:TPU:6, one launch (start us, length us, event | category | flops | bytes accessed | tf_op | source)
XLA Modules:
  0.0 489.6 jit_solution(3216065414461967651)
XLA Ops:
  10.1 7.2 %collective-permute-start.20 = (f32[128]{0:T(128)S(1)}, f32[128]{0:T(128)S(1)}, u32[]{:S(2)}, u32[]{:S(2)}) collective-permute-start(f32[128]{0:T(128)S(1)} %add.270), channel_id=1, source_target_pairs={{0,4},{1,5},{2,6},{3,7},{4,0},{5,1},{6,2},{7,3},{8,12},{9,13},{10,... | collective-permute-start | bytes 1544 | tf_op jit(solution)/shard_map/ppermute | solution.py:32
  20.7 3.5 collective-permute-done.21
  27.6 3.6 collective-permute-done.22
  43.0 7.7 %collective-permute-start.25 = (f32[128]{0:T(128)S(1)}, f32[128]{0:T(128)S(1)}, u32[]{:S(2)}, u32[]{:S(2)}) collective-permute-start(f32[128]{0:T(128)S(1)} %add.275), channel_id=1, source_target_pairs={{0,128},{8,136},{16,144},{24,152},{32,160},{40,168},{48,176},{56,1... | collective-permute-start | bytes 1544 | tf_op jit(solution)/shard_map/ppermute | solution.py:32
  52.4 14.0 %collective-permute-start.26 = (f32[128]{0:T(128)S(1)}, f32[128]{0:T(128)S(1)}, u32[]{:S(2)}, u32[]{:S(2)}) collective-permute-start(f32[128]{0:T(128)S(1)} %add.276), channel_id=1, source_target_pairs={{0,256},{8,264},{16,272},{24,280},{32,288},{40,296},{48,304},{56,3... | collective-permute-start | bytes 1544 | tf_op jit(solution)/shard_map/ppermute | solution.py:32
  68.9 12.6 %collective-permute-start.31 = (bf16[1,32,128]{2,1,0:T(8,128)(2,1)S(1)}, bf16[1,32,128]{2,1,0:T(8,128)(2,1)S(1)}, u32[]{:S(2)}, u32[]{:S(2)}) collective-permute-start(bf16[1,32,128]{2,1,0:T(8,128)(2,1)S(1)} %fusion.14), channel_id=1, source_target_pairs={{0,256},{8,264},{16,272},{24,280},{32,288},{40,296},{48,304},{56,3... | collective-permute-start | bytes 24584 | tf_op jit(solution)/shard_map/ppermute | solution.py:51
  83.2 6.4 %collective-permute-start.32 = (bf16[2,32,128]{2,1,0:T(8,128)(2,1)S(1)}, bf16[2,32,128]{2,1,0:T(8,128)(2,1)S(1)}, u32[]{:S(2)}, u32[]{:S(2)}) collective-permute-start(bf16[2,32,128]{2,1,0:T(8,128)(2,1)S(1)} %maximum_select_fusion.24), channel_id=1, source_target_pairs={{0,128},{8,136},{16,144},{24,152},{32,160},{40,168},{48,176},{56,1... | collective-permute-start | bytes 49160 | tf_op jit(solution)/shard_map/ppermute | solution.py:51
  105.7 5.1 %collective-permute-start.35 = (bf16[16,32,128]{2,1,0:T(8,128)(2,1)S(1)}, bf16[16,32,128]{2,1,0:T(8,128)(2,1)S(1)}, u32[]{:S(2)}, u32[]{:S(2)}) collective-permute-start(bf16[16,32,128]{2,1,0:T(8,128)(2,1)S(1)} %maximum_select_fusion.18), channel_id=1, source_target_pairs={{0,16},{8,24},{16,0},{24,8},{32,48},{40,56},{48,32},{56,40},{64,80... | collective-permute-start | bytes 393224 | tf_op jit(solution)/shard_map/ppermute | solution.py:51
  117.6 4.8 collective-permute-done.36
  123.2 4.1 collective-permute-start.37
  127.4 14.0 %collective-permute-done.37 = bf16[64,32,128]{2,1,0:T(8,128)(2,1)S(1)} collective-permute-done((bf16[64,32,128]{2,1,0:T(8,128)(2,1)S(1)}, bf16[64,32,128]{2,1,0:T(8,128)(2,1)S(1)}, u32[]{:S(2)}, u32[]{:S(2)}) %collective-permute-start.37) | collective-permute-done | bytes 524320 | tf_op jit(solution)/shard_map/ppermute | solution.py:51
  154.8 3.6 collective-permute-start.30
  169.6 4.2 convolution_convert_fusion.1
  173.9 7.4 %reshape.148 = bf16[16384,128]{1,0:T(8,128)(2,1)} reshape(bf16[512,4096]{1,0:T(8,128)(2,1)} %convolution_convert_fusion.1) | data formatting | bytes 8388608 | tf_op jit(solution)/shard_map/reshape | solution.py:129
  181.3 3.6 convolution_add_fusion.1
  186.4 4.3 collective-permute-start.40
  193.9 3.8 collective-permute-start.43
  204.9 3.7 collective-permute-start.45
  210.4 4.9 %collective-permute-start.46 = (f32[3,128]{1,0:T(4,128)S(1)}, f32[3,128]{1,0:T(4,128)S(1)}, u32[]{:S(2)}, u32[]{:S(2)}) collective-permute-start(f32[3,128]{1,0:T(4,128)S(1)} %fusion.79), channel_id=1, source_target_pairs={{0,4},{1,5},{2,6},{3,7},{4,0},{5,1},{6,2},{7,3},{8,12},{9,13},{10,... | collective-permute-start | bytes 4616 | tf_op jit(solution)/shard_map/ppermute | solution.py:32
  217.3 4.3 collective-permute-start.47
  223.2 6.5 %collective-permute-start.48 = (f32[3,128]{1,0:T(4,128)S(1)}, f32[3,128]{1,0:T(4,128)S(1)}, u32[]{:S(2)}, u32[]{:S(2)}) collective-permute-start(f32[3,128]{1,0:T(4,128)S(1)} %add.296), channel_id=1, source_target_pairs={{0,16},{8,24},{16,0},{24,8},{32,48},{40,56},{48,32},{56,40},{64,80... | collective-permute-start | bytes 4616 | tf_op jit(solution)/shard_map/ppermute | solution.py:32
  231.2 6.4 %collective-permute-start.49 = (f32[3,128]{1,0:T(4,128)S(1)}, f32[3,128]{1,0:T(4,128)S(1)}, u32[]{:S(2)}, u32[]{:S(2)}) collective-permute-start(f32[3,128]{1,0:T(4,128)S(1)} %add.297), channel_id=1, source_target_pairs={{0,32},{8,40},{16,48},{24,56},{32,0},{40,8},{48,16},{56,24},{64,96... | collective-permute-start | bytes 4616 | tf_op jit(solution)/shard_map/ppermute | solution.py:32
  239.2 4.8 collective-permute-start.50
  245.5 10.1 %collective-permute-start.51 = (f32[3,128]{1,0:T(4,128)S(1)}, f32[3,128]{1,0:T(4,128)S(1)}, u32[]{:S(2)}, u32[]{:S(2)}) collective-permute-start(f32[3,128]{1,0:T(4,128)S(1)} %add.299), channel_id=1, source_target_pairs={{0,128},{8,136},{16,144},{24,152},{32,160},{40,168},{48,176},{56,1... | collective-permute-start | bytes 4616 | tf_op jit(solution)/shard_map/ppermute | solution.py:32
  257.2 13.7 %collective-permute-start.52 = (f32[3,128]{1,0:T(4,128)S(1)}, f32[3,128]{1,0:T(4,128)S(1)}, u32[]{:S(2)}, u32[]{:S(2)}) collective-permute-start(f32[3,128]{1,0:T(4,128)S(1)} %add.300), channel_id=1, source_target_pairs={{0,256},{8,264},{16,272},{24,280},{32,288},{40,296},{48,304},{56,3... | collective-permute-start | bytes 4616 | tf_op jit(solution)/shard_map/ppermute | solution.py:32
  275.2 12.6 %collective-permute-start.57 = (bf16[1,32,128]{2,1,0:T(8,128)(2,1)S(1)}, bf16[1,32,128]{2,1,0:T(8,128)(2,1)S(1)}, u32[]{:S(2)}, u32[]{:S(2)}) collective-permute-start(bf16[1,32,128]{2,1,0:T(8,128)(2,1)S(1)} %fusion.15), channel_id=1, source_target_pairs={{0,256},{8,264},{16,272},{24,280},{32,288},{40,296},{48,304},{56,3... | collective-permute-start | bytes 24584 | tf_op jit(solution)/shard_map/ppermute | solution.py:51
  289.4 6.7 %collective-permute-start.58 = (bf16[2,32,128]{2,1,0:T(8,128)(2,1)S(1)}, bf16[2,32,128]{2,1,0:T(8,128)(2,1)S(1)}, u32[]{:S(2)}, u32[]{:S(2)}) collective-permute-start(bf16[2,32,128]{2,1,0:T(8,128)(2,1)S(1)} %maximum_select_fusion.25), channel_id=1, source_target_pairs={{0,128},{8,136},{16,144},{24,152},{32,160},{40,168},{48,176},{56,1... | collective-permute-start | bytes 49160 | tf_op jit(solution)/shard_map/ppermute | solution.py:51
  301.1 4.6 collective-permute-done.59
  307.7 4.2 collective-permute-done.60
  314.5 5.8 %collective-permute-done.61 = bf16[16,32,128]{2,1,0:T(8,128)(2,1)S(1)} collective-permute-done((bf16[16,32,128]{2,1,0:T(8,128)(2,1)S(1)}, bf16[16,32,128]{2,1,0:T(8,128)(2,1)S(1)}, u32[]{:S(2)}, u32[]{:S(2)}) %collective-permute-start.61) | collective-permute-done | bytes 131104 | tf_op jit(solution)/shard_map/ppermute | solution.py:51
  322.5 6.1 %collective-permute-done.62 = bf16[32,32,128]{2,1,0:T(8,128)(2,1)S(1)} collective-permute-done((bf16[32,32,128]{2,1,0:T(8,128)(2,1)S(1)}, bf16[32,32,128]{2,1,0:T(8,128)(2,1)S(1)}, u32[]{:S(2)}, u32[]{:S(2)}) %collective-permute-start.62) | collective-permute-done | bytes 262176 | tf_op jit(solution)/shard_map/ppermute | solution.py:51
  329.4 4.9 %collective-permute-start.63 = (bf16[64,32,128]{2,1,0:T(8,128)(2,1)S(1)}, bf16[64,32,128]{2,1,0:T(8,128)(2,1)S(1)}, u32[]{:S(2)}, u32[]{:S(2)}) collective-permute-start(bf16[64,32,128]{2,1,0:T(8,128)(2,1)S(1)} %maximum_select_fusion.14), channel_id=1, source_target_pairs={{0,4},{1,5},{2,6},{3,7},{4,0},{5,1},{6,2},{7,3},{8,12},{9,13},{10,... | collective-permute-start | bytes 1572872 | tf_op jit(solution)/shard_map/ppermute | solution.py:51
  334.4 13.3 %collective-permute-done.63 = bf16[64,32,128]{2,1,0:T(8,128)(2,1)S(1)} collective-permute-done((bf16[64,32,128]{2,1,0:T(8,128)(2,1)S(1)}, bf16[64,32,128]{2,1,0:T(8,128)(2,1)S(1)}, u32[]{:S(2)}, u32[]{:S(2)}) %collective-permute-start.63) | collective-permute-done | bytes 524320 | tf_op jit(solution)/shard_map/ppermute | solution.py:51
  348.6 3.9 collective-permute-start.64
  354.2 11.1 %collective-permute-done.64 = bf16[128,32,128]{2,1,0:T(8,128)(2,1)S(1)} collective-permute-done((bf16[128,32,128]{2,1,0:T(8,128)(2,1)S(1)}, bf16[128,32,128]{2,1,0:T(8,128)(2,1)S(1)}, u32[]{:S(2)}, u32[]{:S(2)}) %collective-permute-start.64) | collective-permute-done | bytes 1048608 | tf_op jit(solution)/shard_map/ppermute | solution.py:51
  381.9 4.2 convolution_convert_fusion
  386.1 7.4 %reshape.150 = bf16[16384,128]{1,0:T(8,128)(2,1)} reshape(bf16[512,4096]{1,0:T(8,128)(2,1)} %convolution_convert_fusion) | data formatting | bytes 8388608 | tf_op jit(solution)/shard_map/reshape | solution.py:129
  393.5 3.6 convolution_add_fusion
  398.7 4.3 collective-permute-start.66
  406.4 3.6 collective-permute-start.69
  417.5 3.7 collective-permute-start.71
  423.0 5.5 %collective-permute-start.72 = (f32[6,128]{1,0:T(8,128)S(1)}, f32[6,128]{1,0:T(8,128)S(1)}, u32[]{:S(2)}, u32[]{:S(2)}) collective-permute-start(f32[6,128]{1,0:T(8,128)S(1)} %add.307), channel_id=1, source_target_pairs={{0,4},{1,5},{2,6},{3,7},{4,0},{5,1},{6,2},{7,3},{8,12},{9,13},{10,... | collective-permute-start | bytes 9224 | tf_op jit(solution)/shard_map/ppermute | solution.py:32
  430.1 4.3 collective-permute-start.73
  435.9 7.5 %collective-permute-start.74 = (f32[6,128]{1,0:T(8,128)S(1)}, f32[6,128]{1,0:T(8,128)S(1)}, u32[]{:S(2)}, u32[]{:S(2)}) collective-permute-start(f32[6,128]{1,0:T(8,128)S(1)} %add.309), channel_id=1, source_target_pairs={{0,16},{8,24},{16,0},{24,8},{32,48},{40,56},{48,32},{56,40},{64,80... | collective-permute-start | bytes 9224 | tf_op jit(solution)/shard_map/ppermute | solution.py:32
  445.0 6.3 %collective-permute-start.75 = (f32[6,128]{1,0:T(8,128)S(1)}, f32[6,128]{1,0:T(8,128)S(1)}, u32[]{:S(2)}, u32[]{:S(2)}) collective-permute-start(f32[6,128]{1,0:T(8,128)S(1)} %add.310), channel_id=1, source_target_pairs={{0,32},{8,40},{16,48},{24,56},{32,0},{40,8},{48,16},{56,24},{64,96... | collective-permute-start | bytes 9224 | tf_op jit(solution)/shard_map/ppermute | solution.py:32
  452.8 5.3 %collective-permute-start.76 = (f32[6,128]{1,0:T(8,128)S(1)}, f32[6,128]{1,0:T(8,128)S(1)}, u32[]{:S(2)}, u32[]{:S(2)}) collective-permute-start(f32[6,128]{1,0:T(8,128)S(1)} %add.311), channel_id=1, source_target_pairs={{0,64},{8,72},{16,80},{24,88},{32,96},{40,104},{48,112},{56,120},{... | collective-permute-start | bytes 9224 | tf_op jit(solution)/shard_map/ppermute | solution.py:32
  459.7 10.1 %collective-permute-start.77 = (f32[6,128]{1,0:T(8,128)S(1)}, f32[6,128]{1,0:T(8,128)S(1)}, u32[]{:S(2)}, u32[]{:S(2)}) collective-permute-start(f32[6,128]{1,0:T(8,128)S(1)} %add.312), channel_id=1, source_target_pairs={{0,128},{8,136},{16,144},{24,152},{32,160},{40,168},{48,176},{56,1... | collective-permute-start | bytes 9224 | tf_op jit(solution)/shard_map/ppermute | solution.py:32
  471.4 13.8 %collective-permute-start.78 = (f32[6,128]{1,0:T(8,128)S(1)}, f32[6,128]{1,0:T(8,128)S(1)}, u32[]{:S(2)}, u32[]{:S(2)}) collective-permute-start(f32[6,128]{1,0:T(8,128)S(1)} %add.313), channel_id=1, source_target_pairs={{0,256},{8,264},{16,272},{24,280},{32,288},{40,296},{48,304},{56,3... | collective-permute-start | bytes 9224 | tf_op jit(solution)/shard_map/ppermute | solution.py:32
  (279 shorter events, 168.6 us)
Async XLA Ops:
  10.1 8.7 %collective-permute-start.20 = (f32[128]{0:T(128)S(1)}, f32[128]{0:T(128)S(1)}, u32[]{:S(2)}, u32[]{:S(2)}) collective-permute-start(f32[128]{0:T(128)S(1)} %add.270), channel_id=1, source_target_pairs={{0,4},{1,5},{2,6},{3,7},{4,0},{5,1},{6,2},{7,3},{8,12},{9,13},{10,... | collective-permute-start | bytes 1544 | tf_op jit(solution)/shard_map/ppermute | solution.py:32
  24.3 7.0 %collective-permute-start.22 = (f32[128]{0:T(128)S(1)}, f32[128]{0:T(128)S(1)}, u32[]{:S(2)}, u32[]{:S(2)}) collective-permute-start(f32[128]{0:T(128)S(1)} %add.272), channel_id=1, source_target_pairs={{0,16},{8,24},{16,0},{24,8},{32,48},{40,56},{48,32},{56,40},{64,80... | collective-permute-start | bytes 1544 | tf_op jit(solution)/shard_map/ppermute | solution.py:32
  36.7 6.3 %collective-permute-start.24 = (f32[128]{0:T(128)S(1)}, f32[128]{0:T(128)S(1)}, u32[]{:S(2)}, u32[]{:S(2)}) collective-permute-start(f32[128]{0:T(128)S(1)} %add.274), channel_id=1, source_target_pairs={{0,64},{8,72},{16,80},{24,88},{32,96},{40,104},{48,112},{56,120},{... | collective-permute-start | bytes 1544 | tf_op jit(solution)/shard_map/ppermute | solution.py:32
  43.0 9.4 %collective-permute-start.25 = (f32[128]{0:T(128)S(1)}, f32[128]{0:T(128)S(1)}, u32[]{:S(2)}, u32[]{:S(2)}) collective-permute-start(f32[128]{0:T(128)S(1)} %add.275), channel_id=1, source_target_pairs={{0,128},{8,136},{16,144},{24,152},{32,160},{40,168},{48,176},{56,1... | collective-permute-start | bytes 1544 | tf_op jit(solution)/shard_map/ppermute | solution.py:32
  52.4 15.5 %collective-permute-start.26 = (f32[128]{0:T(128)S(1)}, f32[128]{0:T(128)S(1)}, u32[]{:S(2)}, u32[]{:S(2)}) collective-permute-start(f32[128]{0:T(128)S(1)} %add.276), channel_id=1, source_target_pairs={{0,256},{8,264},{16,272},{24,280},{32,288},{40,296},{48,304},{56,3... | collective-permute-start | bytes 1544 | tf_op jit(solution)/shard_map/ppermute | solution.py:32
  68.9 14.3 %collective-permute-start.31 = (bf16[1,32,128]{2,1,0:T(8,128)(2,1)S(1)}, bf16[1,32,128]{2,1,0:T(8,128)(2,1)S(1)}, u32[]{:S(2)}, u32[]{:S(2)}) collective-permute-start(bf16[1,32,128]{2,1,0:T(8,128)(2,1)S(1)} %fusion.14), channel_id=1, source_target_pairs={{0,256},{8,264},{16,272},{24,280},{32,288},{40,296},{48,304},{56,3... | collective-permute-start | bytes 24584 | tf_op jit(solution)/shard_map/ppermute | solution.py:51
  83.2 9.6 %collective-permute-start.32 = (bf16[2,32,128]{2,1,0:T(8,128)(2,1)S(1)}, bf16[2,32,128]{2,1,0:T(8,128)(2,1)S(1)}, u32[]{:S(2)}, u32[]{:S(2)}) collective-permute-start(bf16[2,32,128]{2,1,0:T(8,128)(2,1)S(1)} %maximum_select_fusion.24), channel_id=1, source_target_pairs={{0,128},{8,136},{16,144},{24,152},{32,160},{40,168},{48,176},{56,1... | collective-permute-start | bytes 49160 | tf_op jit(solution)/shard_map/ppermute | solution.py:51
  92.8 6.7 %collective-permute-start.33 = (bf16[4,32,128]{2,1,0:T(8,128)(2,1)S(1)}, bf16[4,32,128]{2,1,0:T(8,128)(2,1)S(1)}, u32[]{:S(2)}, u32[]{:S(2)}) collective-permute-start(bf16[4,32,128]{2,1,0:T(8,128)(2,1)S(1)} %maximum_select_fusion.22), channel_id=1, source_target_pairs={{0,64},{8,72},{16,80},{24,88},{32,96},{40,104},{48,112},{56,120},{... | collective-permute-start | bytes 98312 | tf_op jit(solution)/shard_map/ppermute | solution.py:51
  99.5 6.2 %collective-permute-start.34 = (bf16[8,32,128]{2,1,0:T(8,128)(2,1)S(1)}, bf16[8,32,128]{2,1,0:T(8,128)(2,1)S(1)}, u32[]{:S(2)}, u32[]{:S(2)}) collective-permute-start(bf16[8,32,128]{2,1,0:T(8,128)(2,1)S(1)} %maximum_select_fusion.20), channel_id=1, source_target_pairs={{0,32},{8,40},{16,48},{24,56},{32,0},{40,8},{48,16},{56,24},{64,96... | collective-permute-start | bytes 196616 | tf_op jit(solution)/shard_map/ppermute | solution.py:51
  105.7 8.4 %collective-permute-start.35 = (bf16[16,32,128]{2,1,0:T(8,128)(2,1)S(1)}, bf16[16,32,128]{2,1,0:T(8,128)(2,1)S(1)}, u32[]{:S(2)}, u32[]{:S(2)}) collective-permute-start(bf16[16,32,128]{2,1,0:T(8,128)(2,1)S(1)} %maximum_select_fusion.18), channel_id=1, source_target_pairs={{0,16},{8,24},{16,0},{24,8},{32,48},{40,56},{48,32},{56,40},{64,80... | collective-permute-start | bytes 393224 | tf_op jit(solution)/shard_map/ppermute | solution.py:51
  114.1 8.3 %collective-permute-start.36 = (bf16[32,32,128]{2,1,0:T(8,128)(2,1)S(1)}, bf16[32,32,128]{2,1,0:T(8,128)(2,1)S(1)}, u32[]{:S(2)}, u32[]{:S(2)}) collective-permute-start(bf16[32,32,128]{2,1,0:T(8,128)(2,1)S(1)} %maximum_select_fusion.16), channel_id=1, source_target_pairs={{0,8},{8,0},{16,24},{24,16},{32,40},{40,32},{48,56},{56,48},{64,72... | collective-permute-start | bytes 786440 | tf_op jit(solution)/shard_map/ppermute | solution.py:51
  123.2 18.2 %collective-permute-start.37 = (bf16[64,32,128]{2,1,0:T(8,128)(2,1)S(1)}, bf16[64,32,128]{2,1,0:T(8,128)(2,1)S(1)}, u32[]{:S(2)}, u32[]{:S(2)}) collective-permute-start(bf16[64,32,128]{2,1,0:T(8,128)(2,1)S(1)} %maximum_select_fusion.12), channel_id=1, source_target_pairs={{0,4},{1,5},{2,6},{3,7},{4,0},{5,1},{6,2},{7,3},{8,12},{9,13},{10,... | collective-permute-start | bytes 1572872 | tf_op jit(solution)/shard_map/ppermute | solution.py:51
  143.6 18.5 %collective-permute-start.38 = (bf16[128,32,128]{2,1,0:T(8,128)(2,1)S(1)}, bf16[128,32,128]{2,1,0:T(8,128)(2,1)S(1)}, u32[]{:S(2)}, u32[]{:S(2)}) collective-permute-start(bf16[128,32,128]{2,1,0:T(8,128)(2,1)S(1)} %maximum_select_fusion.8), channel_id=1, source_target_pairs={{0,2},{1,3},{2,0},{3,1},{4,6},{5,7},{6,4},{7,5},{8,10},{9,11},{10,... | collective-permute-start | bytes 3145736 | tf_op jit(solution)/shard_map/ppermute | solution.py:51
  148.1 16.4 %collective-permute-start.27 = (f32[128,128]{1,0:T(8,128)}, f32[128,128]{1,0:T(8,128)S(1)}, u32[]{:S(2)}, u32[]{:S(2)}) collective-permute-start(f32[128,128]{1,0:T(8,128)} %get-tuple-element.64), channel_id=1, source_target_pairs={{0,8},{8,16},{16,24},{24,32},{32,40},{40,48},{48,56},{56,64},{64,7... | collective-permute-start | bytes 196616 | tf_op jit(solution)/shard_map/ppermute | solution.py:15
  151.6 12.9 %collective-permute-start.29 = (f32[128,128]{1,0:T(8,128)}, f32[128,128]{1,0:T(8,128)S(1)}, u32[]{:S(2)}, u32[]{:S(2)}) collective-permute-start(f32[128,128]{1,0:T(8,128)} %get-tuple-element.65), channel_id=1, source_target_pairs={{0,1},{1,2},{2,3},{3,4},{4,5},{5,6},{6,7},{8,9},{9,10},{10,11},{11... | collective-permute-start | bytes 196616 | tf_op jit(solution)/shard_map/ppermute | solution.py:15
  153.5 11.0 %collective-permute-start.28 = (f32[128,128]{1,0:T(8,128)}, f32[128,128]{1,0:T(8,128)S(1)}, u32[]{:S(2)}, u32[]{:S(2)}) collective-permute-start(f32[128,128]{1,0:T(8,128)} %get-tuple-element.66), channel_id=1, source_target_pairs={{8,0},{16,8},{24,16},{32,24},{40,32},{48,40},{56,48},{64,56},{72,6... | collective-permute-start | bytes 196616 | tf_op jit(solution)/shard_map/ppermute | solution.py:15
  154.8 9.8 %collective-permute-start.30 = (f32[128,128]{1,0:T(8,128)}, f32[128,128]{1,0:T(8,128)}, u32[]{:S(2)}, u32[]{:S(2)}) collective-permute-start(f32[128,128]{1,0:T(8,128)} %get-tuple-element.67), channel_id=1, source_target_pairs={{1,0},{2,1},{3,2},{4,3},{5,4},{6,5},{7,6},{9,8},{10,9},{11,10},{12... | collective-permute-start | bytes 196616 | tf_op jit(solution)/shard_map/ppermute | solution.py:15
  162.4 6.2 %collective-permute-start.39 = (bf16[256,32,128]{2,1,0:T(8,128)(2,1)S(1)}, bf16[256,32,128]{2,1,0:T(8,128)(2,1)S(1)}, u32[]{:S(2)}, u32[]{:S(2)}) collective-permute-start(bf16[256,32,128]{2,1,0:T(8,128)(2,1)S(1)} %maximum_select_fusion.4), channel_id=1, source_target_pairs={{0,1},{1,0},{2,3},{3,2},{4,5},{5,4},{6,7},{7,6},{8,9},{9,8},{10,11... | collective-permute-start | bytes 6291464 | tf_op jit(solution)/shard_map/ppermute | solution.py:51
  186.4 11.4 %collective-permute-start.40 = (bf16[128,128]{1,0:T(8,128)(2,1)S(1)}, bf16[128,128]{1,0:T(8,128)(2,1)S(1)}, u32[]{:S(2)}, u32[]{:S(2)}) collective-permute-start(bf16[128,128]{1,0:T(8,128)(2,1)S(1)} %get-tuple-element.72), channel_id=1, source_target_pairs={{0,8},{8,16},{16,24},{24,32},{32,40},{40,48},{48,56},{56,64},{64,7... | collective-permute-start | bytes 98312 | tf_op jit(solution)/shard_map/ppermute | solution.py:15
  190.7 7.1 %collective-permute-start.42 = (bf16[128,128]{1,0:T(8,128)(2,1)S(1)}, bf16[128,128]{1,0:T(8,128)(2,1)S(1)}, u32[]{:S(2)}, u32[]{:S(2)}) collective-permute-start(bf16[128,128]{1,0:T(8,128)(2,1)S(1)} %get-tuple-element.73), channel_id=1, source_target_pairs={{0,1},{1,2},{2,3},{3,4},{4,5},{5,6},{6,7},{8,9},{9,10},{10,11},{11... | collective-permute-start | bytes 98312 | tf_op jit(solution)/shard_map/ppermute | solution.py:15
  210.4 7.0 %collective-permute-start.46 = (f32[3,128]{1,0:T(4,128)S(1)}, f32[3,128]{1,0:T(4,128)S(1)}, u32[]{:S(2)}, u32[]{:S(2)}) collective-permute-start(f32[3,128]{1,0:T(4,128)S(1)} %fusion.79), channel_id=1, source_target_pairs={{0,4},{1,5},{2,6},{3,7},{4,0},{5,1},{6,2},{7,3},{8,12},{9,13},{10,... | collective-permute-start | bytes 4616 | tf_op jit(solution)/shard_map/ppermute | solution.py:32
  217.3 5.8 %collective-permute-start.47 = (f32[3,128]{1,0:T(4,128)S(1)}, f32[3,128]{1,0:T(4,128)S(1)}, u32[]{:S(2)}, u32[]{:S(2)}) collective-permute-start(f32[3,128]{1,0:T(4,128)S(1)} %add.295), channel_id=1, source_target_pairs={{0,8},{8,0},{16,24},{24,16},{32,40},{40,32},{48,56},{56,48},{64,72... | collective-permute-start | bytes 4616 | tf_op jit(solution)/shard_map/ppermute | solution.py:32
  223.2 8.1 %collective-permute-start.48 = (f32[3,128]{1,0:T(4,128)S(1)}, f32[3,128]{1,0:T(4,128)S(1)}, u32[]{:S(2)}, u32[]{:S(2)}) collective-permute-start(f32[3,128]{1,0:T(4,128)S(1)} %add.296), channel_id=1, source_target_pairs={{0,16},{8,24},{16,0},{24,8},{32,48},{40,56},{48,32},{56,40},{64,80... | collective-permute-start | bytes 4616 | tf_op jit(solution)/shard_map/ppermute | solution.py:32
  231.2 7.9 %collective-permute-start.49 = (f32[3,128]{1,0:T(4,128)S(1)}, f32[3,128]{1,0:T(4,128)S(1)}, u32[]{:S(2)}, u32[]{:S(2)}) collective-permute-start(f32[3,128]{1,0:T(4,128)S(1)} %add.297), channel_id=1, source_target_pairs={{0,32},{8,40},{16,48},{24,56},{32,0},{40,8},{48,16},{56,24},{64,96... | collective-permute-start | bytes 4616 | tf_op jit(solution)/shard_map/ppermute | solution.py:32
  239.2 6.4 %collective-permute-start.50 = (f32[3,128]{1,0:T(4,128)S(1)}, f32[3,128]{1,0:T(4,128)S(1)}, u32[]{:S(2)}, u32[]{:S(2)}) collective-permute-start(f32[3,128]{1,0:T(4,128)S(1)} %add.298), channel_id=1, source_target_pairs={{0,64},{8,72},{16,80},{24,88},{32,96},{40,104},{48,112},{56,120},{... | collective-permute-start | bytes 4616 | tf_op jit(solution)/shard_map/ppermute | solution.py:32
  245.5 11.7 %collective-permute-start.51 = (f32[3,128]{1,0:T(4,128)S(1)}, f32[3,128]{1,0:T(4,128)S(1)}, u32[]{:S(2)}, u32[]{:S(2)}) collective-permute-start(f32[3,128]{1,0:T(4,128)S(1)} %add.299), channel_id=1, source_target_pairs={{0,128},{8,136},{16,144},{24,152},{32,160},{40,168},{48,176},{56,1... | collective-permute-start | bytes 4616 | tf_op jit(solution)/shard_map/ppermute | solution.py:32
  257.2 15.3 %collective-permute-start.52 = (f32[3,128]{1,0:T(4,128)S(1)}, f32[3,128]{1,0:T(4,128)S(1)}, u32[]{:S(2)}, u32[]{:S(2)}) collective-permute-start(f32[3,128]{1,0:T(4,128)S(1)} %add.300), channel_id=1, source_target_pairs={{0,256},{8,264},{16,272},{24,280},{32,288},{40,296},{48,304},{56,3... | collective-permute-start | bytes 4616 | tf_op jit(solution)/shard_map/ppermute | solution.py:32
  275.2 14.3 %collective-permute-start.57 = (bf16[1,32,128]{2,1,0:T(8,128)(2,1)S(1)}, bf16[1,32,128]{2,1,0:T(8,128)(2,1)S(1)}, u32[]{:S(2)}, u32[]{:S(2)}) collective-permute-start(bf16[1,32,128]{2,1,0:T(8,128)(2,1)S(1)} %fusion.15), channel_id=1, source_target_pairs={{0,256},{8,264},{16,272},{24,280},{32,288},{40,296},{48,304},{56,3... | collective-permute-start | bytes 24584 | tf_op jit(solution)/shard_map/ppermute | solution.py:51
  289.4 9.6 %collective-permute-start.58 = (bf16[2,32,128]{2,1,0:T(8,128)(2,1)S(1)}, bf16[2,32,128]{2,1,0:T(8,128)(2,1)S(1)}, u32[]{:S(2)}, u32[]{:S(2)}) collective-permute-start(bf16[2,32,128]{2,1,0:T(8,128)(2,1)S(1)} %maximum_select_fusion.25), channel_id=1, source_target_pairs={{0,128},{8,136},{16,144},{24,152},{32,160},{40,168},{48,176},{56,1... | collective-permute-start | bytes 49160 | tf_op jit(solution)/shard_map/ppermute | solution.py:51
  299.1 6.7 %collective-permute-start.59 = (bf16[4,32,128]{2,1,0:T(8,128)(2,1)S(1)}, bf16[4,32,128]{2,1,0:T(8,128)(2,1)S(1)}, u32[]{:S(2)}, u32[]{:S(2)}) collective-permute-start(bf16[4,32,128]{2,1,0:T(8,128)(2,1)S(1)} %maximum_select_fusion.23), channel_id=1, source_target_pairs={{0,64},{8,72},{16,80},{24,88},{32,96},{40,104},{48,112},{56,120},{... | collective-permute-start | bytes 98312 | tf_op jit(solution)/shard_map/ppermute | solution.py:51
  305.8 6.2 %collective-permute-start.60 = (bf16[8,32,128]{2,1,0:T(8,128)(2,1)S(1)}, bf16[8,32,128]{2,1,0:T(8,128)(2,1)S(1)}, u32[]{:S(2)}, u32[]{:S(2)}) collective-permute-start(bf16[8,32,128]{2,1,0:T(8,128)(2,1)S(1)} %maximum_select_fusion.21), channel_id=1, source_target_pairs={{0,32},{8,40},{16,48},{24,56},{32,0},{40,8},{48,16},{56,24},{64,96... | collective-permute-start | bytes 196616 | tf_op jit(solution)/shard_map/ppermute | solution.py:51
  312.0 8.4 %collective-permute-start.61 = (bf16[16,32,128]{2,1,0:T(8,128)(2,1)S(1)}, bf16[16,32,128]{2,1,0:T(8,128)(2,1)S(1)}, u32[]{:S(2)}, u32[]{:S(2)}) collective-permute-start(bf16[16,32,128]{2,1,0:T(8,128)(2,1)S(1)} %maximum_select_fusion.19), channel_id=1, source_target_pairs={{0,16},{8,24},{16,0},{24,8},{32,48},{40,56},{48,32},{56,40},{64,80... | collective-permute-start | bytes 393224 | tf_op jit(solution)/shard_map/ppermute | solution.py:51
  320.4 8.3 %collective-permute-start.62 = (bf16[32,32,128]{2,1,0:T(8,128)(2,1)S(1)}, bf16[32,32,128]{2,1,0:T(8,128)(2,1)S(1)}, u32[]{:S(2)}, u32[]{:S(2)}) collective-permute-start(bf16[32,32,128]{2,1,0:T(8,128)(2,1)S(1)} %maximum_select_fusion.17), channel_id=1, source_target_pairs={{0,8},{8,0},{16,24},{24,16},{32,40},{40,32},{48,56},{56,48},{64,72... | collective-permute-start | bytes 786440 | tf_op jit(solution)/shard_map/ppermute | solution.py:51
  329.4 18.2 %collective-permute-start.63 = (bf16[64,32,128]{2,1,0:T(8,128)(2,1)S(1)}, bf16[64,32,128]{2,1,0:T(8,128)(2,1)S(1)}, u32[]{:S(2)}, u32[]{:S(2)}) collective-permute-start(bf16[64,32,128]{2,1,0:T(8,128)(2,1)S(1)} %maximum_select_fusion.14), channel_id=1, source_target_pairs={{0,4},{1,5},{2,6},{3,7},{4,0},{5,1},{6,2},{7,3},{8,12},{9,13},{10,... | collective-permute-start | bytes 1572872 | tf_op jit(solution)/shard_map/ppermute | solution.py:51
  348.6 16.7 %collective-permute-start.64 = (bf16[128,32,128]{2,1,0:T(8,128)(2,1)S(1)}, bf16[128,32,128]{2,1,0:T(8,128)(2,1)S(1)}, u32[]{:S(2)}, u32[]{:S(2)}) collective-permute-start(bf16[128,32,128]{2,1,0:T(8,128)(2,1)S(1)} %maximum_select_fusion.10), channel_id=1, source_target_pairs={{0,2},{1,3},{2,0},{3,1},{4,6},{5,7},{6,4},{7,5},{8,10},{9,11},{10,... | collective-permute-start | bytes 3145736 | tf_op jit(solution)/shard_map/ppermute | solution.py:51
  365.6 15.2 %collective-permute-start.65 = (bf16[256,32,128]{2,1,0:T(8,128)(2,1)S(1)}, bf16[256,32,128]{2,1,0:T(8,128)(2,1)S(1)}, u32[]{:S(2)}, u32[]{:S(2)}) collective-permute-start(bf16[256,32,128]{2,1,0:T(8,128)(2,1)S(1)} %maximum_select_fusion.6), channel_id=1, source_target_pairs={{0,1},{1,0},{2,3},{3,2},{4,5},{5,4},{6,7},{7,6},{8,9},{9,8},{10,11... | collective-permute-start | bytes 6291464 | tf_op jit(solution)/shard_map/ppermute | solution.py:51
  367.7 9.0 %collective-permute-start.53 = (f32[128,128]{1,0:T(8,128)S(1)}, f32[128,128]{1,0:T(8,128)S(1)}, u32[]{:S(2)}, u32[]{:S(2)}) collective-permute-start(f32[128,128]{1,0:T(8,128)S(1)} %get-tuple-element.60), channel_id=1, source_target_pairs={{0,8},{8,16},{16,24},{24,32},{32,40},{40,48},{48,56},{56,64},{64,7... | collective-permute-start | bytes 196616 | tf_op jit(solution)/shard_map/ppermute | solution.py:15
  369.9 6.9 %collective-permute-start.55 = (f32[128,128]{1,0:T(8,128)S(1)}, f32[128,128]{1,0:T(8,128)S(1)}, u32[]{:S(2)}, u32[]{:S(2)}) collective-permute-start(f32[128,128]{1,0:T(8,128)S(1)} %get-tuple-element.61), channel_id=1, source_target_pairs={{0,1},{1,2},{2,3},{3,4},{4,5},{5,6},{6,7},{8,9},{9,10},{10,11},{11... | collective-permute-start | bytes 196616 | tf_op jit(solution)/shard_map/ppermute | solution.py:15
  372.0 6.2 %collective-permute-start.54 = (f32[128,128]{1,0:T(8,128)S(1)}, f32[128,128]{1,0:T(8,128)S(1)}, u32[]{:S(2)}, u32[]{:S(2)}) collective-permute-start(f32[128,128]{1,0:T(8,128)S(1)} %get-tuple-element.62), channel_id=1, source_target_pairs={{8,0},{16,8},{24,16},{32,24},{40,32},{48,40},{56,48},{64,56},{72,6... | collective-permute-start | bytes 196616 | tf_op jit(solution)/shard_map/ppermute | solution.py:15
  398.7 11.4 %collective-permute-start.66 = (bf16[128,128]{1,0:T(8,128)(2,1)S(1)}, bf16[128,128]{1,0:T(8,128)(2,1)S(1)}, u32[]{:S(2)}, u32[]{:S(2)}) collective-permute-start(bf16[128,128]{1,0:T(8,128)(2,1)S(1)} %get-tuple-element.68), channel_id=1, source_target_pairs={{0,8},{8,16},{16,24},{24,32},{32,40},{40,48},{48,56},{56,64},{64,7... | collective-permute-start | bytes 98312 | tf_op jit(solution)/shard_map/ppermute | solution.py:15
  402.9 7.1 %collective-permute-start.68 = (bf16[128,128]{1,0:T(8,128)(2,1)S(1)}, bf16[128,128]{1,0:T(8,128)(2,1)S(1)}, u32[]{:S(2)}, u32[]{:S(2)}) collective-permute-start(bf16[128,128]{1,0:T(8,128)(2,1)S(1)} %get-tuple-element.69), channel_id=1, source_target_pairs={{0,1},{1,2},{2,3},{3,4},{4,5},{5,6},{6,7},{8,9},{9,10},{10,11},{11... | collective-permute-start | bytes 98312 | tf_op jit(solution)/shard_map/ppermute | solution.py:15
  423.0 7.1 %collective-permute-start.72 = (f32[6,128]{1,0:T(8,128)S(1)}, f32[6,128]{1,0:T(8,128)S(1)}, u32[]{:S(2)}, u32[]{:S(2)}) collective-permute-start(f32[6,128]{1,0:T(8,128)S(1)} %add.307), channel_id=1, source_target_pairs={{0,4},{1,5},{2,6},{3,7},{4,0},{5,1},{6,2},{7,3},{8,12},{9,13},{10,... | collective-permute-start | bytes 9224 | tf_op jit(solution)/shard_map/ppermute | solution.py:32
  430.1 5.8 %collective-permute-start.73 = (f32[6,128]{1,0:T(8,128)S(1)}, f32[6,128]{1,0:T(8,128)S(1)}, u32[]{:S(2)}, u32[]{:S(2)}) collective-permute-start(f32[6,128]{1,0:T(8,128)S(1)} %add.308), channel_id=1, source_target_pairs={{0,8},{8,0},{16,24},{24,16},{32,40},{40,32},{48,56},{56,48},{64,72... | collective-permute-start | bytes 9224 | tf_op jit(solution)/shard_map/ppermute | solution.py:32
  435.9 9.1 %collective-permute-start.74 = (f32[6,128]{1,0:T(8,128)S(1)}, f32[6,128]{1,0:T(8,128)S(1)}, u32[]{:S(2)}, u32[]{:S(2)}) collective-permute-start(f32[6,128]{1,0:T(8,128)S(1)} %add.309), channel_id=1, source_target_pairs={{0,16},{8,24},{16,0},{24,8},{32,48},{40,56},{48,32},{56,40},{64,80... | collective-permute-start | bytes 9224 | tf_op jit(solution)/shard_map/ppermute | solution.py:32
  445.0 7.9 %collective-permute-start.75 = (f32[6,128]{1,0:T(8,128)S(1)}, f32[6,128]{1,0:T(8,128)S(1)}, u32[]{:S(2)}, u32[]{:S(2)}) collective-permute-start(f32[6,128]{1,0:T(8,128)S(1)} %add.310), channel_id=1, source_target_pairs={{0,32},{8,40},{16,48},{24,56},{32,0},{40,8},{48,16},{56,24},{64,96... | collective-permute-start | bytes 9224 | tf_op jit(solution)/shard_map/ppermute | solution.py:32
  452.8 6.9 %collective-permute-start.76 = (f32[6,128]{1,0:T(8,128)S(1)}, f32[6,128]{1,0:T(8,128)S(1)}, u32[]{:S(2)}, u32[]{:S(2)}) collective-permute-start(f32[6,128]{1,0:T(8,128)S(1)} %add.311), channel_id=1, source_target_pairs={{0,64},{8,72},{16,80},{24,88},{32,96},{40,104},{48,112},{56,120},{... | collective-permute-start | bytes 9224 | tf_op jit(solution)/shard_map/ppermute | solution.py:32
  459.7 11.7 %collective-permute-start.77 = (f32[6,128]{1,0:T(8,128)S(1)}, f32[6,128]{1,0:T(8,128)S(1)}, u32[]{:S(2)}, u32[]{:S(2)}) collective-permute-start(f32[6,128]{1,0:T(8,128)S(1)} %add.312), channel_id=1, source_target_pairs={{0,128},{8,136},{16,144},{24,152},{32,160},{40,168},{48,176},{56,1... | collective-permute-start | bytes 9224 | tf_op jit(solution)/shard_map/ppermute | solution.py:32
  471.4 15.4 %collective-permute-start.78 = (f32[6,128]{1,0:T(8,128)S(1)}, f32[6,128]{1,0:T(8,128)S(1)}, u32[]{:S(2)}, u32[]{:S(2)}) collective-permute-start(f32[6,128]{1,0:T(8,128)S(1)} %add.313), channel_id=1, source_target_pairs={{0,256},{8,264},{16,272},{24,280},{32,288},{40,296},{48,304},{56,3... | collective-permute-start | bytes 9224 | tf_op jit(solution)/shard_map/ppermute | solution.py:32
  (59 other events, 1285.3 us)

commit v5 on v4

--- a/solution.py
+++ b/solution.py
@@ -121,9 +121,9 @@
         residual = lax.dot_general(
             basis, rounded, (((0,), (0,)), ((), ())), preferred_element_type=jnp.float32
         ).astype(jnp.bfloat16)
-        gathered = coarse_gather(residual).reshape(selection.shape[0], -1)
-        placed = lax.dot_general(
-            selection, gathered, (((0,), (0,)), ((), ())), preferred_element_type=jnp.float32
+        gathered = coarse_gather(residual).reshape(selection.shape[0], basis_count, system_count)
+        placed = jnp.einsum(
+            "bq,bck->qck", selection, gathered, preferred_element_type=jnp.float32
         ).astype(jnp.bfloat16)
         solved = jnp.dot(
             coarse_rows, placed.reshape(-1, system_count), preferred_element_type=jnp.float32

time: 494 us -> 502 us (1.016)
  waiting for transfers between devices: 138 us -> 155 us
  local copies, waits for them, and re-layouts: 33.5 us -> 23.1 us
  other arithmetic: 13.9 us -> 19.1 us
    ppermute x18, waiting for transfers between devices: 83.4 us -> 99.1 us  [doubling_gather(): got = lax.ppermute(held, axis, [(i, i ^ step) for i in range(count)])]
    reshape x2 -> x0, local copies, waits for them, and re-layouts: 14.8 us -> none  [precondition(): placed.reshape(-1, system_count)]
    convert_element_type x0 -> x2, local copies, waits for them, and re-layouts: none -> 9.35 us  [precondition(): placed = jnp.einsum('bq,bck->qck', selection, gathered, preferred_element...]
    unnamed x103 -> x51, local copies, waits for them, and re-layouts: 8.77 us -> 1.45 us
  transfers between devices with their start and end apart: 61 -> 61, of which waited for: 49 -> 49; matrix products, arithmetic and copies ran while one was open for 2% -> 3% of each run, Pallas kernels for 0% -> 0%
where the time goes in v5:
time: 502 us; the launch traced here: 497 us
  starting transfers between devices  280 us (56%)
  waiting for transfers between devices  155 us (31%)
  local copies, waits for them, and re-layouts  23.1 us (5%)
  other arithmetic  19.1 us (4%)
  matrix products  16.5 us (3%)
    ppermute x27, starting transfers between devices, allsum(): lax.ppermute(value, axis, [(i, i ^ step) for i in range(count)])  157 us
    ppermute x18, waiting for transfers between devices, doubling_gather(): got = lax.ppermute(held, axis, [(i, i ^ step) for i in range(count)])  99.1 us
    ppermute x18, starting transfers between devices, doubling_gather(): got = lax.ppermute(held, axis, [(i, i ^ step) for i in range(count)])  81.1 us
    ppermute x27, waiting for transfers between devices, allsum(): lax.ppermute(value, axis, [(i, i ^ step) for i in range(count)])  51.5 us
    ppermute x16, starting transfers between devices, neighbours(): return (lax.ppermute(rows[1], axis, up), lax.ppermute(rows[0], axis, down))  41.7 us
  transfers between devices with their start and end apart: 61, of which 49 were waited for; matrix products, arithmetic and copies ran while one was open for 3% of the time, Pallas kernels for 0%

profile of v5, /device:TPU:6, one launch (start us, length us, event | category | flops | bytes accessed | tf_op | source)
XLA Modules:
  0.0 497.2 jit_solution(3513868006969045951)
XLA Ops:
  10.1 7.2 %collective-permute-start.20 = (f32[128]{0:T(128)S(1)}, f32[128]{0:T(128)S(1)}, u32[]{:S(2)}, u32[]{:S(2)}) collective-permute-start(f32[128]{0:T(128)S(1)} %add.270), channel_id=1, source_target_pairs={{0,4},{1,5},{2,6},{3,7},{4,0},{5,1},{6,2},{7,3},{8,12},{9,13},{10,... | collective-permute-start | bytes 1544 | tf_op jit(solution)/shard_map/ppermute | solution.py:32
  20.7 3.5 collective-permute-done.21
  27.6 3.6 collective-permute-done.22
  43.0 7.7 %collective-permute-start.25 = (f32[128]{0:T(128)S(1)}, f32[128]{0:T(128)S(1)}, u32[]{:S(2)}, u32[]{:S(2)}) collective-permute-start(f32[128]{0:T(128)S(1)} %add.275), channel_id=1, source_target_pairs={{0,128},{8,136},{16,144},{24,152},{32,160},{40,168},{48,176},{56,1... | collective-permute-start | bytes 1544 | tf_op jit(solution)/shard_map/ppermute | solution.py:32
  52.4 14.0 %collective-permute-start.26 = (f32[128]{0:T(128)S(1)}, f32[128]{0:T(128)S(1)}, u32[]{:S(2)}, u32[]{:S(2)}) collective-permute-start(f32[128]{0:T(128)S(1)} %add.276), channel_id=1, source_target_pairs={{0,256},{8,264},{16,272},{24,280},{32,288},{40,296},{48,304},{56,3... | collective-permute-start | bytes 1544 | tf_op jit(solution)/shard_map/ppermute | solution.py:32
  68.9 12.6 %collective-permute-start.31 = (bf16[1,32,128]{2,1,0:T(8,128)(2,1)S(1)}, bf16[1,32,128]{2,1,0:T(8,128)(2,1)S(1)}, u32[]{:S(2)}, u32[]{:S(2)}) collective-permute-start(bf16[1,32,128]{2,1,0:T(8,128)(2,1)S(1)} %fusion.12), channel_id=1, source_target_pairs={{0,256},{8,264},{16,272},{24,280},{32,288},{40,296},{48,304},{56,3... | collective-permute-start | bytes 24584 | tf_op jit(solution)/shard_map/ppermute | solution.py:51
  83.2 6.4 %collective-permute-start.32 = (bf16[2,32,128]{2,1,0:T(8,128)(2,1)S(1)}, bf16[2,32,128]{2,1,0:T(8,128)(2,1)S(1)}, u32[]{:S(2)}, u32[]{:S(2)}) collective-permute-start(bf16[2,32,128]{2,1,0:T(8,128)(2,1)S(1)} %maximum_select_fusion.16), channel_id=1, source_target_pairs={{0,128},{8,136},{16,144},{24,152},{32,160},{40,168},{48,176},{56,1... | collective-permute-start | bytes 49160 | tf_op jit(solution)/shard_map/ppermute | solution.py:51
  105.9 5.1 %collective-permute-start.35 = (bf16[16,32,128]{2,1,0:T(8,128)(2,1)S(1)}, bf16[16,32,128]{2,1,0:T(8,128)(2,1)S(1)}, u32[]{:S(2)}, u32[]{:S(2)}) collective-permute-start(bf16[16,32,128]{2,1,0:T(8,128)(2,1)S(1)} %maximum_select_fusion.10), channel_id=1, source_target_pairs={{0,16},{8,24},{16,0},{24,8},{32,48},{40,56},{48,32},{56,40},{64,80... | collective-permute-start | bytes 393224 | tf_op jit(solution)/shard_map/ppermute | solution.py:51
  114.3 3.5 collective-permute-start.36
  117.8 4.8 collective-permute-done.36
  122.6 4.1 collective-permute-start.37
  126.8 14.0 %collective-permute-done.37 = bf16[64,32,128]{2,1,0:T(8,128)(2,1)S(1)} collective-permute-done((bf16[64,32,128]{2,1,0:T(8,128)(2,1)S(1)}, bf16[64,32,128]{2,1,0:T(8,128)(2,1)S(1)}, u32[]{:S(2)}, u32[]{:S(2)}) %collective-permute-start.37) | collective-permute-done | bytes 524320 | tf_op jit(solution)/shard_map/ppermute | solution.py:51
  143.8 14.0 %collective-permute-done.38 = bf16[128,32,128]{2,1,0:T(8,128)(2,1)} collective-permute-done((bf16[128,32,128]{2,1,0:T(8,128)(2,1)S(1)}, bf16[128,32,128]{2,1,0:T(8,128)(2,1)}, u32[]{:S(2)}, u32[]{:S(2)}) %collective-permute-start.38) | collective-permute-done | bytes 1048608 | tf_op jit(solution)/shard_map/ppermute | solution.py:51
  175.9 3.5 gather_fusion.1
  187.6 4.7 copy.18
  192.3 3.6 convolution_add_fusion.1
  197.4 4.3 collective-permute-start.40
  204.9 3.8 collective-permute-start.43
  215.9 3.7 collective-permute-start.45
  221.4 4.0 collective-permute-start.46
  228.4 4.3 collective-permute-start.47
  234.2 6.5 %collective-permute-start.48 = (f32[3,128]{1,0:T(4,128)S(1)}, f32[3,128]{1,0:T(4,128)S(1)}, u32[]{:S(2)}, u32[]{:S(2)}) collective-permute-start(f32[3,128]{1,0:T(4,128)S(1)} %add.296), channel_id=1, source_target_pairs={{0,16},{8,24},{16,0},{24,8},{32,48},{40,56},{48,32},{56,40},{64,80... | collective-permute-start | bytes 4616 | tf_op jit(solution)/shard_map/ppermute | solution.py:32
  242.3 6.4 %collective-permute-start.49 = (f32[3,128]{1,0:T(4,128)S(1)}, f32[3,128]{1,0:T(4,128)S(1)}, u32[]{:S(2)}, u32[]{:S(2)}) collective-permute-start(f32[3,128]{1,0:T(4,128)S(1)} %add.297), channel_id=1, source_target_pairs={{0,32},{8,40},{16,48},{24,56},{32,0},{40,8},{48,16},{56,24},{64,96... | collective-permute-start | bytes 4616 | tf_op jit(solution)/shard_map/ppermute | solution.py:32
  250.2 4.5 collective-permute-start.50
  256.6 9.5 %collective-permute-start.51 = (f32[3,128]{1,0:T(4,128)S(1)}, f32[3,128]{1,0:T(4,128)S(1)}, u32[]{:S(2)}, u32[]{:S(2)}) collective-permute-start(f32[3,128]{1,0:T(4,128)S(1)} %add.299), channel_id=1, source_target_pairs={{0,128},{8,136},{16,144},{24,152},{32,160},{40,168},{48,176},{56,1... | collective-permute-start | bytes 4616 | tf_op jit(solution)/shard_map/ppermute | solution.py:32
  267.6 13.8 %collective-permute-start.52 = (f32[3,128]{1,0:T(4,128)S(1)}, f32[3,128]{1,0:T(4,128)S(1)}, u32[]{:S(2)}, u32[]{:S(2)}) collective-permute-start(f32[3,128]{1,0:T(4,128)S(1)} %add.300), channel_id=1, source_target_pairs={{0,256},{8,264},{16,272},{24,280},{32,288},{40,296},{48,304},{56,3... | collective-permute-start | bytes 4616 | tf_op jit(solution)/shard_map/ppermute | solution.py:32
  285.1 12.6 %collective-permute-start.57 = (bf16[1,32,128]{2,1,0:T(8,128)(2,1)S(1)}, bf16[1,32,128]{2,1,0:T(8,128)(2,1)S(1)}, u32[]{:S(2)}, u32[]{:S(2)}) collective-permute-start(bf16[1,32,128]{2,1,0:T(8,128)(2,1)S(1)} %fusion.13), channel_id=1, source_target_pairs={{0,256},{8,264},{16,272},{24,280},{32,288},{40,296},{48,304},{56,3... | collective-permute-start | bytes 24584 | tf_op jit(solution)/shard_map/ppermute | solution.py:51
  299.3 6.7 %collective-permute-start.58 = (bf16[2,32,128]{2,1,0:T(8,128)(2,1)S(1)}, bf16[2,32,128]{2,1,0:T(8,128)(2,1)S(1)}, u32[]{:S(2)}, u32[]{:S(2)}) collective-permute-start(bf16[2,32,128]{2,1,0:T(8,128)(2,1)S(1)} %maximum_select_fusion.17), channel_id=1, source_target_pairs={{0,128},{8,136},{16,144},{24,152},{32,160},{40,168},{48,176},{56,1... | collective-permute-start | bytes 49160 | tf_op jit(solution)/shard_map/ppermute | solution.py:51
  311.0 4.6 collective-permute-done.59
  317.6 4.2 collective-permute-done.60
  324.4 5.9 %collective-permute-done.61 = bf16[16,32,128]{2,1,0:T(8,128)(2,1)S(1)} collective-permute-done((bf16[16,32,128]{2,1,0:T(8,128)(2,1)S(1)}, bf16[16,32,128]{2,1,0:T(8,128)(2,1)S(1)}, u32[]{:S(2)}, u32[]{:S(2)}) %collective-permute-start.61) | collective-permute-done | bytes 131104 | tf_op jit(solution)/shard_map/ppermute | solution.py:51
  332.4 6.1 %collective-permute-done.62 = bf16[32,32,128]{2,1,0:T(8,128)(2,1)S(1)} collective-permute-done((bf16[32,32,128]{2,1,0:T(8,128)(2,1)S(1)}, bf16[32,32,128]{2,1,0:T(8,128)(2,1)S(1)}, u32[]{:S(2)}, u32[]{:S(2)}) %collective-permute-start.62) | collective-permute-done | bytes 262176 | tf_op jit(solution)/shard_map/ppermute | solution.py:51
  338.6 4.8 collective-permute-start.63
  343.5 13.3 %collective-permute-done.63 = bf16[64,32,128]{2,1,0:T(8,128)(2,1)S(1)} collective-permute-done((bf16[64,32,128]{2,1,0:T(8,128)(2,1)S(1)}, bf16[64,32,128]{2,1,0:T(8,128)(2,1)S(1)}, u32[]{:S(2)}, u32[]{:S(2)}) %collective-permute-start.63) | collective-permute-done | bytes 524320 | tf_op jit(solution)/shard_map/ppermute | solution.py:51
  357.0 3.7 collective-permute-start.64
  360.7 13.0 %collective-permute-done.64 = bf16[128,32,128]{2,1,0:T(8,128)(2,1)S(1)} collective-permute-done((bf16[128,32,128]{2,1,0:T(8,128)(2,1)S(1)}, bf16[128,32,128]{2,1,0:T(8,128)(2,1)S(1)}, u32[]{:S(2)}, u32[]{:S(2)}) %collective-permute-start.64) | collective-permute-done | bytes 1048608 | tf_op jit(solution)/shard_map/ppermute | solution.py:51
  396.7 4.7 copy.21
  401.5 3.6 convolution_add_fusion
  406.6 4.3 collective-permute-start.66
  414.1 3.6 collective-permute-start.69
  425.2 3.7 collective-permute-start.71
  430.7 5.3 %collective-permute-start.72 = (f32[6,128]{1,0:T(8,128)S(1)}, f32[6,128]{1,0:T(8,128)S(1)}, u32[]{:S(2)}, u32[]{:S(2)}) collective-permute-start(f32[6,128]{1,0:T(8,128)S(1)} %add.307), channel_id=1, source_target_pairs={{0,4},{1,5},{2,6},{3,7},{4,0},{5,1},{6,2},{7,3},{8,12},{9,13},{10,... | collective-permute-start | bytes 9224 | tf_op jit(solution)/shard_map/ppermute | solution.py:32
  437.7 4.3 collective-permute-start.73
  443.5 7.3 %collective-permute-start.74 = (f32[6,128]{1,0:T(8,128)S(1)}, f32[6,128]{1,0:T(8,128)S(1)}, u32[]{:S(2)}, u32[]{:S(2)}) collective-permute-start(f32[6,128]{1,0:T(8,128)S(1)} %add.309), channel_id=1, source_target_pairs={{0,16},{8,24},{16,0},{24,8},{32,48},{40,56},{48,32},{56,40},{64,80... | collective-permute-start | bytes 9224 | tf_op jit(solution)/shard_map/ppermute | solution.py:32
  452.4 6.3 %collective-permute-start.75 = (f32[6,128]{1,0:T(8,128)S(1)}, f32[6,128]{1,0:T(8,128)S(1)}, u32[]{:S(2)}, u32[]{:S(2)}) collective-permute-start(f32[6,128]{1,0:T(8,128)S(1)} %add.310), channel_id=1, source_target_pairs={{0,32},{8,40},{16,48},{24,56},{32,0},{40,8},{48,16},{56,24},{64,96... | collective-permute-start | bytes 9224 | tf_op jit(solution)/shard_map/ppermute | solution.py:32
  460.2 5.7 %collective-permute-start.76 = (f32[6,128]{1,0:T(8,128)S(1)}, f32[6,128]{1,0:T(8,128)S(1)}, u32[]{:S(2)}, u32[]{:S(2)}) collective-permute-start(f32[6,128]{1,0:T(8,128)S(1)} %add.311), channel_id=1, source_target_pairs={{0,64},{8,72},{16,80},{24,88},{32,96},{40,104},{48,112},{56,120},{... | collective-permute-start | bytes 9224 | tf_op jit(solution)/shard_map/ppermute | solution.py:32
  467.5 10.1 %collective-permute-start.77 = (f32[6,128]{1,0:T(8,128)S(1)}, f32[6,128]{1,0:T(8,128)S(1)}, u32[]{:S(2)}, u32[]{:S(2)}) collective-permute-start(f32[6,128]{1,0:T(8,128)S(1)} %add.312), channel_id=1, source_target_pairs={{0,128},{8,136},{16,144},{24,152},{32,160},{40,168},{48,176},{56,1... | collective-permute-start | bytes 9224 | tf_op jit(solution)/shard_map/ppermute | solution.py:32
  479.1 13.8 %collective-permute-start.78 = (f32[6,128]{1,0:T(8,128)S(1)}, f32[6,128]{1,0:T(8,128)S(1)}, u32[]{:S(2)}, u32[]{:S(2)}) collective-permute-start(f32[6,128]{1,0:T(8,128)S(1)} %add.313), channel_id=1, source_target_pairs={{0,256},{8,264},{16,272},{24,280},{32,288},{40,296},{48,304},{56,3... | collective-permute-start | bytes 9224 | tf_op jit(solution)/shard_map/ppermute | solution.py:32
  (223 shorter events, 173.4 us)
Async XLA Ops:
  10.1 8.7 %collective-permute-start.20 = (f32[128]{0:T(128)S(1)}, f32[128]{0:T(128)S(1)}, u32[]{:S(2)}, u32[]{:S(2)}) collective-permute-start(f32[128]{0:T(128)S(1)} %add.270), channel_id=1, source_target_pairs={{0,4},{1,5},{2,6},{3,7},{4,0},{5,1},{6,2},{7,3},{8,12},{9,13},{10,... | collective-permute-start | bytes 1544 | tf_op jit(solution)/shard_map/ppermute | solution.py:32
  24.3 7.0 %collective-permute-start.22 = (f32[128]{0:T(128)S(1)}, f32[128]{0:T(128)S(1)}, u32[]{:S(2)}, u32[]{:S(2)}) collective-permute-start(f32[128]{0:T(128)S(1)} %add.272), channel_id=1, source_target_pairs={{0,16},{8,24},{16,0},{24,8},{32,48},{40,56},{48,32},{56,40},{64,80... | collective-permute-start | bytes 1544 | tf_op jit(solution)/shard_map/ppermute | solution.py:32
  36.7 6.3 %collective-permute-start.24 = (f32[128]{0:T(128)S(1)}, f32[128]{0:T(128)S(1)}, u32[]{:S(2)}, u32[]{:S(2)}) collective-permute-start(f32[128]{0:T(128)S(1)} %add.274), channel_id=1, source_target_pairs={{0,64},{8,72},{16,80},{24,88},{32,96},{40,104},{48,112},{56,120},{... | collective-permute-start | bytes 1544 | tf_op jit(solution)/shard_map/ppermute | solution.py:32
  43.0 9.4 %collective-permute-start.25 = (f32[128]{0:T(128)S(1)}, f32[128]{0:T(128)S(1)}, u32[]{:S(2)}, u32[]{:S(2)}) collective-permute-start(f32[128]{0:T(128)S(1)} %add.275), channel_id=1, source_target_pairs={{0,128},{8,136},{16,144},{24,152},{32,160},{40,168},{48,176},{56,1... | collective-permute-start | bytes 1544 | tf_op jit(solution)/shard_map/ppermute | solution.py:32
  52.4 15.5 %collective-permute-start.26 = (f32[128]{0:T(128)S(1)}, f32[128]{0:T(128)S(1)}, u32[]{:S(2)}, u32[]{:S(2)}) collective-permute-start(f32[128]{0:T(128)S(1)} %add.276), channel_id=1, source_target_pairs={{0,256},{8,264},{16,272},{24,280},{32,288},{40,296},{48,304},{56,3... | collective-permute-start | bytes 1544 | tf_op jit(solution)/shard_map/ppermute | solution.py:32
  68.9 14.3 %collective-permute-start.31 = (bf16[1,32,128]{2,1,0:T(8,128)(2,1)S(1)}, bf16[1,32,128]{2,1,0:T(8,128)(2,1)S(1)}, u32[]{:S(2)}, u32[]{:S(2)}) collective-permute-start(bf16[1,32,128]{2,1,0:T(8,128)(2,1)S(1)} %fusion.12), channel_id=1, source_target_pairs={{0,256},{8,264},{16,272},{24,280},{32,288},{40,296},{48,304},{56,3... | collective-permute-start | bytes 24584 | tf_op jit(solution)/shard_map/ppermute | solution.py:51
  83.2 9.6 %collective-permute-start.32 = (bf16[2,32,128]{2,1,0:T(8,128)(2,1)S(1)}, bf16[2,32,128]{2,1,0:T(8,128)(2,1)S(1)}, u32[]{:S(2)}, u32[]{:S(2)}) collective-permute-start(bf16[2,32,128]{2,1,0:T(8,128)(2,1)S(1)} %maximum_select_fusion.16), channel_id=1, source_target_pairs={{0,128},{8,136},{16,144},{24,152},{32,160},{40,168},{48,176},{56,1... | collective-permute-start | bytes 49160 | tf_op jit(solution)/shard_map/ppermute | solution.py:51
  92.8 6.7 %collective-permute-start.33 = (bf16[4,32,128]{2,1,0:T(8,128)(2,1)S(1)}, bf16[4,32,128]{2,1,0:T(8,128)(2,1)S(1)}, u32[]{:S(2)}, u32[]{:S(2)}) collective-permute-start(bf16[4,32,128]{2,1,0:T(8,128)(2,1)S(1)} %maximum_select_fusion.14), channel_id=1, source_target_pairs={{0,64},{8,72},{16,80},{24,88},{32,96},{40,104},{48,112},{56,120},{... | collective-permute-start | bytes 98312 | tf_op jit(solution)/shard_map/ppermute | solution.py:51
  99.6 6.3 %collective-permute-start.34 = (bf16[8,32,128]{2,1,0:T(8,128)(2,1)S(1)}, bf16[8,32,128]{2,1,0:T(8,128)(2,1)S(1)}, u32[]{:S(2)}, u32[]{:S(2)}) collective-permute-start(bf16[8,32,128]{2,1,0:T(8,128)(2,1)S(1)} %maximum_select_fusion.12), channel_id=1, source_target_pairs={{0,32},{8,40},{16,48},{24,56},{32,0},{40,8},{48,16},{56,24},{64,96... | collective-permute-start | bytes 196616 | tf_op jit(solution)/shard_map/ppermute | solution.py:51
  105.9 8.4 %collective-permute-start.35 = (bf16[16,32,128]{2,1,0:T(8,128)(2,1)S(1)}, bf16[16,32,128]{2,1,0:T(8,128)(2,1)S(1)}, u32[]{:S(2)}, u32[]{:S(2)}) collective-permute-start(bf16[16,32,128]{2,1,0:T(8,128)(2,1)S(1)} %maximum_select_fusion.10), channel_id=1, source_target_pairs={{0,16},{8,24},{16,0},{24,8},{32,48},{40,56},{48,32},{56,40},{64,80... | collective-permute-start | bytes 393224 | tf_op jit(solution)/shard_map/ppermute | solution.py:51
  114.3 8.3 %collective-permute-start.36 = (bf16[32,32,128]{2,1,0:T(8,128)(2,1)S(1)}, bf16[32,32,128]{2,1,0:T(8,128)(2,1)S(1)}, u32[]{:S(2)}, u32[]{:S(2)}) collective-permute-start(bf16[32,32,128]{2,1,0:T(8,128)(2,1)S(1)} %maximum_select_fusion.8), channel_id=1, source_target_pairs={{0,8},{8,0},{16,24},{24,16},{32,40},{40,32},{48,56},{56,48},{64,72... | collective-permute-start | bytes 786440 | tf_op jit(solution)/shard_map/ppermute | solution.py:51
  122.6 18.2 %collective-permute-start.37 = (bf16[64,32,128]{2,1,0:T(8,128)(2,1)S(1)}, bf16[64,32,128]{2,1,0:T(8,128)(2,1)S(1)}, u32[]{:S(2)}, u32[]{:S(2)}) collective-permute-start(bf16[64,32,128]{2,1,0:T(8,128)(2,1)S(1)} %maximum_select_fusion.6), channel_id=1, source_target_pairs={{0,4},{1,5},{2,6},{3,7},{4,0},{5,1},{6,2},{7,3},{8,12},{9,13},{10,... | collective-permute-start | bytes 1572872 | tf_op jit(solution)/shard_map/ppermute | solution.py:51
  141.0 16.8 %collective-permute-start.38 = (bf16[128,32,128]{2,1,0:T(8,128)(2,1)S(1)}, bf16[128,32,128]{2,1,0:T(8,128)(2,1)}, u32[]{:S(2)}, u32[]{:S(2)}) collective-permute-start(bf16[128,32,128]{2,1,0:T(8,128)(2,1)S(1)} %maximum_select_fusion.4), channel_id=1, source_target_pairs={{0,2},{1,3},{2,0},{3,1},{4,6},{5,7},{6,4},{7,5},{8,10},{9,11},{10,... | collective-permute-start | bytes 3145736 | tf_op jit(solution)/shard_map/ppermute | solution.py:51
  160.3 21.9 %collective-permute-start.39 = (bf16[256,32,128]{2,1,0:T(8,128)(2,1)S(1)}, bf16[256,32,128]{2,1,0:T(8,128)(2,1)}, u32[]{:S(2)}, u32[]{:S(2)}) collective-permute-start(bf16[256,32,128]{2,1,0:T(8,128)(2,1)S(1)} %maximum_select_fusion.2), channel_id=1, source_target_pairs={{0,1},{1,0},{2,3},{3,2},{4,5},{5,4},{6,7},{7,6},{8,9},{9,8},{10,11... | collective-permute-start | bytes 6291464 | tf_op jit(solution)/shard_map/ppermute | solution.py:51
  165.5 13.9 %collective-permute-start.27 = (f32[128,128]{1,0:T(8,128)}, f32[128,128]{1,0:T(8,128)S(1)}, u32[]{:S(2)}, u32[]{:S(2)}) collective-permute-start(f32[128,128]{1,0:T(8,128)} %get-tuple-element.64), channel_id=1, source_target_pairs={{0,8},{8,16},{16,24},{24,32},{32,40},{40,48},{48,56},{56,64},{64,7... | collective-permute-start | bytes 196616 | tf_op jit(solution)/shard_map/ppermute | solution.py:15
  169.0 10.5 %collective-permute-start.29 = (f32[128,128]{1,0:T(8,128)}, f32[128,128]{1,0:T(8,128)S(1)}, u32[]{:S(2)}, u32[]{:S(2)}) collective-permute-start(f32[128,128]{1,0:T(8,128)} %get-tuple-element.65), channel_id=1, source_target_pairs={{0,1},{1,2},{2,3},{3,4},{4,5},{5,6},{6,7},{8,9},{9,10},{10,11},{11... | collective-permute-start | bytes 196616 | tf_op jit(solution)/shard_map/ppermute | solution.py:15
  171.1 8.4 %collective-permute-start.28 = (f32[128,128]{1,0:T(8,128)S(1)}, f32[128,128]{1,0:T(8,128)}, u32[]{:S(2)}, u32[]{:S(2)}) collective-permute-start(f32[128,128]{1,0:T(8,128)S(1)} %get-tuple-element.66), channel_id=1, source_target_pairs={{8,0},{16,8},{24,16},{32,24},{40,32},{48,40},{56,48},{64,56},{72,6... | collective-permute-start | bytes 196616 | tf_op jit(solution)/shard_map/ppermute | solution.py:15
  172.4 7.1 %collective-permute-start.30 = (f32[128,128]{1,0:T(8,128)S(1)}, f32[128,128]{1,0:T(8,128)}, u32[]{:S(2)}, u32[]{:S(2)}) collective-permute-start(f32[128,128]{1,0:T(8,128)S(1)} %get-tuple-element.67), channel_id=1, source_target_pairs={{1,0},{2,1},{3,2},{4,3},{5,4},{6,5},{7,6},{9,8},{10,9},{11,10},{12... | collective-permute-start | bytes 196616 | tf_op jit(solution)/shard_map/ppermute | solution.py:15
  197.4 11.4 %collective-permute-start.40 = (bf16[128,128]{1,0:T(8,128)(2,1)S(1)}, bf16[128,128]{1,0:T(8,128)(2,1)S(1)}, u32[]{:S(2)}, u32[]{:S(2)}) collective-permute-start(bf16[128,128]{1,0:T(8,128)(2,1)S(1)} %get-tuple-element.72), channel_id=1, source_target_pairs={{0,8},{8,16},{16,24},{24,32},{32,40},{40,48},{48,56},{56,64},{64,7... | collective-permute-start | bytes 98312 | tf_op jit(solution)/shard_map/ppermute | solution.py:15
  201.7 7.1 %collective-permute-start.42 = (bf16[128,128]{1,0:T(8,128)(2,1)S(1)}, bf16[128,128]{1,0:T(8,128)(2,1)S(1)}, u32[]{:S(2)}, u32[]{:S(2)}) collective-permute-start(bf16[128,128]{1,0:T(8,128)(2,1)S(1)} %get-tuple-element.73), channel_id=1, source_target_pairs={{0,1},{1,2},{2,3},{3,4},{4,5},{5,6},{6,7},{8,9},{9,10},{10,11},{11... | collective-permute-start | bytes 98312 | tf_op jit(solution)/shard_map/ppermute | solution.py:15
  221.4 7.0 %collective-permute-start.46 = (f32[3,128]{1,0:T(4,128)S(1)}, f32[3,128]{1,0:T(4,128)S(1)}, u32[]{:S(2)}, u32[]{:S(2)}) collective-permute-start(f32[3,128]{1,0:T(4,128)S(1)} %fusion.78), channel_id=1, source_target_pairs={{0,4},{1,5},{2,6},{3,7},{4,0},{5,1},{6,2},{7,3},{8,12},{9,13},{10,... | collective-permute-start | bytes 4616 | tf_op jit(solution)/shard_map/ppermute | solution.py:32
  228.4 5.8 %collective-permute-start.47 = (f32[3,128]{1,0:T(4,128)S(1)}, f32[3,128]{1,0:T(4,128)S(1)}, u32[]{:S(2)}, u32[]{:S(2)}) collective-permute-start(f32[3,128]{1,0:T(4,128)S(1)} %add.295), channel_id=1, source_target_pairs={{0,8},{8,0},{16,24},{24,16},{32,40},{40,32},{48,56},{56,48},{64,72... | collective-permute-start | bytes 4616 | tf_op jit(solution)/shard_map/ppermute | solution.py:32
  234.2 8.1 %collective-permute-start.48 = (f32[3,128]{1,0:T(4,128)S(1)}, f32[3,128]{1,0:T(4,128)S(1)}, u32[]{:S(2)}, u32[]{:S(2)}) collective-permute-start(f32[3,128]{1,0:T(4,128)S(1)} %add.296), channel_id=1, source_target_pairs={{0,16},{8,24},{16,0},{24,8},{32,48},{40,56},{48,32},{56,40},{64,80... | collective-permute-start | bytes 4616 | tf_op jit(solution)/shard_map/ppermute | solution.py:32
  242.3 7.9 %collective-permute-start.49 = (f32[3,128]{1,0:T(4,128)S(1)}, f32[3,128]{1,0:T(4,128)S(1)}, u32[]{:S(2)}, u32[]{:S(2)}) collective-permute-start(f32[3,128]{1,0:T(4,128)S(1)} %add.297), channel_id=1, source_target_pairs={{0,32},{8,40},{16,48},{24,56},{32,0},{40,8},{48,16},{56,24},{64,96... | collective-permute-start | bytes 4616 | tf_op jit(solution)/shard_map/ppermute | solution.py:32
  250.2 6.4 %collective-permute-start.50 = (f32[3,128]{1,0:T(4,128)S(1)}, f32[3,128]{1,0:T(4,128)S(1)}, u32[]{:S(2)}, u32[]{:S(2)}) collective-permute-start(f32[3,128]{1,0:T(4,128)S(1)} %add.298), channel_id=1, source_target_pairs={{0,64},{8,72},{16,80},{24,88},{32,96},{40,104},{48,112},{56,120},{... | collective-permute-start | bytes 4616 | tf_op jit(solution)/shard_map/ppermute | solution.py:32
  256.6 11.0 %collective-permute-start.51 = (f32[3,128]{1,0:T(4,128)S(1)}, f32[3,128]{1,0:T(4,128)S(1)}, u32[]{:S(2)}, u32[]{:S(2)}) collective-permute-start(f32[3,128]{1,0:T(4,128)S(1)} %add.299), channel_id=1, source_target_pairs={{0,128},{8,136},{16,144},{24,152},{32,160},{40,168},{48,176},{56,1... | collective-permute-start | bytes 4616 | tf_op jit(solution)/shard_map/ppermute | solution.py:32
  267.6 15.3 %collective-permute-start.52 = (f32[3,128]{1,0:T(4,128)S(1)}, f32[3,128]{1,0:T(4,128)S(1)}, u32[]{:S(2)}, u32[]{:S(2)}) collective-permute-start(f32[3,128]{1,0:T(4,128)S(1)} %add.300), channel_id=1, source_target_pairs={{0,256},{8,264},{16,272},{24,280},{32,288},{40,296},{48,304},{56,3... | collective-permute-start | bytes 4616 | tf_op jit(solution)/shard_map/ppermute | solution.py:32
  285.1 14.3 %collective-permute-start.57 = (bf16[1,32,128]{2,1,0:T(8,128)(2,1)S(1)}, bf16[1,32,128]{2,1,0:T(8,128)(2,1)S(1)}, u32[]{:S(2)}, u32[]{:S(2)}) collective-permute-start(bf16[1,32,128]{2,1,0:T(8,128)(2,1)S(1)} %fusion.13), channel_id=1, source_target_pairs={{0,256},{8,264},{16,272},{24,280},{32,288},{40,296},{48,304},{56,3... | collective-permute-start | bytes 24584 | tf_op jit(solution)/shard_map/ppermute | solution.py:51
  299.3 9.6 %collective-permute-start.58 = (bf16[2,32,128]{2,1,0:T(8,128)(2,1)S(1)}, bf16[2,32,128]{2,1,0:T(8,128)(2,1)S(1)}, u32[]{:S(2)}, u32[]{:S(2)}) collective-permute-start(bf16[2,32,128]{2,1,0:T(8,128)(2,1)S(1)} %maximum_select_fusion.17), channel_id=1, source_target_pairs={{0,128},{8,136},{16,144},{24,152},{32,160},{40,168},{48,176},{56,1... | collective-permute-start | bytes 49160 | tf_op jit(solution)/shard_map/ppermute | solution.py:51
  309.0 6.7 %collective-permute-start.59 = (bf16[4,32,128]{2,1,0:T(8,128)(2,1)S(1)}, bf16[4,32,128]{2,1,0:T(8,128)(2,1)S(1)}, u32[]{:S(2)}, u32[]{:S(2)}) collective-permute-start(bf16[4,32,128]{2,1,0:T(8,128)(2,1)S(1)} %maximum_select_fusion.15), channel_id=1, source_target_pairs={{0,64},{8,72},{16,80},{24,88},{32,96},{40,104},{48,112},{56,120},{... | collective-permute-start | bytes 98312 | tf_op jit(solution)/shard_map/ppermute | solution.py:51
  315.7 6.2 %collective-permute-start.60 = (bf16[8,32,128]{2,1,0:T(8,128)(2,1)S(1)}, bf16[8,32,128]{2,1,0:T(8,128)(2,1)S(1)}, u32[]{:S(2)}, u32[]{:S(2)}) collective-permute-start(bf16[8,32,128]{2,1,0:T(8,128)(2,1)S(1)} %maximum_select_fusion.13), channel_id=1, source_target_pairs={{0,32},{8,40},{16,48},{24,56},{32,0},{40,8},{48,16},{56,24},{64,96... | collective-permute-start | bytes 196616 | tf_op jit(solution)/shard_map/ppermute | solution.py:51
  321.9 8.4 %collective-permute-start.61 = (bf16[16,32,128]{2,1,0:T(8,128)(2,1)S(1)}, bf16[16,32,128]{2,1,0:T(8,128)(2,1)S(1)}, u32[]{:S(2)}, u32[]{:S(2)}) collective-permute-start(bf16[16,32,128]{2,1,0:T(8,128)(2,1)S(1)} %maximum_select_fusion.11), channel_id=1, source_target_pairs={{0,16},{8,24},{16,0},{24,8},{32,48},{40,56},{48,32},{56,40},{64,80... | collective-permute-start | bytes 393224 | tf_op jit(solution)/shard_map/ppermute | solution.py:51
  330.3 8.3 %collective-permute-start.62 = (bf16[32,32,128]{2,1,0:T(8,128)(2,1)S(1)}, bf16[32,32,128]{2,1,0:T(8,128)(2,1)S(1)}, u32[]{:S(2)}, u32[]{:S(2)}) collective-permute-start(bf16[32,32,128]{2,1,0:T(8,128)(2,1)S(1)} %maximum_select_fusion.9), channel_id=1, source_target_pairs={{0,8},{8,0},{16,24},{24,16},{32,40},{40,32},{48,56},{56,48},{64,72... | collective-permute-start | bytes 786440 | tf_op jit(solution)/shard_map/ppermute | solution.py:51
  338.6 18.2 %collective-permute-start.63 = (bf16[64,32,128]{2,1,0:T(8,128)(2,1)S(1)}, bf16[64,32,128]{2,1,0:T(8,128)(2,1)S(1)}, u32[]{:S(2)}, u32[]{:S(2)}) collective-permute-start(bf16[64,32,128]{2,1,0:T(8,128)(2,1)S(1)} %maximum_select_fusion.7), channel_id=1, source_target_pairs={{0,4},{1,5},{2,6},{3,7},{4,0},{5,1},{6,2},{7,3},{8,12},{9,13},{10,... | collective-permute-start | bytes 1572872 | tf_op jit(solution)/shard_map/ppermute | solution.py:51
  357.0 16.7 %collective-permute-start.64 = (bf16[128,32,128]{2,1,0:T(8,128)(2,1)S(1)}, bf16[128,32,128]{2,1,0:T(8,128)(2,1)S(1)}, u32[]{:S(2)}, u32[]{:S(2)}) collective-permute-start(bf16[128,32,128]{2,1,0:T(8,128)(2,1)S(1)} %maximum_select_fusion.5), channel_id=1, source_target_pairs={{0,2},{1,3},{2,0},{3,1},{4,6},{5,7},{6,4},{7,5},{8,10},{9,11},{10,... | collective-permute-start | bytes 3145736 | tf_op jit(solution)/shard_map/ppermute | solution.py:51
  374.0 17.4 %collective-permute-start.65 = (bf16[256,32,128]{2,1,0:T(8,128)(2,1)S(1)}, bf16[256,32,128]{2,1,0:T(8,128)(2,1)}, u32[]{:S(2)}, u32[]{:S(2)}) collective-permute-start(bf16[256,32,128]{2,1,0:T(8,128)(2,1)S(1)} %maximum_select_fusion.3), channel_id=1, source_target_pairs={{0,1},{1,0},{2,3},{3,2},{4,5},{5,4},{6,7},{7,6},{8,9},{9,8},{10,11... | collective-permute-start | bytes 6291464 | tf_op jit(solution)/shard_map/ppermute | solution.py:51
  378.5 9.0 %collective-permute-start.53 = (f32[128,128]{1,0:T(8,128)S(1)}, f32[128,128]{1,0:T(8,128)S(1)}, u32[]{:S(2)}, u32[]{:S(2)}) collective-permute-start(f32[128,128]{1,0:T(8,128)S(1)} %get-tuple-element.60), channel_id=1, source_target_pairs={{0,8},{8,16},{16,24},{24,32},{32,40},{40,48},{48,56},{56,64},{64,7... | collective-permute-start | bytes 196616 | tf_op jit(solution)/shard_map/ppermute | solution.py:15
  380.6 6.9 %collective-permute-start.55 = (f32[128,128]{1,0:T(8,128)S(1)}, f32[128,128]{1,0:T(8,128)S(1)}, u32[]{:S(2)}, u32[]{:S(2)}) collective-permute-start(f32[128,128]{1,0:T(8,128)S(1)} %get-tuple-element.61), channel_id=1, source_target_pairs={{0,1},{1,2},{2,3},{3,4},{4,5},{5,6},{6,7},{8,9},{9,10},{10,11},{11... | collective-permute-start | bytes 196616 | tf_op jit(solution)/shard_map/ppermute | solution.py:15
  382.8 6.2 %collective-permute-start.54 = (f32[128,128]{1,0:T(8,128)S(1)}, f32[128,128]{1,0:T(8,128)S(1)}, u32[]{:S(2)}, u32[]{:S(2)}) collective-permute-start(f32[128,128]{1,0:T(8,128)S(1)} %get-tuple-element.62), channel_id=1, source_target_pairs={{8,0},{16,8},{24,16},{32,24},{40,32},{48,40},{56,48},{64,56},{72,6... | collective-permute-start | bytes 196616 | tf_op jit(solution)/shard_map/ppermute | solution.py:15
  406.6 11.2 %collective-permute-start.66 = (bf16[128,128]{1,0:T(8,128)(2,1)S(1)}, bf16[128,128]{1,0:T(8,128)(2,1)S(1)}, u32[]{:S(2)}, u32[]{:S(2)}) collective-permute-start(bf16[128,128]{1,0:T(8,128)(2,1)S(1)} %get-tuple-element.68), channel_id=1, source_target_pairs={{0,8},{8,16},{16,24},{24,32},{32,40},{40,48},{48,56},{56,64},{64,7... | collective-permute-start | bytes 98312 | tf_op jit(solution)/shard_map/ppermute | solution.py:15
  410.9 6.9 %collective-permute-start.68 = (bf16[128,128]{1,0:T(8,128)(2,1)S(1)}, bf16[128,128]{1,0:T(8,128)(2,1)S(1)}, u32[]{:S(2)}, u32[]{:S(2)}) collective-permute-start(bf16[128,128]{1,0:T(8,128)(2,1)S(1)} %get-tuple-element.69), channel_id=1, source_target_pairs={{0,1},{1,2},{2,3},{3,4},{4,5},{5,6},{6,7},{8,9},{9,10},{10,11},{11... | collective-permute-start | bytes 98312 | tf_op jit(solution)/shard_map/ppermute | solution.py:15
  430.7 7.0 %collective-permute-start.72 = (f32[6,128]{1,0:T(8,128)S(1)}, f32[6,128]{1,0:T(8,128)S(1)}, u32[]{:S(2)}, u32[]{:S(2)}) collective-permute-start(f32[6,128]{1,0:T(8,128)S(1)} %add.307), channel_id=1, source_target_pairs={{0,4},{1,5},{2,6},{3,7},{4,0},{5,1},{6,2},{7,3},{8,12},{9,13},{10,... | collective-permute-start | bytes 9224 | tf_op jit(solution)/shard_map/ppermute | solution.py:32
  437.7 5.8 %collective-permute-start.73 = (f32[6,128]{1,0:T(8,128)S(1)}, f32[6,128]{1,0:T(8,128)S(1)}, u32[]{:S(2)}, u32[]{:S(2)}) collective-permute-start(f32[6,128]{1,0:T(8,128)S(1)} %add.308), channel_id=1, source_target_pairs={{0,8},{8,0},{16,24},{24,16},{32,40},{40,32},{48,56},{56,48},{64,72... | collective-permute-start | bytes 9224 | tf_op jit(solution)/shard_map/ppermute | solution.py:32
  443.5 8.9 %collective-permute-start.74 = (f32[6,128]{1,0:T(8,128)S(1)}, f32[6,128]{1,0:T(8,128)S(1)}, u32[]{:S(2)}, u32[]{:S(2)}) collective-permute-start(f32[6,128]{1,0:T(8,128)S(1)} %add.309), channel_id=1, source_target_pairs={{0,16},{8,24},{16,0},{24,8},{32,48},{40,56},{48,32},{56,40},{64,80... | collective-permute-start | bytes 9224 | tf_op jit(solution)/shard_map/ppermute | solution.py:32
  452.4 7.8 %collective-permute-start.75 = (f32[6,128]{1,0:T(8,128)S(1)}, f32[6,128]{1,0:T(8,128)S(1)}, u32[]{:S(2)}, u32[]{:S(2)}) collective-permute-start(f32[6,128]{1,0:T(8,128)S(1)} %add.310), channel_id=1, source_target_pairs={{0,32},{8,40},{16,48},{24,56},{32,0},{40,8},{48,16},{56,24},{64,96... | collective-permute-start | bytes 9224 | tf_op jit(solution)/shard_map/ppermute | solution.py:32
  460.2 7.2 %collective-permute-start.76 = (f32[6,128]{1,0:T(8,128)S(1)}, f32[6,128]{1,0:T(8,128)S(1)}, u32[]{:S(2)}, u32[]{:S(2)}) collective-permute-start(f32[6,128]{1,0:T(8,128)S(1)} %add.311), channel_id=1, source_target_pairs={{0,64},{8,72},{16,80},{24,88},{32,96},{40,104},{48,112},{56,120},{... | collective-permute-start | bytes 9224 | tf_op jit(solution)/shard_map/ppermute | solution.py:32
  467.5 11.7 %collective-permute-start.77 = (f32[6,128]{1,0:T(8,128)S(1)}, f32[6,128]{1,0:T(8,128)S(1)}, u32[]{:S(2)}, u32[]{:S(2)}) collective-permute-start(f32[6,128]{1,0:T(8,128)S(1)} %add.312), channel_id=1, source_target_pairs={{0,128},{8,136},{16,144},{24,152},{32,160},{40,168},{48,176},{56,1... | collective-permute-start | bytes 9224 | tf_op jit(solution)/shard_map/ppermute | solution.py:32
  479.1 15.3 %collective-permute-start.78 = (f32[6,128]{1,0:T(8,128)S(1)}, f32[6,128]{1,0:T(8,128)S(1)}, u32[]{:S(2)}, u32[]{:S(2)}) collective-permute-start(f32[6,128]{1,0:T(8,128)S(1)} %add.313), channel_id=1, source_target_pairs={{0,256},{8,264},{16,272},{24,280},{32,288},{40,296},{48,304},{56,3... | collective-permute-start | bytes 9224 | tf_op jit(solution)/shard_map/ppermute | solution.py:32
  (38 other events, 1473.6 us)

commit v6 on v4

--- a/solution.py
+++ b/solution.py
@@ -22,7 +22,8 @@
 
 
 def allsum(value):
-    for axis in ("gy", "gx"):
+    value = lax.psum(value, "gy")
+    for axis in ("gx",):
         count = lax.axis_size(axis)
         if count & (count - 1):
             value = lax.psum(value, axis)

time: 494 us -> 484 us (0.980)
  starting transfers between devices: 282 us -> 237 us
  blocking collectives: 0 us -> 39.4 us
    ppermute x27 -> x18, starting transfers between devices: 159 us -> 118 us  [allsum(): lax.ppermute(value, axis, [(i, i ^ step) for i in range(count)])]
    psum x0 -> x3, blocking collectives: none -> 39.4 us  [allsum(): value = lax.psum(value, 'gy')]
    ppermute x27 -> x18, waiting for transfers between devices: 50.2 us -> 41.5 us  [allsum(): lax.ppermute(value, axis, [(i, i ^ step) for i in range(count)])]
  transfers between devices with their start and end apart: 61 -> 52, of which waited for: 49 -> 40; matrix products, arithmetic and copies ran while one was open for 2% -> 3% of each run, Pallas kernels for 0% -> 0%
where the time goes in v6:
time: 484 us; the launch traced here: 480 us
  starting transfers between devices  237 us (49%)
  waiting for transfers between devices  134 us (28%)
  blocking collectives  39.4 us (8%)
  local copies, waits for them, and re-layouts  33.5 us (7%)
  matrix products  17.5 us (4%)
  other arithmetic  14.1 us (3%)
    ppermute x18, starting transfers between devices, allsum(): lax.ppermute(value, axis, [(i, i ^ step) for i in range(count)])  118 us
    ppermute x18, waiting for transfers between devices, doubling_gather(): got = lax.ppermute(held, axis, [(i, i ^ step) for i in range(count)])  87.6 us
    ppermute x18, starting transfers between devices, doubling_gather(): got = lax.ppermute(held, axis, [(i, i ^ step) for i in range(count)])  77.9 us
    ppermute x18, waiting for transfers between devices, allsum(): lax.ppermute(value, axis, [(i, i ^ step) for i in range(count)])  41.5 us
    ppermute x16, starting transfers between devices, neighbours(): return (lax.ppermute(rows[1], axis, up), lax.ppermute(rows[0], axis, down))  41.4 us
    psum x3, blocking collectives, allsum(): value = lax.psum(value, 'gy')  39.4 us
    reshape x2, local copies, waits for them, and re-layouts, precondition(): placed.reshape(-1, system_count)  14.9 us
  transfers between devices with their start and end apart: 52, of which 40 were waited for; matrix products, arithmetic and copies ran while one was open for 3% of the time, Pallas kernels for 0%

profile of v6, /device:TPU:6, one launch (start us, length us, event | category | flops | bytes accessed | tf_op | source)
XLA Modules:
  0.0 479.6 jit_solution(1322125724503588691)
XLA Ops:
  1.6 14.3 %psum.35 = f32[128]{0:T(128)S(1)} all-reduce(f32[128]{0:T(128)S(1)} %multiply_reduce_fusion.10), channel_id=1, replica_groups=mesh['gx'=64,'gy'=8] {'gy'}, use_global_device_ids=true, to_apply=%region_1.0 | all-reduce | flops 128 | bytes 1024 | tf_op jit(solution)/shard_map/psum | solution.py:25
  23.3 5.0 %collective-permute-done.13 = f32[128]{0:T(128)S(1)} collective-permute-done((f32[128]{0:T(128)S(1)}, f32[128]{0:T(128)S(1)}, u32[]{:S(2)}, u32[]{:S(2)}) %collective-permute-start.13) | collective-permute-done | bytes 544 | tf_op jit(solution)/shard_map/ppermute | solution.py:33
  35.7 4.4 collective-permute-done.15
  40.1 5.7 %collective-permute-start.16 = (f32[128]{0:T(128)S(1)}, f32[128]{0:T(128)S(1)}, u32[]{:S(2)}, u32[]{:S(2)}) collective-permute-start(f32[128]{0:T(128)S(1)} %add.237), channel_id=1, source_target_pairs={{0,128},{8,136},{16,144},{24,152},{32,160},{40,168},{48,176},{56,1... | collective-permute-start | bytes 1544 | tf_op jit(solution)/shard_map/ppermute | solution.py:33
  45.8 3.7 collective-permute-done.16
  49.5 12.0 %collective-permute-start.17 = (f32[128]{0:T(128)S(1)}, f32[128]{0:T(128)S(1)}, u32[]{:S(2)}, u32[]{:S(2)}) collective-permute-start(f32[128]{0:T(128)S(1)} %add.238), channel_id=1, source_target_pairs={{0,256},{8,264},{16,272},{24,280},{32,288},{40,296},{48,304},{56,3... | collective-permute-start | bytes 1544 | tf_op jit(solution)/shard_map/ppermute | solution.py:33
  64.6 12.0 %collective-permute-start.22 = (bf16[1,32,128]{2,1,0:T(8,128)(2,1)S(1)}, bf16[1,32,128]{2,1,0:T(8,128)(2,1)S(1)}, u32[]{:S(2)}, u32[]{:S(2)}) collective-permute-start(bf16[1,32,128]{2,1,0:T(8,128)(2,1)S(1)} %fusion.14), channel_id=1, source_target_pairs={{0,256},{8,264},{16,272},{24,280},{32,288},{40,296},{48,304},{56,3... | collective-permute-start | bytes 24584 | tf_op jit(solution)/shard_map/ppermute | solution.py:52
  78.9 5.7 %collective-permute-start.23 = (bf16[2,32,128]{2,1,0:T(8,128)(2,1)S(1)}, bf16[2,32,128]{2,1,0:T(8,128)(2,1)S(1)}, u32[]{:S(2)}, u32[]{:S(2)}) collective-permute-start(bf16[2,32,128]{2,1,0:T(8,128)(2,1)S(1)} %maximum_select_fusion.24), channel_id=1, source_target_pairs={{0,128},{8,136},{16,144},{24,152},{32,160},{40,168},{48,176},{56,1... | collective-permute-start | bytes 49160 | tf_op jit(solution)/shard_map/ppermute | solution.py:52
  84.6 3.8 collective-permute-done.23
  91.3 4.0 collective-permute-done.24
  97.5 4.0 collective-permute-done.25
  101.5 4.3 collective-permute-start.26
  105.8 4.0 collective-permute-done.26
  112.6 5.6 %collective-permute-done.27 = bf16[32,32,128]{2,1,0:T(8,128)(2,1)S(1)} collective-permute-done((bf16[32,32,128]{2,1,0:T(8,128)(2,1)S(1)}, bf16[32,32,128]{2,1,0:T(8,128)(2,1)S(1)}, u32[]{:S(2)}, u32[]{:S(2)}) %collective-permute-start.27) | collective-permute-done | bytes 262176 | tf_op jit(solution)/shard_map/ppermute | solution.py:52
  119.0 3.7 collective-permute-start.28
  122.7 13.4 %collective-permute-done.28 = bf16[64,32,128]{2,1,0:T(8,128)(2,1)S(1)} collective-permute-done((bf16[64,32,128]{2,1,0:T(8,128)(2,1)S(1)}, bf16[64,32,128]{2,1,0:T(8,128)(2,1)S(1)}, u32[]{:S(2)}, u32[]{:S(2)}) %collective-permute-start.28) | collective-permute-done | bytes 524320 | tf_op jit(solution)/shard_map/ppermute | solution.py:52
  138.3 4.1 collective-permute-start.29
  150.8 3.6 collective-permute-start.21
  165.6 4.2 convolution_convert_fusion.1
  169.8 7.4 %reshape.148 = bf16[16384,128]{1,0:T(8,128)(2,1)} reshape(bf16[512,4096]{1,0:T(8,128)(2,1)} %convolution_convert_fusion.1) | data formatting | bytes 8388608 | tf_op jit(solution)/shard_map/reshape | solution.py:130
  182.4 4.3 collective-permute-start.31
  198.0 12.5 %psum.36 = f32[3,128]{1,0:T(4,128)S(1)} all-reduce(f32[3,128]{1,0:T(4,128)S(1)} %pad_maximum_fusion.4), channel_id=1, replica_groups=mesh['gx'=64,'gy'=8] {'gy'}, use_global_device_ids=true, to_apply=%region_6.7 | all-reduce | flops 384 | bytes 3072 | tf_op jit(solution)/shard_map/psum | solution.py:25
  210.5 4.3 collective-permute-start.35
  216.3 5.9 %collective-permute-start.36 = (f32[3,128]{1,0:T(4,128)S(1)}, f32[3,128]{1,0:T(4,128)S(1)}, u32[]{:S(2)}, u32[]{:S(2)}) collective-permute-start(f32[3,128]{1,0:T(4,128)S(1)} %add.255), channel_id=1, source_target_pairs={{0,16},{8,24},{16,0},{24,8},{32,48},{40,56},{48,32},{56,40},{64,80... | collective-permute-start | bytes 4616 | tf_op jit(solution)/shard_map/ppermute | solution.py:33
  223.7 7.1 %collective-permute-start.37 = (f32[3,128]{1,0:T(4,128)S(1)}, f32[3,128]{1,0:T(4,128)S(1)}, u32[]{:S(2)}, u32[]{:S(2)}) collective-permute-start(f32[3,128]{1,0:T(4,128)S(1)} %add.256), channel_id=1, source_target_pairs={{0,32},{8,40},{16,48},{24,56},{32,0},{40,8},{48,16},{56,24},{64,96... | collective-permute-start | bytes 4616 | tf_op jit(solution)/shard_map/ppermute | solution.py:33
  232.4 4.4 collective-permute-start.38
  238.8 10.0 %collective-permute-start.39 = (f32[3,128]{1,0:T(4,128)S(1)}, f32[3,128]{1,0:T(4,128)S(1)}, u32[]{:S(2)}, u32[]{:S(2)}) collective-permute-start(f32[3,128]{1,0:T(4,128)S(1)} %add.258), channel_id=1, source_target_pairs={{0,128},{8,136},{16,144},{24,152},{32,160},{40,168},{48,176},{56,1... | collective-permute-start | bytes 4616 | tf_op jit(solution)/shard_map/ppermute | solution.py:33
  250.4 13.9 %collective-permute-start.40 = (f32[3,128]{1,0:T(4,128)S(1)}, f32[3,128]{1,0:T(4,128)S(1)}, u32[]{:S(2)}, u32[]{:S(2)}) collective-permute-start(f32[3,128]{1,0:T(4,128)S(1)} %add.259), channel_id=1, source_target_pairs={{0,256},{8,264},{16,272},{24,280},{32,288},{40,296},{48,304},{56,3... | collective-permute-start | bytes 4616 | tf_op jit(solution)/shard_map/ppermute | solution.py:33
  268.6 12.6 %collective-permute-start.45 = (bf16[1,32,128]{2,1,0:T(8,128)(2,1)S(1)}, bf16[1,32,128]{2,1,0:T(8,128)(2,1)S(1)}, u32[]{:S(2)}, u32[]{:S(2)}) collective-permute-start(bf16[1,32,128]{2,1,0:T(8,128)(2,1)S(1)} %fusion.15), channel_id=1, source_target_pairs={{0,256},{8,264},{16,272},{24,280},{32,288},{40,296},{48,304},{56,3... | collective-permute-start | bytes 24584 | tf_op jit(solution)/shard_map/ppermute | solution.py:52
  282.8 6.5 %collective-permute-start.46 = (bf16[2,32,128]{2,1,0:T(8,128)(2,1)S(1)}, bf16[2,32,128]{2,1,0:T(8,128)(2,1)S(1)}, u32[]{:S(2)}, u32[]{:S(2)}) collective-permute-start(bf16[2,32,128]{2,1,0:T(8,128)(2,1)S(1)} %maximum_select_fusion.25), channel_id=1, source_target_pairs={{0,128},{8,136},{16,144},{24,152},{32,160},{40,168},{48,176},{56,1... | collective-permute-start | bytes 49160 | tf_op jit(solution)/shard_map/ppermute | solution.py:52
  294.3 4.8 collective-permute-done.47
  301.2 4.1 collective-permute-done.48
  307.3 6.4 %collective-permute-done.49 = bf16[16,32,128]{2,1,0:T(8,128)(2,1)S(1)} collective-permute-done((bf16[16,32,128]{2,1,0:T(8,128)(2,1)S(1)}, bf16[16,32,128]{2,1,0:T(8,128)(2,1)S(1)}, u32[]{:S(2)}, u32[]{:S(2)}) %collective-permute-start.49) | collective-permute-done | bytes 131104 | tf_op jit(solution)/shard_map/ppermute | solution.py:52
  315.6 6.3 %collective-permute-done.50 = bf16[32,32,128]{2,1,0:T(8,128)(2,1)S(1)} collective-permute-done((bf16[32,32,128]{2,1,0:T(8,128)(2,1)S(1)}, bf16[32,32,128]{2,1,0:T(8,128)(2,1)S(1)}, u32[]{:S(2)}, u32[]{:S(2)}) %collective-permute-start.50) | collective-permute-done | bytes 262176 | tf_op jit(solution)/shard_map/ppermute | solution.py:52
  322.8 5.3 %collective-permute-start.51 = (bf16[64,32,128]{2,1,0:T(8,128)(2,1)S(1)}, bf16[64,32,128]{2,1,0:T(8,128)(2,1)S(1)}, u32[]{:S(2)}, u32[]{:S(2)}) collective-permute-start(bf16[64,32,128]{2,1,0:T(8,128)(2,1)S(1)} %maximum_select_fusion.14), channel_id=1, source_target_pairs={{0,4},{1,5},{2,6},{3,7},{4,0},{5,1},{6,2},{7,3},{8,12},{9,13},{10,... | collective-permute-start | bytes 1572872 | tf_op jit(solution)/shard_map/ppermute | solution.py:52
  328.1 12.9 %collective-permute-done.51 = bf16[64,32,128]{2,1,0:T(8,128)(2,1)S(1)} collective-permute-done((bf16[64,32,128]{2,1,0:T(8,128)(2,1)S(1)}, bf16[64,32,128]{2,1,0:T(8,128)(2,1)S(1)}, u32[]{:S(2)}, u32[]{:S(2)}) %collective-permute-start.51) | collective-permute-done | bytes 524320 | tf_op jit(solution)/shard_map/ppermute | solution.py:52
  341.9 4.1 collective-permute-start.52
  347.7 11.1 %collective-permute-done.52 = bf16[128,32,128]{2,1,0:T(8,128)(2,1)S(1)} collective-permute-done((bf16[128,32,128]{2,1,0:T(8,128)(2,1)S(1)}, bf16[128,32,128]{2,1,0:T(8,128)(2,1)S(1)}, u32[]{:S(2)}, u32[]{:S(2)}) %collective-permute-start.52) | collective-permute-done | bytes 1048608 | tf_op jit(solution)/shard_map/ppermute | solution.py:52
  375.2 4.2 convolution_convert_fusion
  379.4 7.4 %reshape.150 = bf16[16384,128]{1,0:T(8,128)(2,1)} reshape(bf16[512,4096]{1,0:T(8,128)(2,1)} %convolution_convert_fusion) | data formatting | bytes 8388608 | tf_op jit(solution)/shard_map/reshape | solution.py:130
  392.0 4.3 collective-permute-start.54
  407.5 12.5 %psum.37 = f32[6,128]{1,0:T(8,128)S(1)} all-reduce(f32[6,128]{1,0:T(8,128)S(1)} %stack.126), channel_id=1, replica_groups=mesh['gx'=64,'gy'=8] {'gy'}, use_global_device_ids=true, to_apply=%region_18.19 | all-reduce | flops 768 | bytes 6144 | tf_op jit(solution)/shard_map/psum | solution.py:25
  420.1 4.3 collective-permute-start.58
  425.9 7.7 %collective-permute-start.59 = (f32[6,128]{1,0:T(8,128)S(1)}, f32[6,128]{1,0:T(8,128)S(1)}, u32[]{:S(2)}, u32[]{:S(2)}) collective-permute-start(f32[6,128]{1,0:T(8,128)S(1)} %add.265), channel_id=1, source_target_pairs={{0,16},{8,24},{16,0},{24,8},{32,48},{40,56},{48,32},{56,40},{64,80... | collective-permute-start | bytes 9224 | tf_op jit(solution)/shard_map/ppermute | solution.py:33
  435.1 5.9 %collective-permute-start.60 = (f32[6,128]{1,0:T(8,128)S(1)}, f32[6,128]{1,0:T(8,128)S(1)}, u32[]{:S(2)}, u32[]{:S(2)}) collective-permute-start(f32[6,128]{1,0:T(8,128)S(1)} %add.266), channel_id=1, source_target_pairs={{0,32},{8,40},{16,48},{24,56},{32,0},{40,8},{48,16},{56,24},{64,96... | collective-permute-start | bytes 9224 | tf_op jit(solution)/shard_map/ppermute | solution.py:33
  442.6 5.8 %collective-permute-start.61 = (f32[6,128]{1,0:T(8,128)S(1)}, f32[6,128]{1,0:T(8,128)S(1)}, u32[]{:S(2)}, u32[]{:S(2)}) collective-permute-start(f32[6,128]{1,0:T(8,128)S(1)} %add.267), channel_id=1, source_target_pairs={{0,64},{8,72},{16,80},{24,88},{32,96},{40,104},{48,112},{56,120},{... | collective-permute-start | bytes 9224 | tf_op jit(solution)/shard_map/ppermute | solution.py:33
  450.0 9.7 %collective-permute-start.62 = (f32[6,128]{1,0:T(8,128)S(1)}, f32[6,128]{1,0:T(8,128)S(1)}, u32[]{:S(2)}, u32[]{:S(2)}) collective-permute-start(f32[6,128]{1,0:T(8,128)S(1)} %add.268), channel_id=1, source_target_pairs={{0,128},{8,136},{16,144},{24,152},{32,160},{40,168},{48,176},{56,1... | collective-permute-start | bytes 9224 | tf_op jit(solution)/shard_map/ppermute | solution.py:33
  461.3 13.9 %collective-permute-start.63 = (f32[6,128]{1,0:T(8,128)S(1)}, f32[6,128]{1,0:T(8,128)S(1)}, u32[]{:S(2)}, u32[]{:S(2)}) collective-permute-start(f32[6,128]{1,0:T(8,128)S(1)} %add.269), channel_id=1, source_target_pairs={{0,256},{8,264},{16,272},{24,280},{32,288},{40,296},{48,304},{56,3... | collective-permute-start | bytes 9224 | tf_op jit(solution)/shard_map/ppermute | solution.py:33
  (253 shorter events, 139.0 us)
Async XLA Ops:
  21.3 7.0 %collective-permute-start.13 = (f32[128]{0:T(128)S(1)}, f32[128]{0:T(128)S(1)}, u32[]{:S(2)}, u32[]{:S(2)}) collective-permute-start(f32[128]{0:T(128)S(1)} %add.234), channel_id=1, source_target_pairs={{0,16},{8,24},{16,0},{24,8},{32,48},{40,56},{48,32},{56,40},{64,80... | collective-permute-start | bytes 1544 | tf_op jit(solution)/shard_map/ppermute | solution.py:33
  28.3 5.5 %collective-permute-start.14 = (f32[128]{0:T(128)S(1)}, f32[128]{0:T(128)S(1)}, u32[]{:S(2)}, u32[]{:S(2)}) collective-permute-start(f32[128]{0:T(128)S(1)} %add.235), channel_id=1, source_target_pairs={{0,32},{8,40},{16,48},{24,56},{32,0},{40,8},{48,16},{56,24},{64,96... | collective-permute-start | bytes 1544 | tf_op jit(solution)/shard_map/ppermute | solution.py:33
  33.8 6.3 %collective-permute-start.15 = (f32[128]{0:T(128)S(1)}, f32[128]{0:T(128)S(1)}, u32[]{:S(2)}, u32[]{:S(2)}) collective-permute-start(f32[128]{0:T(128)S(1)} %add.236), channel_id=1, source_target_pairs={{0,64},{8,72},{16,80},{24,88},{32,96},{40,104},{48,112},{56,120},{... | collective-permute-start | bytes 1544 | tf_op jit(solution)/shard_map/ppermute | solution.py:33
  40.1 9.4 %collective-permute-start.16 = (f32[128]{0:T(128)S(1)}, f32[128]{0:T(128)S(1)}, u32[]{:S(2)}, u32[]{:S(2)}) collective-permute-start(f32[128]{0:T(128)S(1)} %add.237), channel_id=1, source_target_pairs={{0,128},{8,136},{16,144},{24,152},{32,160},{40,168},{48,176},{56,1... | collective-permute-start | bytes 1544 | tf_op jit(solution)/shard_map/ppermute | solution.py:33
  49.5 14.2 %collective-permute-start.17 = (f32[128]{0:T(128)S(1)}, f32[128]{0:T(128)S(1)}, u32[]{:S(2)}, u32[]{:S(2)}) collective-permute-start(f32[128]{0:T(128)S(1)} %add.238), channel_id=1, source_target_pairs={{0,256},{8,264},{16,272},{24,280},{32,288},{40,296},{48,304},{56,3... | collective-permute-start | bytes 1544 | tf_op jit(solution)/shard_map/ppermute | solution.py:33
  64.6 14.3 %collective-permute-start.22 = (bf16[1,32,128]{2,1,0:T(8,128)(2,1)S(1)}, bf16[1,32,128]{2,1,0:T(8,128)(2,1)S(1)}, u32[]{:S(2)}, u32[]{:S(2)}) collective-permute-start(bf16[1,32,128]{2,1,0:T(8,128)(2,1)S(1)} %fusion.14), channel_id=1, source_target_pairs={{0,256},{8,264},{16,272},{24,280},{32,288},{40,296},{48,304},{56,3... | collective-permute-start | bytes 24584 | tf_op jit(solution)/shard_map/ppermute | solution.py:52
  78.9 9.5 %collective-permute-start.23 = (bf16[2,32,128]{2,1,0:T(8,128)(2,1)S(1)}, bf16[2,32,128]{2,1,0:T(8,128)(2,1)S(1)}, u32[]{:S(2)}, u32[]{:S(2)}) collective-permute-start(bf16[2,32,128]{2,1,0:T(8,128)(2,1)S(1)} %maximum_select_fusion.24), channel_id=1, source_target_pairs={{0,128},{8,136},{16,144},{24,152},{32,160},{40,168},{48,176},{56,1... | collective-permute-start | bytes 49160 | tf_op jit(solution)/shard_map/ppermute | solution.py:52
  88.4 6.8 %collective-permute-start.24 = (bf16[4,32,128]{2,1,0:T(8,128)(2,1)S(1)}, bf16[4,32,128]{2,1,0:T(8,128)(2,1)S(1)}, u32[]{:S(2)}, u32[]{:S(2)}) collective-permute-start(bf16[4,32,128]{2,1,0:T(8,128)(2,1)S(1)} %maximum_select_fusion.22), channel_id=1, source_target_pairs={{0,64},{8,72},{16,80},{24,88},{32,96},{40,104},{48,112},{56,120},{... | collective-permute-start | bytes 98312 | tf_op jit(solution)/shard_map/ppermute | solution.py:52
  95.3 6.2 %collective-permute-start.25 = (bf16[8,32,128]{2,1,0:T(8,128)(2,1)S(1)}, bf16[8,32,128]{2,1,0:T(8,128)(2,1)S(1)}, u32[]{:S(2)}, u32[]{:S(2)}) collective-permute-start(bf16[8,32,128]{2,1,0:T(8,128)(2,1)S(1)} %maximum_select_fusion.20), channel_id=1, source_target_pairs={{0,32},{8,40},{16,48},{24,56},{32,0},{40,8},{48,16},{56,24},{64,96... | collective-permute-start | bytes 196616 | tf_op jit(solution)/shard_map/ppermute | solution.py:52
  101.5 8.4 %collective-permute-start.26 = (bf16[16,32,128]{2,1,0:T(8,128)(2,1)S(1)}, bf16[16,32,128]{2,1,0:T(8,128)(2,1)S(1)}, u32[]{:S(2)}, u32[]{:S(2)}) collective-permute-start(bf16[16,32,128]{2,1,0:T(8,128)(2,1)S(1)} %maximum_select_fusion.18), channel_id=1, source_target_pairs={{0,16},{8,24},{16,0},{24,8},{32,48},{40,56},{48,32},{56,40},{64,80... | collective-permute-start | bytes 393224 | tf_op jit(solution)/shard_map/ppermute | solution.py:52
  109.9 8.3 %collective-permute-start.27 = (bf16[32,32,128]{2,1,0:T(8,128)(2,1)S(1)}, bf16[32,32,128]{2,1,0:T(8,128)(2,1)S(1)}, u32[]{:S(2)}, u32[]{:S(2)}) collective-permute-start(bf16[32,32,128]{2,1,0:T(8,128)(2,1)S(1)} %maximum_select_fusion.16), channel_id=1, source_target_pairs={{0,8},{8,0},{16,24},{24,16},{32,40},{40,32},{48,56},{56,48},{64,72... | collective-permute-start | bytes 786440 | tf_op jit(solution)/shard_map/ppermute | solution.py:52
  119.0 17.2 %collective-permute-start.28 = (bf16[64,32,128]{2,1,0:T(8,128)(2,1)S(1)}, bf16[64,32,128]{2,1,0:T(8,128)(2,1)S(1)}, u32[]{:S(2)}, u32[]{:S(2)}) collective-permute-start(bf16[64,32,128]{2,1,0:T(8,128)(2,1)S(1)} %maximum_select_fusion.12), channel_id=1, source_target_pairs={{0,4},{1,5},{2,6},{3,7},{4,0},{5,1},{6,2},{7,3},{8,12},{9,13},{10,... | collective-permute-start | bytes 1572872 | tf_op jit(solution)/shard_map/ppermute | solution.py:52
  138.3 19.8 %collective-permute-start.29 = (bf16[128,32,128]{2,1,0:T(8,128)(2,1)S(1)}, bf16[128,32,128]{2,1,0:T(8,128)(2,1)S(1)}, u32[]{:S(2)}, u32[]{:S(2)}) collective-permute-start(bf16[128,32,128]{2,1,0:T(8,128)(2,1)S(1)} %maximum_select_fusion.8), channel_id=1, source_target_pairs={{0,2},{1,3},{2,0},{3,1},{4,6},{5,7},{6,4},{7,5},{8,10},{9,11},{10,... | collective-permute-start | bytes 3145736 | tf_op jit(solution)/shard_map/ppermute | solution.py:52
  144.2 16.3 %collective-permute-start.18 = (f32[128,128]{1,0:T(8,128)}, f32[128,128]{1,0:T(8,128)S(1)}, u32[]{:S(2)}, u32[]{:S(2)}) collective-permute-start(f32[128,128]{1,0:T(8,128)} %get-tuple-element.64), channel_id=1, source_target_pairs={{0,8},{8,16},{16,24},{24,32},{32,40},{40,48},{48,56},{56,64},{64,7... | collective-permute-start | bytes 196616 | tf_op jit(solution)/shard_map/ppermute | solution.py:15
  147.6 12.9 %collective-permute-start.20 = (f32[128,128]{1,0:T(8,128)}, f32[128,128]{1,0:T(8,128)S(1)}, u32[]{:S(2)}, u32[]{:S(2)}) collective-permute-start(f32[128,128]{1,0:T(8,128)} %get-tuple-element.65), channel_id=1, source_target_pairs={{0,1},{1,2},{2,3},{3,4},{4,5},{5,6},{6,7},{8,9},{9,10},{10,11},{11... | collective-permute-start | bytes 196616 | tf_op jit(solution)/shard_map/ppermute | solution.py:15
  149.5 11.0 %collective-permute-start.19 = (f32[128,128]{1,0:T(8,128)}, f32[128,128]{1,0:T(8,128)S(1)}, u32[]{:S(2)}, u32[]{:S(2)}) collective-permute-start(f32[128,128]{1,0:T(8,128)} %get-tuple-element.66), channel_id=1, source_target_pairs={{8,0},{16,8},{24,16},{32,24},{40,32},{48,40},{56,48},{64,56},{72,6... | collective-permute-start | bytes 196616 | tf_op jit(solution)/shard_map/ppermute | solution.py:15
  150.8 9.8 %collective-permute-start.21 = (f32[128,128]{1,0:T(8,128)}, f32[128,128]{1,0:T(8,128)}, u32[]{:S(2)}, u32[]{:S(2)}) collective-permute-start(f32[128,128]{1,0:T(8,128)} %get-tuple-element.67), channel_id=1, source_target_pairs={{1,0},{2,1},{3,2},{4,3},{5,4},{6,5},{7,6},{9,8},{10,9},{11,10},{12... | collective-permute-start | bytes 196616 | tf_op jit(solution)/shard_map/ppermute | solution.py:15
  158.5 6.2 %collective-permute-start.30 = (bf16[256,32,128]{2,1,0:T(8,128)(2,1)S(1)}, bf16[256,32,128]{2,1,0:T(8,128)(2,1)S(1)}, u32[]{:S(2)}, u32[]{:S(2)}) collective-permute-start(bf16[256,32,128]{2,1,0:T(8,128)(2,1)S(1)} %maximum_select_fusion.4), channel_id=1, source_target_pairs={{0,1},{1,0},{2,3},{3,2},{4,5},{5,4},{6,7},{7,6},{8,9},{9,8},{10,11... | collective-permute-start | bytes 6291464 | tf_op jit(solution)/shard_map/ppermute | solution.py:52
  182.4 11.2 %collective-permute-start.31 = (bf16[128,128]{1,0:T(8,128)(2,1)S(1)}, bf16[128,128]{1,0:T(8,128)(2,1)S(1)}, u32[]{:S(2)}, u32[]{:S(2)}) collective-permute-start(bf16[128,128]{1,0:T(8,128)(2,1)S(1)} %get-tuple-element.72), channel_id=1, source_target_pairs={{0,8},{8,16},{16,24},{24,32},{32,40},{40,48},{48,56},{56,64},{64,7... | collective-permute-start | bytes 98312 | tf_op jit(solution)/shard_map/ppermute | solution.py:15
  186.7 6.9 %collective-permute-start.33 = (bf16[128,128]{1,0:T(8,128)(2,1)S(1)}, bf16[128,128]{1,0:T(8,128)(2,1)S(1)}, u32[]{:S(2)}, u32[]{:S(2)}) collective-permute-start(bf16[128,128]{1,0:T(8,128)(2,1)S(1)} %get-tuple-element.73), channel_id=1, source_target_pairs={{0,1},{1,2},{2,3},{3,4},{4,5},{5,6},{6,7},{8,9},{9,10},{10,11},{11... | collective-permute-start | bytes 98312 | tf_op jit(solution)/shard_map/ppermute | solution.py:15
  188.6 5.8 %collective-permute-start.32 = (bf16[128,128]{1,0:T(8,128)(2,1)S(1)}, bf16[128,128]{1,0:T(8,128)(2,1)S(1)}, u32[]{:S(2)}, u32[]{:S(2)}) collective-permute-start(bf16[128,128]{1,0:T(8,128)(2,1)S(1)} %get-tuple-element.74), channel_id=1, source_target_pairs={{8,0},{16,8},{24,16},{32,24},{40,32},{48,40},{56,48},{64,56},{72,6... | collective-permute-start | bytes 98312 | tf_op jit(solution)/shard_map/ppermute | solution.py:15
  210.5 5.8 %collective-permute-start.35 = (f32[3,128]{1,0:T(4,128)S(1)}, f32[3,128]{1,0:T(4,128)S(1)}, u32[]{:S(2)}, u32[]{:S(2)}) collective-permute-start(f32[3,128]{1,0:T(4,128)S(1)} %psum.36), channel_id=1, source_target_pairs={{0,8},{8,0},{16,24},{24,16},{32,40},{40,32},{48,56},{56,48},{64,72... | collective-permute-start | bytes 4616 | tf_op jit(solution)/shard_map/ppermute | solution.py:33
  216.3 7.4 %collective-permute-start.36 = (f32[3,128]{1,0:T(4,128)S(1)}, f32[3,128]{1,0:T(4,128)S(1)}, u32[]{:S(2)}, u32[]{:S(2)}) collective-permute-start(f32[3,128]{1,0:T(4,128)S(1)} %add.255), channel_id=1, source_target_pairs={{0,16},{8,24},{16,0},{24,8},{32,48},{40,56},{48,32},{56,40},{64,80... | collective-permute-start | bytes 4616 | tf_op jit(solution)/shard_map/ppermute | solution.py:33
  223.7 8.7 %collective-permute-start.37 = (f32[3,128]{1,0:T(4,128)S(1)}, f32[3,128]{1,0:T(4,128)S(1)}, u32[]{:S(2)}, u32[]{:S(2)}) collective-permute-start(f32[3,128]{1,0:T(4,128)S(1)} %add.256), channel_id=1, source_target_pairs={{0,32},{8,40},{16,48},{24,56},{32,0},{40,8},{48,16},{56,24},{64,96... | collective-permute-start | bytes 4616 | tf_op jit(solution)/shard_map/ppermute | solution.py:33
  232.4 6.4 %collective-permute-start.38 = (f32[3,128]{1,0:T(4,128)S(1)}, f32[3,128]{1,0:T(4,128)S(1)}, u32[]{:S(2)}, u32[]{:S(2)}) collective-permute-start(f32[3,128]{1,0:T(4,128)S(1)} %add.257), channel_id=1, source_target_pairs={{0,64},{8,72},{16,80},{24,88},{32,96},{40,104},{48,112},{56,120},{... | collective-permute-start | bytes 4616 | tf_op jit(solution)/shard_map/ppermute | solution.py:33
  238.8 11.6 %collective-permute-start.39 = (f32[3,128]{1,0:T(4,128)S(1)}, f32[3,128]{1,0:T(4,128)S(1)}, u32[]{:S(2)}, u32[]{:S(2)}) collective-permute-start(f32[3,128]{1,0:T(4,128)S(1)} %add.258), channel_id=1, source_target_pairs={{0,128},{8,136},{16,144},{24,152},{32,160},{40,168},{48,176},{56,1... | collective-permute-start | bytes 4616 | tf_op jit(solution)/shard_map/ppermute | solution.py:33
  250.4 15.5 %collective-permute-start.40 = (f32[3,128]{1,0:T(4,128)S(1)}, f32[3,128]{1,0:T(4,128)S(1)}, u32[]{:S(2)}, u32[]{:S(2)}) collective-permute-start(f32[3,128]{1,0:T(4,128)S(1)} %add.259), channel_id=1, source_target_pairs={{0,256},{8,264},{16,272},{24,280},{32,288},{40,296},{48,304},{56,3... | collective-permute-start | bytes 4616 | tf_op jit(solution)/shard_map/ppermute | solution.py:33
  268.6 14.3 %collective-permute-start.45 = (bf16[1,32,128]{2,1,0:T(8,128)(2,1)S(1)}, bf16[1,32,128]{2,1,0:T(8,128)(2,1)S(1)}, u32[]{:S(2)}, u32[]{:S(2)}) collective-permute-start(bf16[1,32,128]{2,1,0:T(8,128)(2,1)S(1)} %fusion.15), channel_id=1, source_target_pairs={{0,256},{8,264},{16,272},{24,280},{32,288},{40,296},{48,304},{56,3... | collective-permute-start | bytes 24584 | tf_op jit(solution)/shard_map/ppermute | solution.py:52
  282.8 9.6 %collective-permute-start.46 = (bf16[2,32,128]{2,1,0:T(8,128)(2,1)S(1)}, bf16[2,32,128]{2,1,0:T(8,128)(2,1)S(1)}, u32[]{:S(2)}, u32[]{:S(2)}) collective-permute-start(bf16[2,32,128]{2,1,0:T(8,128)(2,1)S(1)} %maximum_select_fusion.25), channel_id=1, source_target_pairs={{0,128},{8,136},{16,144},{24,152},{32,160},{40,168},{48,176},{56,1... | collective-permute-start | bytes 49160 | tf_op jit(solution)/shard_map/ppermute | solution.py:52
  292.4 6.7 %collective-permute-start.47 = (bf16[4,32,128]{2,1,0:T(8,128)(2,1)S(1)}, bf16[4,32,128]{2,1,0:T(8,128)(2,1)S(1)}, u32[]{:S(2)}, u32[]{:S(2)}) collective-permute-start(bf16[4,32,128]{2,1,0:T(8,128)(2,1)S(1)} %maximum_select_fusion.23), channel_id=1, source_target_pairs={{0,64},{8,72},{16,80},{24,88},{32,96},{40,104},{48,112},{56,120},{... | collective-permute-start | bytes 98312 | tf_op jit(solution)/shard_map/ppermute | solution.py:52
  299.1 6.2 %collective-permute-start.48 = (bf16[8,32,128]{2,1,0:T(8,128)(2,1)S(1)}, bf16[8,32,128]{2,1,0:T(8,128)(2,1)S(1)}, u32[]{:S(2)}, u32[]{:S(2)}) collective-permute-start(bf16[8,32,128]{2,1,0:T(8,128)(2,1)S(1)} %maximum_select_fusion.21), channel_id=1, source_target_pairs={{0,32},{8,40},{16,48},{24,56},{32,0},{40,8},{48,16},{56,24},{64,96... | collective-permute-start | bytes 196616 | tf_op jit(solution)/shard_map/ppermute | solution.py:52
  305.3 8.4 %collective-permute-start.49 = (bf16[16,32,128]{2,1,0:T(8,128)(2,1)S(1)}, bf16[16,32,128]{2,1,0:T(8,128)(2,1)S(1)}, u32[]{:S(2)}, u32[]{:S(2)}) collective-permute-start(bf16[16,32,128]{2,1,0:T(8,128)(2,1)S(1)} %maximum_select_fusion.19), channel_id=1, source_target_pairs={{0,16},{8,24},{16,0},{24,8},{32,48},{40,56},{48,32},{56,40},{64,80... | collective-permute-start | bytes 393224 | tf_op jit(solution)/shard_map/ppermute | solution.py:52
  313.7 8.3 %collective-permute-start.50 = (bf16[32,32,128]{2,1,0:T(8,128)(2,1)S(1)}, bf16[32,32,128]{2,1,0:T(8,128)(2,1)S(1)}, u32[]{:S(2)}, u32[]{:S(2)}) collective-permute-start(bf16[32,32,128]{2,1,0:T(8,128)(2,1)S(1)} %maximum_select_fusion.17), channel_id=1, source_target_pairs={{0,8},{8,0},{16,24},{24,16},{32,40},{40,32},{48,56},{56,48},{64,72... | collective-permute-start | bytes 786440 | tf_op jit(solution)/shard_map/ppermute | solution.py:52
  322.8 18.2 %collective-permute-start.51 = (bf16[64,32,128]{2,1,0:T(8,128)(2,1)S(1)}, bf16[64,32,128]{2,1,0:T(8,128)(2,1)S(1)}, u32[]{:S(2)}, u32[]{:S(2)}) collective-permute-start(bf16[64,32,128]{2,1,0:T(8,128)(2,1)S(1)} %maximum_select_fusion.14), channel_id=1, source_target_pairs={{0,4},{1,5},{2,6},{3,7},{4,0},{5,1},{6,2},{7,3},{8,12},{9,13},{10,... | collective-permute-start | bytes 1572872 | tf_op jit(solution)/shard_map/ppermute | solution.py:52
  341.9 16.9 %collective-permute-start.52 = (bf16[128,32,128]{2,1,0:T(8,128)(2,1)S(1)}, bf16[128,32,128]{2,1,0:T(8,128)(2,1)S(1)}, u32[]{:S(2)}, u32[]{:S(2)}) collective-permute-start(bf16[128,32,128]{2,1,0:T(8,128)(2,1)S(1)} %maximum_select_fusion.10), channel_id=1, source_target_pairs={{0,2},{1,3},{2,0},{3,1},{4,6},{5,7},{6,4},{7,5},{8,10},{9,11},{10,... | collective-permute-start | bytes 3145736 | tf_op jit(solution)/shard_map/ppermute | solution.py:52
  359.2 15.1 %collective-permute-start.53 = (bf16[256,32,128]{2,1,0:T(8,128)(2,1)S(1)}, bf16[256,32,128]{2,1,0:T(8,128)(2,1)S(1)}, u32[]{:S(2)}, u32[]{:S(2)}) collective-permute-start(bf16[256,32,128]{2,1,0:T(8,128)(2,1)S(1)} %maximum_select_fusion.6), channel_id=1, source_target_pairs={{0,1},{1,0},{2,3},{3,2},{4,5},{5,4},{6,7},{7,6},{8,9},{9,8},{10,11... | collective-permute-start | bytes 6291464 | tf_op jit(solution)/shard_map/ppermute | solution.py:52
  361.3 8.9 %collective-permute-start.41 = (f32[128,128]{1,0:T(8,128)S(1)}, f32[128,128]{1,0:T(8,128)S(1)}, u32[]{:S(2)}, u32[]{:S(2)}) collective-permute-start(f32[128,128]{1,0:T(8,128)S(1)} %get-tuple-element.60), channel_id=1, source_target_pairs={{0,8},{8,16},{16,24},{24,32},{32,40},{40,48},{48,56},{56,64},{64,7... | collective-permute-start | bytes 196616 | tf_op jit(solution)/shard_map/ppermute | solution.py:15
  363.2 7.0 %collective-permute-start.43 = (f32[128,128]{1,0:T(8,128)S(1)}, f32[128,128]{1,0:T(8,128)S(1)}, u32[]{:S(2)}, u32[]{:S(2)}) collective-permute-start(f32[128,128]{1,0:T(8,128)S(1)} %get-tuple-element.61), channel_id=1, source_target_pairs={{0,1},{1,2},{2,3},{3,4},{4,5},{5,6},{6,7},{8,9},{9,10},{10,11},{11... | collective-permute-start | bytes 196616 | tf_op jit(solution)/shard_map/ppermute | solution.py:15
  365.3 6.2 %collective-permute-start.42 = (f32[128,128]{1,0:T(8,128)S(1)}, f32[128,128]{1,0:T(8,128)S(1)}, u32[]{:S(2)}, u32[]{:S(2)}) collective-permute-start(f32[128,128]{1,0:T(8,128)S(1)} %get-tuple-element.62), channel_id=1, source_target_pairs={{8,0},{16,8},{24,16},{32,24},{40,32},{48,40},{56,48},{64,56},{72,6... | collective-permute-start | bytes 196616 | tf_op jit(solution)/shard_map/ppermute | solution.py:15
  392.0 11.2 %collective-permute-start.54 = (bf16[128,128]{1,0:T(8,128)(2,1)S(1)}, bf16[128,128]{1,0:T(8,128)(2,1)S(1)}, u32[]{:S(2)}, u32[]{:S(2)}) collective-permute-start(bf16[128,128]{1,0:T(8,128)(2,1)S(1)} %get-tuple-element.68), channel_id=1, source_target_pairs={{0,8},{8,16},{16,24},{24,32},{32,40},{40,48},{48,56},{56,64},{64,7... | collective-permute-start | bytes 98312 | tf_op jit(solution)/shard_map/ppermute | solution.py:15
  396.3 6.9 %collective-permute-start.56 = (bf16[128,128]{1,0:T(8,128)(2,1)S(1)}, bf16[128,128]{1,0:T(8,128)(2,1)S(1)}, u32[]{:S(2)}, u32[]{:S(2)}) collective-permute-start(bf16[128,128]{1,0:T(8,128)(2,1)S(1)} %get-tuple-element.69), channel_id=1, source_target_pairs={{0,1},{1,2},{2,3},{3,4},{4,5},{5,6},{6,7},{8,9},{9,10},{10,11},{11... | collective-permute-start | bytes 98312 | tf_op jit(solution)/shard_map/ppermute | solution.py:15
  398.2 5.8 %collective-permute-start.55 = (bf16[128,128]{1,0:T(8,128)(2,1)S(1)}, bf16[128,128]{1,0:T(8,128)(2,1)S(1)}, u32[]{:S(2)}, u32[]{:S(2)}) collective-permute-start(bf16[128,128]{1,0:T(8,128)(2,1)S(1)} %get-tuple-element.70), channel_id=1, source_target_pairs={{8,0},{16,8},{24,16},{32,24},{40,32},{48,40},{56,48},{64,56},{72,6... | collective-permute-start | bytes 98312 | tf_op jit(solution)/shard_map/ppermute | solution.py:15
  420.1 5.8 %collective-permute-start.58 = (f32[6,128]{1,0:T(8,128)S(1)}, f32[6,128]{1,0:T(8,128)S(1)}, u32[]{:S(2)}, u32[]{:S(2)}) collective-permute-start(f32[6,128]{1,0:T(8,128)S(1)} %psum.37), channel_id=1, source_target_pairs={{0,8},{8,0},{16,24},{24,16},{32,40},{40,32},{48,56},{56,48},{64,72... | collective-permute-start | bytes 9224 | tf_op jit(solution)/shard_map/ppermute | solution.py:33
  425.9 9.2 %collective-permute-start.59 = (f32[6,128]{1,0:T(8,128)S(1)}, f32[6,128]{1,0:T(8,128)S(1)}, u32[]{:S(2)}, u32[]{:S(2)}) collective-permute-start(f32[6,128]{1,0:T(8,128)S(1)} %add.265), channel_id=1, source_target_pairs={{0,16},{8,24},{16,0},{24,8},{32,48},{40,56},{48,32},{56,40},{64,80... | collective-permute-start | bytes 9224 | tf_op jit(solution)/shard_map/ppermute | solution.py:33
  435.1 7.5 %collective-permute-start.60 = (f32[6,128]{1,0:T(8,128)S(1)}, f32[6,128]{1,0:T(8,128)S(1)}, u32[]{:S(2)}, u32[]{:S(2)}) collective-permute-start(f32[6,128]{1,0:T(8,128)S(1)} %add.266), channel_id=1, source_target_pairs={{0,32},{8,40},{16,48},{24,56},{32,0},{40,8},{48,16},{56,24},{64,96... | collective-permute-start | bytes 9224 | tf_op jit(solution)/shard_map/ppermute | solution.py:33
  442.6 7.4 %collective-permute-start.61 = (f32[6,128]{1,0:T(8,128)S(1)}, f32[6,128]{1,0:T(8,128)S(1)}, u32[]{:S(2)}, u32[]{:S(2)}) collective-permute-start(f32[6,128]{1,0:T(8,128)S(1)} %add.267), channel_id=1, source_target_pairs={{0,64},{8,72},{16,80},{24,88},{32,96},{40,104},{48,112},{56,120},{... | collective-permute-start | bytes 9224 | tf_op jit(solution)/shard_map/ppermute | solution.py:33
  450.0 11.3 %collective-permute-start.62 = (f32[6,128]{1,0:T(8,128)S(1)}, f32[6,128]{1,0:T(8,128)S(1)}, u32[]{:S(2)}, u32[]{:S(2)}) collective-permute-start(f32[6,128]{1,0:T(8,128)S(1)} %add.268), channel_id=1, source_target_pairs={{0,128},{8,136},{16,144},{24,152},{32,160},{40,168},{48,176},{56,1... | collective-permute-start | bytes 9224 | tf_op jit(solution)/shard_map/ppermute | solution.py:33
  461.3 15.5 %collective-permute-start.63 = (f32[6,128]{1,0:T(8,128)S(1)}, f32[6,128]{1,0:T(8,128)S(1)}, u32[]{:S(2)}, u32[]{:S(2)}) collective-permute-start(f32[6,128]{1,0:T(8,128)S(1)} %add.269), channel_id=1, source_target_pairs={{0,256},{8,264},{16,272},{24,280},{32,288},{40,296},{48,304},{56,3... | collective-permute-start | bytes 9224 | tf_op jit(solution)/shard_map/ppermute | solution.py:33
  (49 other events, 1099.2 us)

commit v7 on v6

--- a/solution.py
+++ b/solution.py
@@ -36,7 +36,7 @@
 
 
 GATHER_ROUNDS = (
-    ("gx", 32), ("gx", 16), ("gx", 8), ("gx", 4), ("gx", 2), ("gx", 1), ("gy", 4), ("gy", 2), ("gy", 1),
+    ("gx", 32), ("gx", 16), ("gx", 8), ("gx", 4), ("gx", 2), ("gx", 1),
 )
 
 
@@ -54,16 +54,17 @@
         held = jnp.where(
             upper, jnp.concatenate([got, held], axis=0), jnp.concatenate([held, got], axis=0)
         )
-    return held.reshape(-1, block.shape[-1])
+    return lax.all_gather(held.reshape(-1, block.shape[-1]), "gy", axis=0, tiled=True)
 
 
 def gathered_order(rounds, count_y):
     order = []
-    for position in range(2 ** len(rounds)):
-        index = {"gx": 0, "gy": 0}
-        for bit, (axis, step) in enumerate(rounds):
-            index[axis] += ((position >> bit) & 1) * step
-        order.append(index["gx"] * count_y + index["gy"])
+    for outer in range(count_y):
+        for position in range(2 ** len(rounds)):
+            index = {"gx": 0, "gy": outer}
+            for bit, (axis, step) in enumerate(rounds):
+                index[axis] += ((position >> bit) & 1) * step
+            order.append(index["gx"] * count_y + index["gy"])
     return np.asarray(order, np.int32)
 
 

time: 484 us -> 484 us (level)
  starting transfers between devices: 237 us -> 209 us
  between operations: 3.6 us -> 16.4 us
  waiting for transfers between devices: 134 us -> 145 us
  local copies, waits for them, and re-layouts: 33.5 us -> 39 us
  matrix products: 17.5 us -> 22.4 us
    all_gather x0 -> x2, waiting for transfers between devices: none -> 51.3 us  [doubling_gather(): lax.all_gather(held.reshape(-1, block.shape[-1]), 'gy', axis=0, tiled=True)]
    ppermute x18 -> x12, waiting for transfers between devices: 87.6 us -> 48.1 us  [doubling_gather(): got = lax.ppermute(held, axis, [(i, i ^ step) for i in range(count)])]
    ppermute x18 -> x12, starting transfers between devices: 77.9 us -> 59.3 us  [doubling_gather(): got = lax.ppermute(held, axis, [(i, i ^ step) for i in range(count)])]
    reshape x0 -> x2, local copies, waits for them, and re-layouts: none -> 14.7 us  [precondition(): gathered = coarse_gather(residual).reshape(selection.shape[0], -1)]
    unnamed x101 -> x19, local copies, waits for them, and re-layouts: 8.81 us -> 0.78 us
    ppermute x18, starting transfers between devices: 118 us -> 111 us  [allsum(): lax.ppermute(value, axis, [(i, i ^ step) for i in range(count)])]
    dot_general x2, matrix products: 8.34 us -> 13.2 us  [precondition(): lax.dot_general(selection, gathered, (((0,), (0,)), ((), ())), preferred_...]
  transfers between devices with their start and end apart: 52 -> 48, of which waited for: 40 -> 38; matrix products, arithmetic and copies ran while one was open for 3% -> 1% of each run, Pallas kernels for 0% -> 0%
where the time goes in v7:
time: 484 us; the launch traced here: 480 us
  starting transfers between devices  209 us (43%)
  waiting for transfers between devices  145 us (30%)
  local copies, waits for them, and re-layouts  39 us (8%)
  blocking collectives  37.8 us (8%)
  matrix products  22.4 us (5%)
  between operations  16.4 us (3%)
  other arithmetic  10.6 us (2%)
    ppermute x18, starting transfers between devices, allsum(): lax.ppermute(value, axis, [(i, i ^ step) for i in range(count)])  111 us
    ppermute x12, starting transfers between devices, doubling_gather(): got = lax.ppermute(held, axis, [(i, i ^ step) for i in range(count)])  59.3 us
    all_gather x2, waiting for transfers between devices, doubling_gather(): lax.all_gather(held.reshape(-1, block.shape[-1]), 'gy', axis=0, tiled=True)  51.3 us
    ppermute x12, waiting for transfers between devices, doubling_gather(): got = lax.ppermute(held, axis, [(i, i ^ step) for i in range(count)])  48.1 us
    ppermute x18, waiting for transfers between devices, allsum(): lax.ppermute(value, axis, [(i, i ^ step) for i in range(count)])  41.1 us
    ppermute x16, starting transfers between devices, neighbours(): return (lax.ppermute(rows[1], axis, up), lax.ppermute(rows[0], axis, down))  38.3 us
    psum x3, blocking collectives, allsum(): value = lax.psum(value, 'gy')  37.8 us
    reshape x2, local copies, waits for them, and re-layouts, precondition(): placed.reshape(-1, system_count)  14.9 us
  transfers between devices with their start and end apart: 48, of which 38 were waited for; matrix products, arithmetic and copies ran while one was open for 1% of the time, Pallas kernels for 0%

profile of v7, /device:TPU:6, one launch (start us, length us, event | category | flops | bytes accessed | tf_op | source)
XLA Modules:
  0.0 480.1 jit_solution(6558370175424277475)
XLA Ops:
  8.2 14.3 %psum.35 = f32[128]{0:T(128)S(1)} all-reduce(f32[128]{0:T(128)S(1)} %multiply_reduce_fusion.10), channel_id=1, replica_groups=mesh['gx'=64,'gy'=8] {'gy'}, use_global_device_ids=true, to_apply=%region_1.0 | all-reduce | flops 128 | bytes 1024 | tf_op jit(solution)/shard_map/psum | solution.py:25
  29.9 5.0 %collective-permute-done.13 = f32[128]{0:T(128)S(1)} collective-permute-done((f32[128]{0:T(128)S(1)}, f32[128]{0:T(128)S(1)}, u32[]{:S(2)}, u32[]{:S(2)}) %collective-permute-start.13) | collective-permute-done | bytes 544 | tf_op jit(solution)/shard_map/ppermute | solution.py:33
  42.3 4.4 collective-permute-done.15
  46.7 5.7 %collective-permute-start.16 = (f32[128]{0:T(128)S(1)}, f32[128]{0:T(128)S(1)}, u32[]{:S(2)}, u32[]{:S(2)}) collective-permute-start(f32[128]{0:T(128)S(1)} %add.222), channel_id=1, source_target_pairs={{0,128},{8,136},{16,144},{24,152},{32,160},{40,168},{48,176},{56,1... | collective-permute-start | bytes 1544 | tf_op jit(solution)/shard_map/ppermute | solution.py:33
  52.4 3.7 collective-permute-done.16
  56.1 12.0 %collective-permute-start.17 = (f32[128]{0:T(128)S(1)}, f32[128]{0:T(128)S(1)}, u32[]{:S(2)}, u32[]{:S(2)}) collective-permute-start(f32[128]{0:T(128)S(1)} %add.223), channel_id=1, source_target_pairs={{0,256},{8,264},{16,272},{24,280},{32,288},{40,296},{48,304},{56,3... | collective-permute-start | bytes 1544 | tf_op jit(solution)/shard_map/ppermute | solution.py:33
  71.2 12.0 %collective-permute-start.22 = (bf16[1,32,128]{2,1,0:T(8,128)(2,1)S(1)}, bf16[1,32,128]{2,1,0:T(8,128)(2,1)S(1)}, u32[]{:S(2)}, u32[]{:S(2)}) collective-permute-start(bf16[1,32,128]{2,1,0:T(8,128)(2,1)S(1)} %fusion.2), channel_id=1, source_target_pairs={{0,256},{8,264},{16,272},{24,280},{32,288},{40,296},{48,304},{56,3... | collective-permute-start | bytes 24584 | tf_op jit(solution)/shard_map/ppermute | solution.py:52
  85.5 5.7 %collective-permute-start.23 = (bf16[2,32,128]{2,1,0:T(8,128)(2,1)S(1)}, bf16[2,32,128]{2,1,0:T(8,128)(2,1)S(1)}, u32[]{:S(2)}, u32[]{:S(2)}) collective-permute-start(bf16[2,32,128]{2,1,0:T(8,128)(2,1)S(1)} %maximum_select_fusion.10), channel_id=1, source_target_pairs={{0,128},{8,136},{16,144},{24,152},{32,160},{40,168},{48,176},{56,1... | collective-permute-start | bytes 49160 | tf_op jit(solution)/shard_map/ppermute | solution.py:52
  91.3 3.8 collective-permute-done.23
  97.9 4.0 collective-permute-done.24
  104.1 4.0 collective-permute-done.25
  108.1 4.4 collective-permute-start.26
  112.6 4.0 collective-permute-done.26
  119.3 6.3 %collective-permute-done.27 = bf16[32,32,128]{2,1,0:T(8,128)(2,1)S(1)} collective-permute-done((bf16[32,32,128]{2,1,0:T(8,128)(2,1)S(1)}, bf16[32,32,128]{2,1,0:T(8,128)(2,1)S(1)}, u32[]{:S(2)}, u32[]{:S(2)}) %collective-permute-start.27) | collective-permute-done | bytes 262176 | tf_op jit(solution)/shard_map/ppermute | solution.py:52
  133.5 3.6 collective-permute-start.21
  141.1 25.2 %all-gather.3.cloned.1.call-done = bf16[16384,128]{1,0:T(8,128)(2,1)} async-done(((bf16[2048,128]{1,0:T(8,128)(2,1)}), bf16[16384,128]{1,0:T(8,128)(2,1)}) %all-gather.3.cloned.1.call-update) | async-done | bytes 4194320 | tf_op jit(solution)/shard_map/all_gather | solution.py:57
  166.3 7.4 %reshape.132 = bf16[512,4096]{1,0:T(8,128)(2,1)} reshape(bf16[16384,128]{1,0:T(8,128)(2,1)} %all-gather.3.cloned.1.call-done) | data formatting | bytes 8388608 | tf_op jit(solution)/shard_map/reshape | solution.py:126
  173.6 6.6 %convolution_convert_fusion.1 = bf16[512,4096]{1,0:T(8,128)(2,1)} fusion(bf16[512,4096]{1,0:T(8,128)(2,1)} %reshape.132, s32[512]{0:T(512)S(1)} %gather_fusion.1), kind=kOutput, calls=%fused_computation.10 | convolution fusion | flops 2149842944 | bytes 8390656 | tf_op jit(solution)/shard_map/dot_general | solution.py:127
  180.2 7.5 %reshape.133 = bf16[16384,128]{1,0:T(8,128)(2,1)} reshape(bf16[512,4096]{1,0:T(8,128)(2,1)} %convolution_convert_fusion.1) | data formatting | bytes 8388608 | tf_op jit(solution)/shard_map/reshape | solution.py:131
  187.7 3.6 convolution_add_fusion.1
  199.5 3.6 collective-permute-start.31
  207.3 11.7 %psum.36 = f32[3,128]{1,0:T(4,128)S(1)} all-reduce(f32[3,128]{1,0:T(4,128)S(1)} %pad_maximum_fusion.4), channel_id=1, replica_groups=mesh['gx'=64,'gy'=8] {'gy'}, use_global_device_ids=true, to_apply=%region_6.7 | all-reduce | flops 384 | bytes 3072 | tf_op jit(solution)/shard_map/psum | solution.py:25
  219.1 4.3 collective-permute-start.32
  224.9 5.4 %collective-permute-start.33 = (f32[3,128]{1,0:T(4,128)S(1)}, f32[3,128]{1,0:T(4,128)S(1)}, u32[]{:S(2)}, u32[]{:S(2)}) collective-permute-start(f32[3,128]{1,0:T(4,128)S(1)} %add.237), channel_id=1, source_target_pairs={{0,16},{8,24},{16,0},{24,8},{32,48},{40,56},{48,32},{56,40},{64,80... | collective-permute-start | bytes 4616 | tf_op jit(solution)/shard_map/ppermute | solution.py:33
  231.9 6.1 %collective-permute-start.34 = (f32[3,128]{1,0:T(4,128)S(1)}, f32[3,128]{1,0:T(4,128)S(1)}, u32[]{:S(2)}, u32[]{:S(2)}) collective-permute-start(f32[3,128]{1,0:T(4,128)S(1)} %add.238), channel_id=1, source_target_pairs={{0,32},{8,40},{16,48},{24,56},{32,0},{40,8},{48,16},{56,24},{64,96... | collective-permute-start | bytes 4616 | tf_op jit(solution)/shard_map/ppermute | solution.py:33
  239.5 4.9 %collective-permute-start.35 = (f32[3,128]{1,0:T(4,128)S(1)}, f32[3,128]{1,0:T(4,128)S(1)}, u32[]{:S(2)}, u32[]{:S(2)}) collective-permute-start(f32[3,128]{1,0:T(4,128)S(1)} %add.239), channel_id=1, source_target_pairs={{0,64},{8,72},{16,80},{24,88},{32,96},{40,104},{48,112},{56,120},{... | collective-permute-start | bytes 4616 | tf_op jit(solution)/shard_map/ppermute | solution.py:33
  246.0 9.2 %collective-permute-start.36 = (f32[3,128]{1,0:T(4,128)S(1)}, f32[3,128]{1,0:T(4,128)S(1)}, u32[]{:S(2)}, u32[]{:S(2)}) collective-permute-start(f32[3,128]{1,0:T(4,128)S(1)} %add.240), channel_id=1, source_target_pairs={{0,128},{8,136},{16,144},{24,152},{32,160},{40,168},{48,176},{56,1... | collective-permute-start | bytes 4616 | tf_op jit(solution)/shard_map/ppermute | solution.py:33
  256.7 13.0 %collective-permute-start.37 = (f32[3,128]{1,0:T(4,128)S(1)}, f32[3,128]{1,0:T(4,128)S(1)}, u32[]{:S(2)}, u32[]{:S(2)}) collective-permute-start(f32[3,128]{1,0:T(4,128)S(1)} %add.241), channel_id=1, source_target_pairs={{0,256},{8,264},{16,272},{24,280},{32,288},{40,296},{48,304},{56,3... | collective-permute-start | bytes 4616 | tf_op jit(solution)/shard_map/ppermute | solution.py:33
  272.8 12.6 %collective-permute-start.42 = (bf16[1,32,128]{2,1,0:T(8,128)(2,1)S(1)}, bf16[1,32,128]{2,1,0:T(8,128)(2,1)S(1)}, u32[]{:S(2)}, u32[]{:S(2)}) collective-permute-start(bf16[1,32,128]{2,1,0:T(8,128)(2,1)S(1)} %fusion.3), channel_id=1, source_target_pairs={{0,256},{8,264},{16,272},{24,280},{32,288},{40,296},{48,304},{56,3... | collective-permute-start | bytes 24584 | tf_op jit(solution)/shard_map/ppermute | solution.py:52
  287.1 7.5 %collective-permute-start.43 = (bf16[2,32,128]{2,1,0:T(8,128)(2,1)S(1)}, bf16[2,32,128]{2,1,0:T(8,128)(2,1)S(1)}, u32[]{:S(2)}, u32[]{:S(2)}) collective-permute-start(bf16[2,32,128]{2,1,0:T(8,128)(2,1)S(1)} %maximum_select_fusion.11), channel_id=1, source_target_pairs={{0,128},{8,136},{16,144},{24,152},{32,160},{40,168},{48,176},{56,1... | collective-permute-start | bytes 49160 | tf_op jit(solution)/shard_map/ppermute | solution.py:52
  299.7 3.6 collective-permute-done.44
  305.4 4.1 collective-permute-done.45
  311.9 6.0 %collective-permute-done.46 = bf16[16,32,128]{2,1,0:T(8,128)(2,1)S(1)} collective-permute-done((bf16[16,32,128]{2,1,0:T(8,128)(2,1)S(1)}, bf16[16,32,128]{2,1,0:T(8,128)(2,1)S(1)}, u32[]{:S(2)}, u32[]{:S(2)}) %collective-permute-start.46) | collective-permute-done | bytes 131104 | tf_op jit(solution)/shard_map/ppermute | solution.py:52
  319.9 6.3 %collective-permute-done.47 = bf16[32,32,128]{2,1,0:T(8,128)(2,1)S(1)} collective-permute-done((bf16[32,32,128]{2,1,0:T(8,128)(2,1)S(1)}, bf16[32,32,128]{2,1,0:T(8,128)(2,1)S(1)}, u32[]{:S(2)}, u32[]{:S(2)}) %collective-permute-start.47) | collective-permute-done | bytes 262176 | tf_op jit(solution)/shard_map/ppermute | solution.py:52
  333.4 3.8 collective-permute-start.41
  339.3 26.1 %all-gather.5.cloned.1.call-done = bf16[16384,128]{1,0:T(8,128)(2,1)} async-done(((bf16[2048,128]{1,0:T(8,128)(2,1)}), bf16[16384,128]{1,0:T(8,128)(2,1)}) %all-gather.5.cloned.1.call-update) | async-done | bytes 4194320 | tf_op jit(solution)/shard_map/all_gather | solution.py:57
  365.4 7.4 %reshape.135 = bf16[512,4096]{1,0:T(8,128)(2,1)} reshape(bf16[16384,128]{1,0:T(8,128)(2,1)} %all-gather.5.cloned.1.call-done) | data formatting | bytes 8388608 | tf_op jit(solution)/shard_map/reshape | solution.py:126
  372.8 6.6 %convolution_convert_fusion = bf16[512,4096]{1,0:T(8,128)(2,1)} fusion(bf16[512,4096]{1,0:T(8,128)(2,1)} %reshape.135, s32[512]{0:T(512)S(1)} %gather_fusion.1), kind=kOutput, calls=%fused_computation.9 | convolution fusion | flops 2149842944 | bytes 8390656 | tf_op jit(solution)/shard_map/dot_general | solution.py:127
  379.4 7.4 %reshape.136 = bf16[16384,128]{1,0:T(8,128)(2,1)} reshape(bf16[512,4096]{1,0:T(8,128)(2,1)} %convolution_convert_fusion) | data formatting | bytes 8388608 | tf_op jit(solution)/shard_map/reshape | solution.py:131
  386.8 3.6 convolution_add_fusion
  398.5 3.6 collective-permute-start.51
  406.4 11.7 %psum.37 = f32[6,128]{1,0:T(8,128)S(1)} all-reduce(f32[6,128]{1,0:T(8,128)S(1)} %stack.126), channel_id=1, replica_groups=mesh['gx'=64,'gy'=8] {'gy'}, use_global_device_ids=true, to_apply=%region_18.19 | all-reduce | flops 768 | bytes 6144 | tf_op jit(solution)/shard_map/psum | solution.py:25
  418.1 4.3 collective-permute-start.52
  424.0 5.4 %collective-permute-start.53 = (f32[6,128]{1,0:T(8,128)S(1)}, f32[6,128]{1,0:T(8,128)S(1)}, u32[]{:S(2)}, u32[]{:S(2)}) collective-permute-start(f32[6,128]{1,0:T(8,128)S(1)} %add.247), channel_id=1, source_target_pairs={{0,16},{8,24},{16,0},{24,8},{32,48},{40,56},{48,32},{56,40},{64,80... | collective-permute-start | bytes 9224 | tf_op jit(solution)/shard_map/ppermute | solution.py:33
  431.0 6.1 %collective-permute-start.54 = (f32[6,128]{1,0:T(8,128)S(1)}, f32[6,128]{1,0:T(8,128)S(1)}, u32[]{:S(2)}, u32[]{:S(2)}) collective-permute-start(f32[6,128]{1,0:T(8,128)S(1)} %add.248), channel_id=1, source_target_pairs={{0,32},{8,40},{16,48},{24,56},{32,0},{40,8},{48,16},{56,24},{64,96... | collective-permute-start | bytes 9224 | tf_op jit(solution)/shard_map/ppermute | solution.py:33
  438.6 4.9 %collective-permute-start.55 = (f32[6,128]{1,0:T(8,128)S(1)}, f32[6,128]{1,0:T(8,128)S(1)}, u32[]{:S(2)}, u32[]{:S(2)}) collective-permute-start(f32[6,128]{1,0:T(8,128)S(1)} %add.249), channel_id=1, source_target_pairs={{0,64},{8,72},{16,80},{24,88},{32,96},{40,104},{48,112},{56,120},{... | collective-permute-start | bytes 9224 | tf_op jit(solution)/shard_map/ppermute | solution.py:33
  445.1 9.2 %collective-permute-start.56 = (f32[6,128]{1,0:T(8,128)S(1)}, f32[6,128]{1,0:T(8,128)S(1)}, u32[]{:S(2)}, u32[]{:S(2)}) collective-permute-start(f32[6,128]{1,0:T(8,128)S(1)} %add.250), channel_id=1, source_target_pairs={{0,128},{8,136},{16,144},{24,152},{32,160},{40,168},{48,176},{56,1... | collective-permute-start | bytes 9224 | tf_op jit(solution)/shard_map/ppermute | solution.py:33
  455.9 13.0 %collective-permute-start.57 = (f32[6,128]{1,0:T(8,128)S(1)}, f32[6,128]{1,0:T(8,128)S(1)}, u32[]{:S(2)}, u32[]{:S(2)}) collective-permute-start(f32[6,128]{1,0:T(8,128)S(1)} %add.251), channel_id=1, source_target_pairs={{0,256},{8,264},{16,272},{24,280},{32,288},{40,296},{48,304},{56,3... | collective-permute-start | bytes 9224 | tf_op jit(solution)/shard_map/ppermute | solution.py:33
  (157 shorter events, 109.1 us)
Async XLA Ops:
  7.2 159.1 %all-gather.3.cloned.1.call-start = ((), (), s32[]{:S(2)}) async-start(), calls=%async_computation | async-start | bytes 4718592 | tf_op jit(solution)/shard_map/all_gather | solution.py:57
  22.5 5.5 %collective-permute-start.12 = (f32[128]{0:T(128)S(1)}, f32[128]{0:T(128)S(1)}, u32[]{:S(2)}, u32[]{:S(2)}) collective-permute-start(f32[128]{0:T(128)S(1)} %psum.35), channel_id=1, source_target_pairs={{0,8},{8,0},{16,24},{24,16},{32,40},{40,32},{48,56},{56,48},{64,72... | collective-permute-start | bytes 1544 | tf_op jit(solution)/shard_map/ppermute | solution.py:33
  27.9 7.0 %collective-permute-start.13 = (f32[128]{0:T(128)S(1)}, f32[128]{0:T(128)S(1)}, u32[]{:S(2)}, u32[]{:S(2)}) collective-permute-start(f32[128]{0:T(128)S(1)} %add.219), channel_id=1, source_target_pairs={{0,16},{8,24},{16,0},{24,8},{32,48},{40,56},{48,32},{56,40},{64,80... | collective-permute-start | bytes 1544 | tf_op jit(solution)/shard_map/ppermute | solution.py:33
  34.9 5.5 %collective-permute-start.14 = (f32[128]{0:T(128)S(1)}, f32[128]{0:T(128)S(1)}, u32[]{:S(2)}, u32[]{:S(2)}) collective-permute-start(f32[128]{0:T(128)S(1)} %add.220), channel_id=1, source_target_pairs={{0,32},{8,40},{16,48},{24,56},{32,0},{40,8},{48,16},{56,24},{64,96... | collective-permute-start | bytes 1544 | tf_op jit(solution)/shard_map/ppermute | solution.py:33
  40.4 6.3 %collective-permute-start.15 = (f32[128]{0:T(128)S(1)}, f32[128]{0:T(128)S(1)}, u32[]{:S(2)}, u32[]{:S(2)}) collective-permute-start(f32[128]{0:T(128)S(1)} %add.221), channel_id=1, source_target_pairs={{0,64},{8,72},{16,80},{24,88},{32,96},{40,104},{48,112},{56,120},{... | collective-permute-start | bytes 1544 | tf_op jit(solution)/shard_map/ppermute | solution.py:33
  46.7 9.4 %collective-permute-start.16 = (f32[128]{0:T(128)S(1)}, f32[128]{0:T(128)S(1)}, u32[]{:S(2)}, u32[]{:S(2)}) collective-permute-start(f32[128]{0:T(128)S(1)} %add.222), channel_id=1, source_target_pairs={{0,128},{8,136},{16,144},{24,152},{32,160},{40,168},{48,176},{56,1... | collective-permute-start | bytes 1544 | tf_op jit(solution)/shard_map/ppermute | solution.py:33
  56.1 14.2 %collective-permute-start.17 = (f32[128]{0:T(128)S(1)}, f32[128]{0:T(128)S(1)}, u32[]{:S(2)}, u32[]{:S(2)}) collective-permute-start(f32[128]{0:T(128)S(1)} %add.223), channel_id=1, source_target_pairs={{0,256},{8,264},{16,272},{24,280},{32,288},{40,296},{48,304},{56,3... | collective-permute-start | bytes 1544 | tf_op jit(solution)/shard_map/ppermute | solution.py:33
  71.2 14.3 %collective-permute-start.22 = (bf16[1,32,128]{2,1,0:T(8,128)(2,1)S(1)}, bf16[1,32,128]{2,1,0:T(8,128)(2,1)S(1)}, u32[]{:S(2)}, u32[]{:S(2)}) collective-permute-start(bf16[1,32,128]{2,1,0:T(8,128)(2,1)S(1)} %fusion.2), channel_id=1, source_target_pairs={{0,256},{8,264},{16,272},{24,280},{32,288},{40,296},{48,304},{56,3... | collective-permute-start | bytes 24584 | tf_op jit(solution)/shard_map/ppermute | solution.py:52
  85.5 9.5 %collective-permute-start.23 = (bf16[2,32,128]{2,1,0:T(8,128)(2,1)S(1)}, bf16[2,32,128]{2,1,0:T(8,128)(2,1)S(1)}, u32[]{:S(2)}, u32[]{:S(2)}) collective-permute-start(bf16[2,32,128]{2,1,0:T(8,128)(2,1)S(1)} %maximum_select_fusion.10), channel_id=1, source_target_pairs={{0,128},{8,136},{16,144},{24,152},{32,160},{40,168},{48,176},{56,1... | collective-permute-start | bytes 49160 | tf_op jit(solution)/shard_map/ppermute | solution.py:52
  95.0 6.8 %collective-permute-start.24 = (bf16[4,32,128]{2,1,0:T(8,128)(2,1)S(1)}, bf16[4,32,128]{2,1,0:T(8,128)(2,1)S(1)}, u32[]{:S(2)}, u32[]{:S(2)}) collective-permute-start(bf16[4,32,128]{2,1,0:T(8,128)(2,1)S(1)} %maximum_select_fusion.8), channel_id=1, source_target_pairs={{0,64},{8,72},{16,80},{24,88},{32,96},{40,104},{48,112},{56,120},{... | collective-permute-start | bytes 98312 | tf_op jit(solution)/shard_map/ppermute | solution.py:52
  101.9 6.2 %collective-permute-start.25 = (bf16[8,32,128]{2,1,0:T(8,128)(2,1)S(1)}, bf16[8,32,128]{2,1,0:T(8,128)(2,1)S(1)}, u32[]{:S(2)}, u32[]{:S(2)}) collective-permute-start(bf16[8,32,128]{2,1,0:T(8,128)(2,1)S(1)} %maximum_select_fusion.6), channel_id=1, source_target_pairs={{0,32},{8,40},{16,48},{24,56},{32,0},{40,8},{48,16},{56,24},{64,96... | collective-permute-start | bytes 196616 | tf_op jit(solution)/shard_map/ppermute | solution.py:52
  108.1 8.5 %collective-permute-start.26 = (bf16[16,32,128]{2,1,0:T(8,128)(2,1)S(1)}, bf16[16,32,128]{2,1,0:T(8,128)(2,1)S(1)}, u32[]{:S(2)}, u32[]{:S(2)}) collective-permute-start(bf16[16,32,128]{2,1,0:T(8,128)(2,1)S(1)} %maximum_select_fusion.4), channel_id=1, source_target_pairs={{0,16},{8,24},{16,0},{24,8},{32,48},{40,56},{48,32},{56,40},{64,80... | collective-permute-start | bytes 393224 | tf_op jit(solution)/shard_map/ppermute | solution.py:52
  116.6 9.0 %collective-permute-start.27 = (bf16[32,32,128]{2,1,0:T(8,128)(2,1)S(1)}, bf16[32,32,128]{2,1,0:T(8,128)(2,1)S(1)}, u32[]{:S(2)}, u32[]{:S(2)}) collective-permute-start(bf16[32,32,128]{2,1,0:T(8,128)(2,1)S(1)} %maximum_select_fusion.2), channel_id=1, source_target_pairs={{0,8},{8,0},{16,24},{24,16},{32,40},{40,32},{48,56},{56,48},{64,72... | collective-permute-start | bytes 786440 | tf_op jit(solution)/shard_map/ppermute | solution.py:52
  126.5 238.9 %all-gather.5.cloned.1.call-start = ((), (), s32[]{:S(2)}) async-start(), calls=%async_computation.1 | async-start | bytes 4718592 | tf_op jit(solution)/shard_map/all_gather | solution.py:57
  128.3 12.4 %collective-permute-start.18 = (f32[128,128]{1,0:T(8,128)S(1)}, f32[128,128]{1,0:T(8,128)S(1)}, u32[]{:S(2)}, u32[]{:S(2)}) collective-permute-start(f32[128,128]{1,0:T(8,128)S(1)} %get-tuple-element.64), channel_id=1, source_target_pairs={{0,8},{8,16},{16,24},{24,32},{32,40},{40,48},{48,56},{56,64},{64,7... | collective-permute-start | bytes 196616 | tf_op jit(solution)/shard_map/ppermute | solution.py:15
  130.3 10.4 %collective-permute-start.20 = (f32[128,128]{1,0:T(8,128)S(1)}, f32[128,128]{1,0:T(8,128)S(1)}, u32[]{:S(2)}, u32[]{:S(2)}) collective-permute-start(f32[128,128]{1,0:T(8,128)S(1)} %get-tuple-element.65), channel_id=1, source_target_pairs={{0,1},{1,2},{2,3},{3,4},{4,5},{5,6},{6,7},{8,9},{9,10},{10,11},{11... | collective-permute-start | bytes 196616 | tf_op jit(solution)/shard_map/ppermute | solution.py:15
  132.2 8.5 %collective-permute-start.19 = (f32[128,128]{1,0:T(8,128)S(1)}, f32[128,128]{1,0:T(8,128)S(1)}, u32[]{:S(2)}, u32[]{:S(2)}) collective-permute-start(f32[128,128]{1,0:T(8,128)S(1)} %get-tuple-element.66), channel_id=1, source_target_pairs={{8,0},{16,8},{24,16},{32,24},{40,32},{48,40},{56,48},{64,56},{72,6... | collective-permute-start | bytes 196616 | tf_op jit(solution)/shard_map/ppermute | solution.py:15
  133.5 7.2 %collective-permute-start.21 = (f32[128,128]{1,0:T(8,128)S(1)}, f32[128,128]{1,0:T(8,128)S(1)}, u32[]{:S(2)}, u32[]{:S(2)}) collective-permute-start(f32[128,128]{1,0:T(8,128)S(1)} %get-tuple-element.67), channel_id=1, source_target_pairs={{1,0},{2,1},{3,2},{4,3},{5,4},{6,5},{7,6},{9,8},{10,9},{11,10},{12... | collective-permute-start | bytes 196616 | tf_op jit(solution)/shard_map/ppermute | solution.py:15
  192.8 10.3 %collective-permute-start.28 = (bf16[128,128]{1,0:T(8,128)(2,1)S(1)}, bf16[128,128]{1,0:T(8,128)(2,1)S(1)}, u32[]{:S(2)}, u32[]{:S(2)}) collective-permute-start(bf16[128,128]{1,0:T(8,128)(2,1)S(1)} %get-tuple-element.72), channel_id=1, source_target_pairs={{0,8},{8,16},{16,24},{24,32},{32,40},{40,48},{48,56},{56,64},{64,7... | collective-permute-start | bytes 98312 | tf_op jit(solution)/shard_map/ppermute | solution.py:15
  196.2 6.9 %collective-permute-start.30 = (bf16[128,128]{1,0:T(8,128)(2,1)S(1)}, bf16[128,128]{1,0:T(8,128)(2,1)S(1)}, u32[]{:S(2)}, u32[]{:S(2)}) collective-permute-start(bf16[128,128]{1,0:T(8,128)(2,1)S(1)} %get-tuple-element.73), channel_id=1, source_target_pairs={{0,1},{1,2},{2,3},{3,4},{4,5},{5,6},{6,7},{8,9},{9,10},{10,11},{11... | collective-permute-start | bytes 98312 | tf_op jit(solution)/shard_map/ppermute | solution.py:15
  198.2 5.8 %collective-permute-start.29 = (bf16[128,128]{1,0:T(8,128)(2,1)S(1)}, bf16[128,128]{1,0:T(8,128)(2,1)S(1)}, u32[]{:S(2)}, u32[]{:S(2)}) collective-permute-start(bf16[128,128]{1,0:T(8,128)(2,1)S(1)} %get-tuple-element.74), channel_id=1, source_target_pairs={{8,0},{16,8},{24,16},{32,24},{40,32},{48,40},{56,48},{64,56},{72,6... | collective-permute-start | bytes 98312 | tf_op jit(solution)/shard_map/ppermute | solution.py:15
  199.5 5.2 %collective-permute-start.31 = (bf16[128,128]{1,0:T(8,128)(2,1)S(1)}, bf16[128,128]{1,0:T(8,128)(2,1)S(1)}, u32[]{:S(2)}, u32[]{:S(2)}) collective-permute-start(bf16[128,128]{1,0:T(8,128)(2,1)S(1)} %get-tuple-element.75), channel_id=1, source_target_pairs={{1,0},{2,1},{3,2},{4,3},{5,4},{6,5},{7,6},{9,8},{10,9},{11,10},{12... | collective-permute-start | bytes 98312 | tf_op jit(solution)/shard_map/ppermute | solution.py:15
  219.1 5.8 %collective-permute-start.32 = (f32[3,128]{1,0:T(4,128)S(1)}, f32[3,128]{1,0:T(4,128)S(1)}, u32[]{:S(2)}, u32[]{:S(2)}) collective-permute-start(f32[3,128]{1,0:T(4,128)S(1)} %psum.36), channel_id=1, source_target_pairs={{0,8},{8,0},{16,24},{24,16},{32,40},{40,32},{48,56},{56,48},{64,72... | collective-permute-start | bytes 4616 | tf_op jit(solution)/shard_map/ppermute | solution.py:33
  224.9 7.0 %collective-permute-start.33 = (f32[3,128]{1,0:T(4,128)S(1)}, f32[3,128]{1,0:T(4,128)S(1)}, u32[]{:S(2)}, u32[]{:S(2)}) collective-permute-start(f32[3,128]{1,0:T(4,128)S(1)} %add.237), channel_id=1, source_target_pairs={{0,16},{8,24},{16,0},{24,8},{32,48},{40,56},{48,32},{56,40},{64,80... | collective-permute-start | bytes 4616 | tf_op jit(solution)/shard_map/ppermute | solution.py:33
  231.9 7.6 %collective-permute-start.34 = (f32[3,128]{1,0:T(4,128)S(1)}, f32[3,128]{1,0:T(4,128)S(1)}, u32[]{:S(2)}, u32[]{:S(2)}) collective-permute-start(f32[3,128]{1,0:T(4,128)S(1)} %add.238), channel_id=1, source_target_pairs={{0,32},{8,40},{16,48},{24,56},{32,0},{40,8},{48,16},{56,24},{64,96... | collective-permute-start | bytes 4616 | tf_op jit(solution)/shard_map/ppermute | solution.py:33
  239.5 6.5 %collective-permute-start.35 = (f32[3,128]{1,0:T(4,128)S(1)}, f32[3,128]{1,0:T(4,128)S(1)}, u32[]{:S(2)}, u32[]{:S(2)}) collective-permute-start(f32[3,128]{1,0:T(4,128)S(1)} %add.239), channel_id=1, source_target_pairs={{0,64},{8,72},{16,80},{24,88},{32,96},{40,104},{48,112},{56,120},{... | collective-permute-start | bytes 4616 | tf_op jit(solution)/shard_map/ppermute | solution.py:33
  246.0 10.8 %collective-permute-start.36 = (f32[3,128]{1,0:T(4,128)S(1)}, f32[3,128]{1,0:T(4,128)S(1)}, u32[]{:S(2)}, u32[]{:S(2)}) collective-permute-start(f32[3,128]{1,0:T(4,128)S(1)} %add.240), channel_id=1, source_target_pairs={{0,128},{8,136},{16,144},{24,152},{32,160},{40,168},{48,176},{56,1... | collective-permute-start | bytes 4616 | tf_op jit(solution)/shard_map/ppermute | solution.py:33
  256.7 14.5 %collective-permute-start.37 = (f32[3,128]{1,0:T(4,128)S(1)}, f32[3,128]{1,0:T(4,128)S(1)}, u32[]{:S(2)}, u32[]{:S(2)}) collective-permute-start(f32[3,128]{1,0:T(4,128)S(1)} %add.241), channel_id=1, source_target_pairs={{0,256},{8,264},{16,272},{24,280},{32,288},{40,296},{48,304},{56,3... | collective-permute-start | bytes 4616 | tf_op jit(solution)/shard_map/ppermute | solution.py:33
  272.8 14.3 %collective-permute-start.42 = (bf16[1,32,128]{2,1,0:T(8,128)(2,1)S(1)}, bf16[1,32,128]{2,1,0:T(8,128)(2,1)S(1)}, u32[]{:S(2)}, u32[]{:S(2)}) collective-permute-start(bf16[1,32,128]{2,1,0:T(8,128)(2,1)S(1)} %fusion.3), channel_id=1, source_target_pairs={{0,256},{8,264},{16,272},{24,280},{32,288},{40,296},{48,304},{56,3... | collective-permute-start | bytes 24584 | tf_op jit(solution)/shard_map/ppermute | solution.py:52
  287.1 9.5 %collective-permute-start.43 = (bf16[2,32,128]{2,1,0:T(8,128)(2,1)S(1)}, bf16[2,32,128]{2,1,0:T(8,128)(2,1)S(1)}, u32[]{:S(2)}, u32[]{:S(2)}) collective-permute-start(bf16[2,32,128]{2,1,0:T(8,128)(2,1)S(1)} %maximum_select_fusion.11), channel_id=1, source_target_pairs={{0,128},{8,136},{16,144},{24,152},{32,160},{40,168},{48,176},{56,1... | collective-permute-start | bytes 49160 | tf_op jit(solution)/shard_map/ppermute | solution.py:52
  296.6 6.7 %collective-permute-start.44 = (bf16[4,32,128]{2,1,0:T(8,128)(2,1)S(1)}, bf16[4,32,128]{2,1,0:T(8,128)(2,1)S(1)}, u32[]{:S(2)}, u32[]{:S(2)}) collective-permute-start(bf16[4,32,128]{2,1,0:T(8,128)(2,1)S(1)} %maximum_select_fusion.9), channel_id=1, source_target_pairs={{0,64},{8,72},{16,80},{24,88},{32,96},{40,104},{48,112},{56,120},{... | collective-permute-start | bytes 98312 | tf_op jit(solution)/shard_map/ppermute | solution.py:52
  303.3 6.2 %collective-permute-start.45 = (bf16[8,32,128]{2,1,0:T(8,128)(2,1)S(1)}, bf16[8,32,128]{2,1,0:T(8,128)(2,1)S(1)}, u32[]{:S(2)}, u32[]{:S(2)}) collective-permute-start(bf16[8,32,128]{2,1,0:T(8,128)(2,1)S(1)} %maximum_select_fusion.7), channel_id=1, source_target_pairs={{0,32},{8,40},{16,48},{24,56},{32,0},{40,8},{48,16},{56,24},{64,96... | collective-permute-start | bytes 196616 | tf_op jit(solution)/shard_map/ppermute | solution.py:52
  309.5 8.4 %collective-permute-start.46 = (bf16[16,32,128]{2,1,0:T(8,128)(2,1)S(1)}, bf16[16,32,128]{2,1,0:T(8,128)(2,1)S(1)}, u32[]{:S(2)}, u32[]{:S(2)}) collective-permute-start(bf16[16,32,128]{2,1,0:T(8,128)(2,1)S(1)} %maximum_select_fusion.5), channel_id=1, source_target_pairs={{0,16},{8,24},{16,0},{24,8},{32,48},{40,56},{48,32},{56,40},{64,80... | collective-permute-start | bytes 393224 | tf_op jit(solution)/shard_map/ppermute | solution.py:52
  317.9 8.4 %collective-permute-start.47 = (bf16[32,32,128]{2,1,0:T(8,128)(2,1)S(1)}, bf16[32,32,128]{2,1,0:T(8,128)(2,1)S(1)}, u32[]{:S(2)}, u32[]{:S(2)}) collective-permute-start(bf16[32,32,128]{2,1,0:T(8,128)(2,1)S(1)} %maximum_select_fusion.3), channel_id=1, source_target_pairs={{0,8},{8,0},{16,24},{24,16},{32,40},{40,32},{48,56},{56,48},{64,72... | collective-permute-start | bytes 786440 | tf_op jit(solution)/shard_map/ppermute | solution.py:52
  328.3 9.0 %collective-permute-start.38 = (f32[128,128]{1,0:T(8,128)S(1)}, f32[128,128]{1,0:T(8,128)S(1)}, u32[]{:S(2)}, u32[]{:S(2)}) collective-permute-start(f32[128,128]{1,0:T(8,128)S(1)} %get-tuple-element.60), channel_id=1, source_target_pairs={{0,8},{8,16},{16,24},{24,32},{32,40},{40,48},{48,56},{56,64},{64,7... | collective-permute-start | bytes 196616 | tf_op jit(solution)/shard_map/ppermute | solution.py:15
  330.2 7.1 %collective-permute-start.40 = (f32[128,128]{1,0:T(8,128)S(1)}, f32[128,128]{1,0:T(8,128)S(1)}, u32[]{:S(2)}, u32[]{:S(2)}) collective-permute-start(f32[128,128]{1,0:T(8,128)S(1)} %get-tuple-element.61), channel_id=1, source_target_pairs={{0,1},{1,2},{2,3},{3,4},{4,5},{5,6},{6,7},{8,9},{9,10},{10,11},{11... | collective-permute-start | bytes 196616 | tf_op jit(solution)/shard_map/ppermute | solution.py:15
  332.1 6.2 %collective-permute-start.39 = (f32[128,128]{1,0:T(8,128)S(1)}, f32[128,128]{1,0:T(8,128)S(1)}, u32[]{:S(2)}, u32[]{:S(2)}) collective-permute-start(f32[128,128]{1,0:T(8,128)S(1)} %get-tuple-element.62), channel_id=1, source_target_pairs={{8,0},{16,8},{24,16},{32,24},{40,32},{48,40},{56,48},{64,56},{72,6... | collective-permute-start | bytes 196616 | tf_op jit(solution)/shard_map/ppermute | solution.py:15
  333.4 5.5 %collective-permute-start.41 = (f32[128,128]{1,0:T(8,128)S(1)}, f32[128,128]{1,0:T(8,128)S(1)}, u32[]{:S(2)}, u32[]{:S(2)}) collective-permute-start(f32[128,128]{1,0:T(8,128)S(1)} %get-tuple-element.63), channel_id=1, source_target_pairs={{1,0},{2,1},{3,2},{4,3},{5,4},{6,5},{7,6},{9,8},{10,9},{11,10},{12... | collective-permute-start | bytes 196616 | tf_op jit(solution)/shard_map/ppermute | solution.py:15
  391.9 10.3 %collective-permute-start.48 = (bf16[128,128]{1,0:T(8,128)(2,1)S(1)}, bf16[128,128]{1,0:T(8,128)(2,1)S(1)}, u32[]{:S(2)}, u32[]{:S(2)}) collective-permute-start(bf16[128,128]{1,0:T(8,128)(2,1)S(1)} %get-tuple-element.68), channel_id=1, source_target_pairs={{0,8},{8,16},{16,24},{24,32},{32,40},{40,48},{48,56},{56,64},{64,7... | collective-permute-start | bytes 98312 | tf_op jit(solution)/shard_map/ppermute | solution.py:15
  395.3 6.9 %collective-permute-start.50 = (bf16[128,128]{1,0:T(8,128)(2,1)S(1)}, bf16[128,128]{1,0:T(8,128)(2,1)S(1)}, u32[]{:S(2)}, u32[]{:S(2)}) collective-permute-start(bf16[128,128]{1,0:T(8,128)(2,1)S(1)} %get-tuple-element.69), channel_id=1, source_target_pairs={{0,1},{1,2},{2,3},{3,4},{4,5},{5,6},{6,7},{8,9},{9,10},{10,11},{11... | collective-permute-start | bytes 98312 | tf_op jit(solution)/shard_map/ppermute | solution.py:15
  397.2 5.8 %collective-permute-start.49 = (bf16[128,128]{1,0:T(8,128)(2,1)S(1)}, bf16[128,128]{1,0:T(8,128)(2,1)S(1)}, u32[]{:S(2)}, u32[]{:S(2)}) collective-permute-start(bf16[128,128]{1,0:T(8,128)(2,1)S(1)} %get-tuple-element.70), channel_id=1, source_target_pairs={{8,0},{16,8},{24,16},{32,24},{40,32},{48,40},{56,48},{64,56},{72,6... | collective-permute-start | bytes 98312 | tf_op jit(solution)/shard_map/ppermute | solution.py:15
  398.5 5.2 %collective-permute-start.51 = (bf16[128,128]{1,0:T(8,128)(2,1)S(1)}, bf16[128,128]{1,0:T(8,128)(2,1)S(1)}, u32[]{:S(2)}, u32[]{:S(2)}) collective-permute-start(bf16[128,128]{1,0:T(8,128)(2,1)S(1)} %get-tuple-element.71), channel_id=1, source_target_pairs={{1,0},{2,1},{3,2},{4,3},{5,4},{6,5},{7,6},{9,8},{10,9},{11,10},{12... | collective-permute-start | bytes 98312 | tf_op jit(solution)/shard_map/ppermute | solution.py:15
  418.1 5.8 %collective-permute-start.52 = (f32[6,128]{1,0:T(8,128)S(1)}, f32[6,128]{1,0:T(8,128)S(1)}, u32[]{:S(2)}, u32[]{:S(2)}) collective-permute-start(f32[6,128]{1,0:T(8,128)S(1)} %psum.37), channel_id=1, source_target_pairs={{0,8},{8,0},{16,24},{24,16},{32,40},{40,32},{48,56},{56,48},{64,72... | collective-permute-start | bytes 9224 | tf_op jit(solution)/shard_map/ppermute | solution.py:33
  424.0 7.0 %collective-permute-start.53 = (f32[6,128]{1,0:T(8,128)S(1)}, f32[6,128]{1,0:T(8,128)S(1)}, u32[]{:S(2)}, u32[]{:S(2)}) collective-permute-start(f32[6,128]{1,0:T(8,128)S(1)} %add.247), channel_id=1, source_target_pairs={{0,16},{8,24},{16,0},{24,8},{32,48},{40,56},{48,32},{56,40},{64,80... | collective-permute-start | bytes 9224 | tf_op jit(solution)/shard_map/ppermute | solution.py:33
  431.0 7.6 %collective-permute-start.54 = (f32[6,128]{1,0:T(8,128)S(1)}, f32[6,128]{1,0:T(8,128)S(1)}, u32[]{:S(2)}, u32[]{:S(2)}) collective-permute-start(f32[6,128]{1,0:T(8,128)S(1)} %add.248), channel_id=1, source_target_pairs={{0,32},{8,40},{16,48},{24,56},{32,0},{40,8},{48,16},{56,24},{64,96... | collective-permute-start | bytes 9224 | tf_op jit(solution)/shard_map/ppermute | solution.py:33
  438.6 6.5 %collective-permute-start.55 = (f32[6,128]{1,0:T(8,128)S(1)}, f32[6,128]{1,0:T(8,128)S(1)}, u32[]{:S(2)}, u32[]{:S(2)}) collective-permute-start(f32[6,128]{1,0:T(8,128)S(1)} %add.249), channel_id=1, source_target_pairs={{0,64},{8,72},{16,80},{24,88},{32,96},{40,104},{48,112},{56,120},{... | collective-permute-start | bytes 9224 | tf_op jit(solution)/shard_map/ppermute | solution.py:33
  445.1 10.8 %collective-permute-start.56 = (f32[6,128]{1,0:T(8,128)S(1)}, f32[6,128]{1,0:T(8,128)S(1)}, u32[]{:S(2)}, u32[]{:S(2)}) collective-permute-start(f32[6,128]{1,0:T(8,128)S(1)} %add.250), channel_id=1, source_target_pairs={{0,128},{8,136},{16,144},{24,152},{32,160},{40,168},{48,176},{56,1... | collective-permute-start | bytes 9224 | tf_op jit(solution)/shard_map/ppermute | solution.py:33
  455.9 14.6 %collective-permute-start.57 = (f32[6,128]{1,0:T(8,128)S(1)}, f32[6,128]{1,0:T(8,128)S(1)}, u32[]{:S(2)}, u32[]{:S(2)}) collective-permute-start(f32[6,128]{1,0:T(8,128)S(1)} %add.251), channel_id=1, source_target_pairs={{0,256},{8,264},{16,272},{24,280},{32,288},{40,296},{48,304},{56,3... | collective-permute-start | bytes 9224 | tf_op jit(solution)/shard_map/ppermute | solution.py:33
  (9 other events, 652.7 us)
Sparse Core Ops, SparseCore 0:
  126.6 39.5 all-gather.2
  327.3 38.0 all-gather.4
